TPU v7x, 128 devices: a whole 4x4x4 slice. The times are simulated.
128 devices in a mesh: expert: 32 (over x_lo, z, y), replica: 4 (over x_hi, core).
Axes of the slice: x: 4 (x_hi: 2, x_lo: 2; x = x_hi * 2 + x_lo), y: 4, z: 4, core: 2. Of those that a mesh axis runs over, the one named last changes fastest.
Arguments:
- tokens: bfloat16 [32768, 7168], P(('expert', 'replica')), may hold values from -6 to 6
- routes: int32 [32768, 8], P(('expert', 'replica')), may hold values from 0 to 255, all different within a row
- counts: int32 [128], P(('expert', 'replica')), may hold values from 128 to 256, as said below
- w_gate: bfloat16 [32, 7168, 2048], P('expert', None, 'replica'), may hold values from -0.0625 to 0.0625
- w_up: bfloat16 [32, 7168, 2048], P('expert', None, 'replica'), may hold values from -0.0625 to 0.0625
Outputs:
- key_cov: float32 [32, 2048, 2048], P('expert', 'replica')
Inputs may be any that keep to these rules, and one draw needn't show every extreme that they name: `counts`: every count is a multiple of 128; some device has 256 and some 128.
All inputs are finite; a program needn't handle non-finite values.
Results may differ from a plain program's by a relative error of at most 0.0039.
Values may be sent and summed in bfloat16 or wider, within the bound.
No kernel may reach another device: no remote copies, remote signals or barrier semaphores. Data moves between devices by JAX's collectives and lax.ppermute only.
A program may use at most 128 MiB of HBM per device.

v0:
```python
import jax
import jax.numpy as jnp
from jax import lax
from jax.sharding import PartitionSpec as P

N_ROUTED = 256
TOP = 8


def slot_tokens(route_block, real_count, expert_total, capacity):
    flat_route = route_block.reshape(-1)
    position = jnp.arange(flat_route.shape[0], dtype=jnp.int32)
    owner_token = position // TOP
    usable = (owner_token < real_count) & (flat_route < expert_total)
    hit_table = (
        (flat_route[:, None] == jnp.arange(expert_total, dtype=jnp.int32)[None, :])
        & usable[:, None]
    ).astype(jnp.int32)
    slot_rank = jnp.sum((jnp.cumsum(hit_table, axis=0) - hit_table) * hit_table, axis=1)
    kept_slot = usable & (slot_rank < capacity)
    slot_index = flat_route * capacity + slot_rank
    slot_match = kept_slot[:, None] & (
        slot_index[:, None] == jnp.arange(expert_total * capacity, dtype=jnp.int32)[None, :]
    )
    filled = jnp.any(slot_match, axis=0)
    source = jnp.sum(jnp.where(slot_match, owner_token[:, None], 0), axis=0)
    return (source, filled)


def body(tokens, routes, counts, w_gate, w_up):
    expert_count = lax.axis_size("expert")
    replica_count = lax.axis_size("replica")
    slot_total, width_model = tokens.shape
    capacity = slot_total * TOP // N_ROUTED
    source, filled = slot_tokens(routes, counts[0], expert_count, capacity)
    slot_rows = jnp.where(filled[:, None], tokens[source], jnp.zeros((), tokens.dtype))
    slot_rows = slot_rows.reshape(expert_count, capacity, width_model)
    gate_matrix = w_gate[0]
    up_matrix = w_up[0]
    replicas = jnp.broadcast_to(
        slot_rows[:, None], (expert_count, replica_count, capacity, width_model)
    )
    replicas = replicas.reshape(expert_count * replica_count, capacity, width_model)
    slot_block = lax.all_to_all(
        replicas, ("expert", "replica"), split_axis=0, concat_axis=0, tiled=True
    )
    gate_pre = jnp.einsum(
        "sce,ef->scf", slot_block, gate_matrix, preferred_element_type=jnp.float32
    )
    up_pre = jnp.einsum("sce,ef->scf", slot_block, up_matrix, preferred_element_type=jnp.float32)
    exchanged = (jax.nn.silu(gate_pre) * up_pre).astype(jnp.bfloat16)
    own_keys = exchanged.reshape(expert_count * replica_count * capacity, exchanged.shape[2])
    factor = 1.0 / (expert_count * capacity)
    key_gram = (
        jnp.einsum(
            "rf,rg->fg",
            own_keys,
            lax.all_gather(own_keys, "replica", axis=1, tiled=True),
            preferred_element_type=jnp.float32,
        )
        * factor
    )
    return key_gram[None]


def solution(mesh):
    return jax.shard_map(
        body,
        mesh=mesh,
        in_specs=(
            P(("expert", "replica"), None),
            P(("expert", "replica"), None),
            P(("expert", "replica")),
            P("expert", None, "replica"),
            P("expert", None, "replica"),
        ),
        out_specs=P("expert", "replica", None),
        check_vma=False,
    )
```

profile of v0, /device:TPU:1, one launch (start us, length us, event | category | flops | bytes accessed | tf_op | source)
XLA Modules:
  0.0 300.9 jit_solution(13397311105587439801)
XLA Ops:
  6.5 0.0 all-gather.2.cloned.1.call-start
  6.5 0.8 copy.20
  7.4 0.1 reshape.100
  7.5 0.1 eq.39
  8.3 9.1 %reduce-window.6 = s32[32,16,128]{2,1,0:T(8,128)S(1)} reduce-window(s32[32,16,128]{2,1,0:T(8,128)S(1)} %fusion.16, s32[]{:T(128)} %constant.36.clone.1), window={size=1x1x128 pad=0_0x0_0x127_0}, to_apply=%region_0.1 | reduce-window | flops 8323072 | bytes 524292 | tf_op jit(solution)/shard_map/reduce-window
  17.4 0.1 slice.10
  17.5 0.2 copy.24
  17.8 0.2 reduce-window.9
  17.9 0.1 broadcast_add_fusion
  18.1 0.1 fusion.13
  18.3 1.4 fusion.5
  19.7 1.6 select_reduce_fusion
  21.3 0.1 broadcast_in_dim.42
  21.4 10.6 %gather_fusion = bf16[256,7168]{1,0:T(8,128)(2,1)} fusion(bf16[256,7168]{1,0:T(8,128)(2,1)} %param.5, s32[1024]{0:T(1024)S(1)} %pad_clamp_fusion), kind=kCustom, calls=%fused_computation | custom fusion | bytes 7341056 | tf_op jit(solution)/shard_map/gather | solution.py:36
  32.0 2.3 bitcast_select_fusion
  34.3 2.0 broadcast_in_dim.47
  36.3 178.7 %all_to_all.5 = bf16[128,8,7168]{2,1,0:T(8,128)(2,1)S(1)} all-to-all(bf16[128,8,7168]{2,1,0:T(8,128)(2,1)S(1)} %bitcast.49), channel_id=1, replica_groups=mesh['expert'=32,'replica'=4] {'expert','replica'}, dimensions={0} | all-to-all | bytes 29360128 | tf_op jit(solution)/shard_map/all_to_all | solution.py:44
  215.0 0.0 copy-start
  215.0 5.2 %copy-done = bf16[128,8,7168]{2,1,0:T(8,128)(2,1)} copy-done((bf16[128,8,7168]{2,1,0:T(8,128)(2,1)}, bf16[128,8,7168]{2,1,0:T(8,128)(2,1)S(1)}, u32[]{:S(2)}) %copy-start) | copy-done | bytes 14680088
  220.2 11.0 %fusion.2 = f32[128,8,512]{2,1,0:T(8,128)} fusion(bf16[128,8,7168]{2,1,0:T(8,128)(2,1)S(1)} %all_to_all.5, bf16[1,7168,512]{2,1,0:T(8,128)(2,1)} %param.8), kind=kOutput, calls=%fused_computation.3 | convolution fusion | flops 7516192768 | bytes 24117248 | tf_op jit(solution)/shard_map/sce,ef->scf/dot_general | solution.py:47
  231.1 14.4 %fusion.8 = bf16[1024,512]{1,0:T(8,128)(2,1)} fusion(bf16[128,8,7168]{2,1,0:T(8,128)(2,1)} %copy-done, bf16[1,7168,512]{2,1,0:T(8,128)(2,1)} %param.9, f32[128,8,512]{2,1,0:T(8,128)} %fusion.2), kind=kOutput, calls=%fused_computation.12 | convolution fusion | flops 7519338496 | bytes 25165824 | tf_op jit(solution)/shard_map/sce,ef->scf/dot_general | solution.py:50
  245.5 0.0 all-gather.2.cloned.1.call-update
  245.5 41.7 %all-gather.2.cloned.1.call-done = bf16[1024,2048]{1,0:T(8,128)(2,1)} async-done(((bf16[1024,512]{1,0:T(8,128)(2,1)}), bf16[1024,2048]{1,0:T(8,128)(2,1)}) %all-gather.2.cloned.1.call-update) | async-done | bytes 4194320 | tf_op jit(solution)/shard_map/all_gather | solution.py:58
  287.2 6.9 %multiply_bitcast_fusion = f32[1,512,2048]{2,1,0:T(8,128)} fusion(bf16[1024,512]{1,0:T(8,128)(2,1)} %fusion.8, bf16[1024,2048]{1,0:T(8,128)(2,1)} %all-gather.2.cloned.1.call-done), kind=kOutput, calls=%fused_computation.5 | convolution fusion | flops 2148532224 | bytes 9437184 | tf_op jit(solution)/shard_map/rf,rg->fg/dot_general | solution.py:55
  (7 shorter events, 0.1 us)
Async XLA Ops:
  6.5 280.7 %all-gather.2.cloned.1.call-start = ((), (), s32[]{:S(2)}) async-start(), calls=%async_computation.1 | async-start | bytes 5242880 | tf_op jit(solution)/shard_map/all_gather | solution.py:58
  215.0 5.2 %copy-start = (bf16[128,8,7168]{2,1,0:T(8,128)(2,1)}, bf16[128,8,7168]{2,1,0:T(8,128)(2,1)S(1)}, u32[]{:S(2)}) copy-start(bf16[128,8,7168]{2,1,0:T(8,128)(2,1)S(1)} %all_to_all.5) | copy-start | bytes 44040196
Sparse Core Ops, SparseCore 0:
  245.6 41.5 all-gather.1
where the time goes:
time: 301 us
  blocking collectives  179 us (59%)
  waiting for transfers between devices  41.7 us (14%)
  matrix products  32.2 us (11%)
  local copies, waits for them, and re-layouts  19.2 us (6%)
  other arithmetic  15 us (5%)
  between operations  14.2 us (5%)
    all_to_all x1, blocking collectives, body(): lax.all_to_all(replicas, ('expert', 'replica'), split_axis=0, concat_axis...  179 us
    all_gather x1, waiting for transfers between devices, body(): lax.all_gather(own_keys, 'replica', axis=1, tiled=True)  41.7 us
    dot_general x1, matrix products, body(): jnp.einsum('sce,ef->scf', slot_block, up_matrix, preferred_element_type=j...  14.4 us
    dot_general x1, matrix products, body(): jnp.einsum('sce,ef->scf', slot_block, gate_matrix, preferred_element_type...  11 us
    gather x1, local copies, waits for them, and re-layouts, body(): tokens[source]  10.6 us
    another operation x3, other arithmetic  9.41 us
    dot_general x1, matrix products, body(): jnp.einsum('rf,rg->fg', own_keys, lax.all_gather(own_keys, 'replica', axi...  6.9 us
    unnamed x3, local copies, waits for them, and re-layouts  6.03 us
  transfers between devices with their start and end apart: 1, of which 1 were waited for; matrix products, arithmetic and copies ran while one was open for 0% of the time, Pallas kernels for 0%

commit v1 on v0

v1 whole, which is shorter than its diff:
```python
import jax
import jax.numpy as jnp
from jax import lax
from jax.sharding import Mesh, NamedSharding, PartitionSpec as P

N_ROUTED = 256
TOP = 8


def slot_onehot(routes, real_count, expert_total, capacity):
    tokens_here = routes.shape[0]
    token = lax.broadcasted_iota(jnp.int32, (tokens_here, 1), 0)
    expert = lax.broadcasted_iota(jnp.int32, (1, 1, expert_total), 2)
    hit = jnp.any(routes[:, :, None] == expert, axis=1) & (token < real_count)
    row = lax.broadcasted_iota(jnp.int32, (tokens_here, tokens_here), 0)
    col = lax.broadcasted_iota(jnp.int32, (tokens_here, tokens_here), 1)
    earlier = (col < row).astype(jnp.bfloat16)
    rank = jnp.dot(earlier, hit.astype(jnp.bfloat16), preferred_element_type=jnp.float32)
    rank = rank.astype(jnp.int32)
    slot = lax.broadcasted_iota(jnp.int32, (1, capacity, 1), 1)
    return hit.T[:, None, :] & (rank.T[:, None, :] == slot)


def body(tokens, routes, counts, w_gate, w_up):
    expert_count = lax.axis_size("expert")
    half_count = lax.axis_size("xh")
    core_count = lax.axis_size("core")
    slot_total, width_model = tokens.shape
    capacity = slot_total * TOP // N_ROUTED
    onehot = slot_onehot(routes, counts[0], expert_count, capacity)
    onehot = jnp.broadcast_to(
        onehot[:, None], (expert_count, half_count, capacity, slot_total)
    ).reshape(expert_count * half_count * capacity, slot_total)
    slot_rows = jnp.dot(
        onehot.astype(tokens.dtype), tokens, preferred_element_type=jnp.float32
    ).astype(tokens.dtype)
    slot_rows = slot_rows.reshape(expert_count * half_count, capacity, width_model)
    slot_block = lax.all_to_all(
        slot_rows, ("expert", "xh"), split_axis=0, concat_axis=0, tiled=True
    )
    slot_block = slot_block.reshape(expert_count * half_count * capacity, width_model)
    slot_block = lax.all_gather(slot_block, "core", axis=0, tiled=True)
    gate_pre = jnp.dot(slot_block, w_gate[0], preferred_element_type=jnp.float32)
    up_pre = jnp.dot(slot_block, w_up[0], preferred_element_type=jnp.float32)
    own_keys = (jax.nn.silu(gate_pre) * up_pre).astype(jnp.bfloat16)
    factor = 1.0 / (expert_count * capacity)
    key_gram = (
        jnp.einsum(
            "rf,rg->fg",
            own_keys,
            lax.all_gather(own_keys, ("xh", "core"), axis=1, tiled=True),
            preferred_element_type=jnp.float32,
        )
        * factor
    )
    return key_gram[None]


def solution(mesh):
    expert_count, replica_count = mesh.devices.shape
    split = Mesh(
        mesh.devices.reshape(expert_count, 2, replica_count // 2), ("expert", "xh", "core")
    )
    rows = ("expert", "xh", "core")
    step = jax.shard_map(
        body,
        mesh=split,
        in_specs=(
            P(rows, None),
            P(rows, None),
            P(rows),
            P("expert", None, ("xh", "core")),
            P("expert", None, ("xh", "core")),
        ),
        out_specs=P("expert", ("xh", "core"), None),
        check_vma=False,
    )
    out_sharding = NamedSharding(mesh, P("expert", "replica", None))

    def run(tokens, routes, counts, w_gate, w_up):
        out = step(tokens, routes, counts, w_gate, w_up)
        return lax.with_sharding_constraint(out, out_sharding)

    return run
```

time: 301 us -> 215 us (0.71)
  blocking collectives: 179 us -> 96.3 us
  waiting for transfers between devices: 41.7 us -> 68.3 us
  local copies, waits for them, and re-layouts: 19.2 us -> 0.04 us
  other arithmetic: 15 us -> 0.84 us
  matrix products: 32.2 us -> 35.3 us
    all_to_all x1, blocking collectives: 179 us -> 96.3 us  [body(): lax.all_to_all(slot_rows, ('expert', 'xh'), split_axis=0, concat_axis=0,...]
    all_gather x1 -> x2, waiting for transfers between devices: 41.7 us -> 68.3 us  [the longest x1 39.9 us: body(): lax.all_gather(own_keys, ('xh', 'core'), axis=1, tiled=True)]
    gather x1 -> x0, local copies, waits for them, and re-layouts: 10.6 us -> none  [body(): tokens[source]]
    another operation x3 -> x0, other arithmetic: 9.41 us -> none
    unnamed x3 -> x2, local copies, waits for them, and re-layouts: 6.03 us -> 0.01 us
    dot_general x3 -> x5, matrix products: 32.2 us -> 35.3 us  [the longest x1 13.3 us: body(): up_pre = jnp.dot(slot_block, w_up[0], preferred_element_type=jnp.float32)]
  transfers between devices with their start and end apart: 1 -> 2, of which waited for: 1 -> 2; matrix products, arithmetic and copies ran while one was open for 0% -> 0% of each run, Pallas kernels for 0% -> 0%
where the time goes in v1:
time: 215 us
  blocking collectives  96.3 us (45%)
  waiting for transfers between devices  68.3 us (32%)
  matrix products  35.3 us (16%)
  between operations  14.1 us (7%)
    all_to_all x1, blocking collectives, body(): lax.all_to_all(slot_rows, ('expert', 'xh'), split_axis=0, concat_axis=0,...  96.3 us
    all_gather x1, waiting for transfers between devices, body(): lax.all_gather(own_keys, ('xh', 'core'), axis=1, tiled=True)  39.9 us
    all_gather x1, waiting for transfers between devices, body(): slot_block = lax.all_gather(slot_block, 'core', axis=0, tiled=True)  28.3 us
    dot_general x1, matrix products, body(): up_pre = jnp.dot(slot_block, w_up[0], preferred_element_type=jnp.float32)  13.3 us
    dot_general x1, matrix products, body(): jnp.dot(slot_block, w_gate[0], preferred_element_type=jnp.float32)  10.8 us
    dot_general x1, matrix products, body(): jnp.einsum('rf,rg->fg', own_keys, lax.all_gather(own_keys, ('xh', 'core')...  6.9 us
  transfers between devices with their start and end apart: 2, of which 2 were waited for; matrix products, arithmetic and copies ran while one was open for 0% of the time, Pallas kernels for 0%

profile of v1, /device:TPU:1, one launch (start us, length us, event | category | flops | bytes accessed | tf_op | source)
XLA Modules:
  0.0 215.0 jit_solution(5587718582403345066)
XLA Ops:
  6.5 0.0 all-gather.3.cloned.1.call-start
  7.2 0.7 fusion.7
  8.0 0.2 convolution_convert_fusion.1
  8.1 0.1 fusion.8
  8.3 4.1 %fusion = bf16[64,8,7168]{2,1,0:T(8,128)(2,1)S(1)} fusion(pred[512,256]{1,0:T(8,128)(4,1)S(1)} %bitcast.25, bf16[256,7168]{1,0:T(8,128)(2,1)} %param.5), kind=kOutput, calls=%fused_computation.1 | convolution fusion | flops 1882718208 | bytes 11141120 | tf_op jit(solution)/shard_map/dot_general | solution.py:34
  12.4 96.3 %all_to_all.5 = bf16[64,8,7168]{2,1,0:T(8,128)(2,1)} all-to-all(bf16[64,8,7168]{2,1,0:T(8,128)(2,1)S(1)} %fusion), channel_id=1, replica_groups=mesh['expert'=32,'xh'=2,'core'=2] {'expert','xh'}, dimensions={0} | all-to-all | bytes 14680064 | tf_op jit(solution)/shard_map/all_to_all | solution.py:38
  108.7 0.0 all-gather.3.cloned.1.call-update
  108.7 0.0 all-gather.5.cloned.1.call-start
  108.8 28.3 %all-gather.3.cloned.1.call-done = bf16[1024,7168]{1,0:T(8,128)(2,1)} async-done(((bf16[512,7168]{1,0:T(8,128)(2,1)}), bf16[1024,7168]{1,0:T(8,128)(2,1)}) %all-gather.3.cloned.1.call-update) | async-done | bytes 14680080 | tf_op jit(solution)/shard_map/all_gather | solution.py:42
  137.1 0.0 copy-start
  137.1 13.3 %fusion.1 = f32[1024,512]{1,0:T(8,128)S(1)} fusion(bf16[1024,7168]{1,0:T(8,128)(2,1)} %all-gather.3.cloned.1.call-done, bf16[1,7168,512]{2,1,0:T(8,128)(2,1)} %param.9), kind=kOutput, calls=%fused_computation.2 | convolution fusion | flops 7516192768 | bytes 24117248 | tf_op jit(solution)/shard_map/dot_general | solution.py:44
  150.4 0.0 copy-done
  150.4 10.8 %multiply_convert_fusion = bf16[1024,512]{1,0:T(8,128)(2,1)} fusion(f32[1024,512]{1,0:T(8,128)S(1)} %fusion.1, bf16[1024,7168]{1,0:T(8,128)(2,1)S(1)} %copy-done, bf16[1,7168,512]{2,1,0:T(8,128)(2,1)} %param.8), kind=kOutput, calls=%fused_computation.7 | convolution fusion | flops 7519338496 | bytes 25165824 | tf_op jit(solution)/shard_map/dot_general | solution.py:43
  161.3 0.0 all-gather.5.cloned.1.call-update
  161.3 39.9 %all-gather.5.cloned.1.call-done = bf16[1024,2048]{1,0:T(8,128)(2,1)} async-done(((bf16[1024,512]{1,0:T(8,128)(2,1)}), bf16[1024,2048]{1,0:T(8,128)(2,1)}) %all-gather.5.cloned.1.call-update) | async-done | bytes 4194320 | tf_op jit(solution)/shard_map/all_gather | solution.py:51
  201.2 6.9 %multiply_bitcast_fusion = f32[1,512,2048]{2,1,0:T(8,128)} fusion(bf16[1024,512]{1,0:T(8,128)(2,1)} %multiply_convert_fusion, bf16[1024,2048]{1,0:T(8,128)(2,1)} %all-gather.5.cloned.1.call-done), kind=kOutput, calls=%fused_computation.6 | convolution fusion | flops 2148532224 | bytes 9437184 | tf_op jit(solution)/shard_map/rf,rg->fg/dot_general | solution.py:48
  (3 shorter events, 0.1 us)
Async XLA Ops:
  6.5 130.6 %all-gather.3.cloned.1.call-start = ((), (), s32[]{:S(2)}) async-start(), calls=%async_computation.1 | async-start | bytes 22020096 | tf_op jit(solution)/shard_map/all_gather | solution.py:42
  108.7 92.5 %all-gather.5.cloned.1.call-start = ((), (), s32[]{:S(2)}) async-start(), calls=%async_computation.2 | async-start | bytes 5242880 | tf_op jit(solution)/shard_map/all_gather | solution.py:51
  137.1 13.3 %copy-start = (bf16[1024,7168]{1,0:T(8,128)(2,1)S(1)}, bf16[1024,7168]{1,0:T(8,128)(2,1)}, u32[]{:S(2)}) copy-start(bf16[1024,7168]{1,0:T(8,128)(2,1)} %all-gather.3.cloned.1.call-done) | copy-start | bytes 44040196
Sparse Core Ops, SparseCore 0:
  108.9 28.2 all-gather.2
  161.4 39.7 all-gather.4

commit v2 on v1

--- a/solution.py
+++ b/solution.py
@@ -39,20 +39,30 @@
         slot_rows, ("expert", "xh"), split_axis=0, concat_axis=0, tiled=True
     )
     slot_block = slot_block.reshape(expert_count * half_count * capacity, width_model)
-    slot_block = lax.all_gather(slot_block, "core", axis=0, tiled=True)
-    gate_pre = jnp.dot(slot_block, w_gate[0], preferred_element_type=jnp.float32)
-    up_pre = jnp.dot(slot_block, w_up[0], preferred_element_type=jnp.float32)
-    own_keys = (jax.nn.silu(gate_pre) * up_pre).astype(jnp.bfloat16)
+    partner = lax.ppermute(slot_block, "core", [(c, (c + 1) % core_count) for c in range(core_count)])
     factor = 1.0 / (expert_count * capacity)
-    key_gram = (
-        jnp.einsum(
-            "rf,rg->fg",
-            own_keys,
-            lax.all_gather(own_keys, ("xh", "core"), axis=1, tiled=True),
-            preferred_element_type=jnp.float32,
+    own_keys, gathered = [], []
+    for rows in (slot_block, partner):
+        gate_pre = jnp.dot(rows, w_gate[0], preferred_element_type=jnp.float32)
+        up_pre = jnp.dot(rows, w_up[0], preferred_element_type=jnp.float32)
+        keys = (jax.nn.silu(gate_pre) * up_pre).astype(jnp.bfloat16)
+        own_keys.append(keys)
+        gathered.append(lax.all_gather(keys, ("xh", "core"), axis=0))
+    first_core = lax.axis_index("core") == 0
+    from_core = (
+        jnp.where(first_core, own_keys[0], own_keys[1]),
+        jnp.where(first_core, own_keys[1], own_keys[0]),
+    )
+    blocks = []
+    for replica in range(half_count * core_count):
+        source = replica % core_count
+        block = jnp.dot(
+            from_core[source].T, gathered[0][replica], preferred_element_type=jnp.float32
+        ) + jnp.dot(
+            from_core[1 - source].T, gathered[1][replica], preferred_element_type=jnp.float32
         )
-        * factor
-    )
+        blocks.append(block)
+    key_gram = jnp.concatenate(blocks, axis=1) * factor
     return key_gram[None]
 
 

time: 215 us -> 197 us (0.916)
  waiting for transfers between devices: 68.3 us -> 25.9 us
  matrix products: 35.3 us -> 48.3 us
  local copies, waits for them, and re-layouts: 0.04 us -> 5.41 us
  starting transfers between devices: 0.04 us -> 2.82 us
  other arithmetic: 0.84 us -> 3.37 us
    all_gather x2, waiting for transfers between devices: 68.3 us -> 25.9 us  [body(): gathered.append(lax.all_gather(keys, ('xh', 'core'), axis=0))]
    dot_general x3 -> x12, matrix products: 31 us -> 43.9 us  [the longest x2 18.1 us: body(): up_pre = jnp.dot(rows, w_up[0], preferred_element_type=jnp.float32)]
    mul x0 -> x1, local copies, waits for them, and re-layouts: none -> 5.34 us  [body(): key_gram = jnp.concatenate(blocks, axis=1) * factor]
    ppermute x0 -> x1, starting transfers between devices: none -> 2.6 us  [body(): lax.ppermute(slot_block, 'core', [(c, (c + 1) % core_count) for c in rang...]
    mul x0 -> x1, other arithmetic: none -> 2.47 us  [body(): key_gram = jnp.concatenate(blocks, axis=1) * factor]
  transfers between devices with their start and end apart: 2 -> 3, of which waited for: 2 -> 2; matrix products, arithmetic and copies ran while one was open for 0% -> 20% of each run, Pallas kernels for 0% -> 0%
where the time goes in v2:
time: 197 us
  blocking collectives  96.6 us (49%)
  matrix products  48.3 us (25%)
  waiting for transfers between devices  25.9 us (13%)
  between operations  14.3 us (7%)
  local copies, waits for them, and re-layouts  5.41 us (3%)
  other arithmetic  3.37 us (2%)
  starting transfers between devices  2.82 us (1%)
    all_to_all x1, blocking collectives, body(): lax.all_to_all(slot_rows, ('expert', 'xh'), split_axis=0, concat_axis=0,...  96.6 us
    all_gather x2, waiting for transfers between devices, body(): gathered.append(lax.all_gather(keys, ('xh', 'core'), axis=0))  25.9 us
    dot_general x2, matrix products, body(): up_pre = jnp.dot(rows, w_up[0], preferred_element_type=jnp.float32)  18.1 us
    dot_general x2, matrix products, body(): gate_pre = jnp.dot(rows, w_gate[0], preferred_element_type=jnp.float32)  14.9 us
    dot_general x4, matrix products, body(): jnp.dot(from_core[source].T, gathered[0][replica], preferred_element_type...  6.1 us
    mul x1, local copies, waits for them, and re-layouts, body(): key_gram = jnp.concatenate(blocks, axis=1) * factor  5.34 us
    dot_general x4, matrix products, body(): jnp.dot(from_core[1 - source].T, gathered[1][replica], preferred_element_...  4.87 us
    dot_general x1, matrix products, body(): jnp.dot(onehot.astype(tokens.dtype), tokens, preferred_element_type=jnp.f...  4.26 us
  transfers between devices with their start and end apart: 3, of which 2 were waited for; matrix products, arithmetic and copies ran while one was open for 20% of the time, Pallas kernels for 0%

profile of v2, /device:TPU:1, one launch (start us, length us, event | category | flops | bytes accessed | tf_op | source)
XLA Modules:
  0.0 196.7 jit_solution(443448000608172700)
XLA Ops:
  6.5 0.0 all-gather.5.cloned.1.call-start
  6.5 0.7 fusion.31
  7.9 0.2 convolution_convert_fusion.1
  8.1 0.1 fusion.32
  8.3 0.0 slice-start
  8.3 4.3 %fusion = bf16[64,8,7168]{2,1,0:T(8,128)(2,1)S(1)} fusion(pred[512,256]{1,0:T(8,128)(4,1)S(1)} %bitcast.48, bf16[256,7168]{1,0:T(8,128)(2,1)} %param.5), kind=kOutput, calls=%fused_computation.1 | convolution fusion | flops 1882718208 | bytes 11141120 | tf_op jit(solution)/shard_map/dot_general | solution.py:34
  12.5 0.0 slice-start.1
  12.5 96.6 %all_to_all.5 = bf16[64,8,7168]{2,1,0:T(8,128)(2,1)} all-to-all(bf16[64,8,7168]{2,1,0:T(8,128)(2,1)S(1)} %fusion), channel_id=1, replica_groups=mesh['expert'=32,'xh'=2,'core'=2] {'expert','xh'}, dimensions={0} | all-to-all | bytes 14680064 | tf_op jit(solution)/shard_map/all_to_all | solution.py:38
  109.1 0.0 slice-start.2
  109.1 0.0 slice-start.3
  109.1 2.6 %collective-permute-start = (bf16[512,7168]{1,0:T(8,128)(2,1)}, bf16[512,7168]{1,0:T(8,128)(2,1)}, u32[]{:S(2)}, u32[]{:S(2)}) collective-permute-start(bf16[512,7168]{1,0:T(8,128)(2,1)} %bitcast.4), channel_id=1, source_target_pairs={{0,1},{1,0},{2,3},{3,2},{4,5},{5,4},{6,7},{7,6},{8,9},{9,8},{10,11... | collective-permute-start | bytes 22020104 | tf_op jit(solution)/shard_map/ppermute | solution.py:42
  111.7 0.0 slice-done
  111.7 0.0 slice-done.1
  111.7 6.4 %fusion.7 = f32[512,512]{1,0:T(8,128)S(1)} fusion(bf16[1,7168,512]{2,1,0:T(8,128)(2,1)S(1)} %bitcast.50, bf16[64,8,7168]{2,1,0:T(8,128)(2,1)} %all_to_all.5), kind=kOutput, calls=%fused_computation.8 | convolution fusion | flops 3758096384 | bytes 15728640 | tf_op jit(solution)/shard_map/dot_general | solution.py:46
  118.1 0.0 slice-done.2
  118.1 0.0 slice-done.3
  118.1 8.0 %fusion.16 = bf16[512,512]{1,0:T(8,128)(2,1)} fusion(bf16[1,7168,512]{2,1,0:T(8,128)(2,1)S(1)} %bitcast.52, f32[512,512]{1,0:T(8,128)S(1)} %fusion.7, bf16[64,8,7168]{2,1,0:T(8,128)(2,1)} %all_to_all.5), kind=kOutput, calls=%fused_computation.20 | convolution fusion | flops 3759669248 | bytes 16252928 | tf_op jit(solution)/shard_map/dot_general | solution.py:47
  126.1 0.0 all-gather.5.cloned.1.call-update
  126.1 0.2 all-gather.7.cloned.1.call-start
  126.4 0.0 copy-start
  126.4 0.0 collective-permute-done
  126.4 8.5 %fusion.5 = f32[512,512]{1,0:T(8,128)S(1)} fusion(bf16[512,7168]{1,0:T(8,128)(2,1)} %collective-permute-done, bf16[1,7168,512]{2,1,0:T(8,128)(2,1)} %param.8), kind=kOutput, calls=%fused_computation.6 | convolution fusion | flops 3758096384 | bytes 15728640 | tf_op jit(solution)/shard_map/dot_general | solution.py:46
  134.9 0.0 copy-done
  134.9 10.1 %broadcast_select_fusion.1 = (bf16[512,512]{1,0:T(8,128)(2,1)S(1)}, bf16[512,512]{1,0:T(8,128)(2,1)}) fusion(bf16[512,512]{1,0:T(8,128)(2,1)S(1)} %copy-done, pred[]{:T(512)S(6)} %eq.33, f32[512,512]{1,0:T(8,128)S(1)} %fusion.5, bf16[512,7168]{1,0:T(8,128)(2,1)} %collective-permute-done, bf16[1,7168,512]{2,1,0:T(8,128)(2,1)} %param.9), kind=kOutput, calls=%fused_computation.36 | convolution fusion | flops 3759931392 | bytes 17301504 | tf_op jit(solution)/shard_map/dot_general | solution.py:47
  145.0 0.0 all-gather.7.cloned.1.call-update
  145.0 0.1 broadcast_select_fusion
  145.1 4.3 %all-gather.5.cloned.1.call-done = bf16[2048,512]{1,0:T(8,128)(2,1)} async-done(((bf16[512,512]{1,0:T(8,128)(2,1)}), bf16[2048,512]{1,0:T(8,128)(2,1)}) %all-gather.5.cloned.1.call-update) | async-done | bytes 2097168 | tf_op jit(solution)/shard_map/all_gather | solution.py:50
  149.4 0.0 copy-start.1
  149.4 2.6 %fusion.29 = f32[512,512]{0,1:T(8,128)} fusion(bf16[512,512]{1,0:T(8,128)(2,1)S(1)} %get-tuple-element.5, bf16[2048,512]{1,0:T(8,128)(2,1)} %all-gather.5.cloned.1.call-done), kind=kOutput, calls=%fused_computation.33 | convolution fusion | flops 268435456 | bytes 2097152 | tf_op jit(solution)/shard_map/dot_general | solution.py:59
  152.0 1.5 fusion.23
  153.6 0.0 copy-done.1
  153.6 1.5 fusion.26
  155.0 0.5 fusion.20
  155.5 21.6 %all-gather.7.cloned.1.call-done = bf16[2048,512]{1,0:T(8,128)(2,1)} async-done(((bf16[512,512]{1,0:T(8,128)(2,1)}), bf16[2048,512]{1,0:T(8,128)(2,1)}) %all-gather.7.cloned.1.call-update) | async-done | bytes 2097168 | tf_op jit(solution)/shard_map/all_gather | solution.py:50
  177.1 0.0 copy-start.2
  177.1 2.0 %fusion.15 = f32[1,512,512]{1,2,0:T(8,128)S(1)} fusion(f32[512,512]{0,1:T(8,128)} %fusion.29, bf16[512,512]{1,0:T(8,128)(2,1)S(1)} %broadcast_select_fusion, bf16[2048,512]{1,0:T(8,128)(2,1)} %all-gather.7.cloned.1.call-done), kind=kOutput, calls=%fused_computation.19 | convolution fusion | flops 268697600 | bytes 3145728 | tf_op jit(solution)/shard_map/dot_general | solution.py:61
  179.1 1.9 fusion.14
  181.0 0.0 copy-done.2
  181.0 0.5 fusion.13
  181.5 0.5 fusion.12
  182.0 2.5 %maximum_multiply_fusion = f32[1,512,2048]{1,2,0:T(8,128)} fusion(f32[1,512,512]{1,2,0:T(8,128)S(1)} %fusion.12, f32[1,512,512]{1,2,0:T(8,128)S(1)} %fusion.13, f32[1,512,512]{1,2,0:T(8,128)S(1)} %fusion.14, f32[1,512,512]{1,2,0:T(8,128)S(1)} %fusion.15), kind=kLoop, calls=%fused_computation.10 | loop fusion | flops 4194304 | bytes 8388608 | tf_op jit(solution)/shard_map/mul | solution.py:65
  184.5 5.3 %copy.9 = f32[1,512,2048]{2,1,0:T(8,128)} copy(f32[1,512,2048]{1,2,0:T(8,128)} %maximum_multiply_fusion) | data formatting | bytes 8388608 | tf_op jit(solution)/shard_map/mul | solution.py:65
  (5 shorter events, 0.1 us)
Async XLA Ops:
  6.5 142.9 %all-gather.5.cloned.1.call-start = ((), (), s32[]{:S(2)}) async-start(), calls=%async_computation.1 | async-start | bytes 2621440 | tf_op jit(solution)/shard_map/all_gather | solution.py:50
  8.3 103.5 %slice-start = ((s8[7340032]{0:T(1024)(128)(4,1)}), s8[3145728]{0:T(1024)(128)(4,1)S(1)}, s32[]{:S(2)}) async-start(s8[7340032]{0:T(1024)(128)(4,1)} %bitcast.49), calls=%async_computation.3 | async-start | bytes 6291456
  12.5 99.2 %slice-start.1 = ((s8[7340032]{0:T(1024)(128)(4,1)}), s8[4194304]{0:T(1024)(128)(4,1)S(1)}, s32[]{:S(2)}) async-start(s8[7340032]{0:T(1024)(128)(4,1)} %bitcast.49), calls=%async_computation.4 | async-start | bytes 8388608
  109.1 9.0 %slice-start.2 = ((s8[7340032]{0:T(1024)(128)(4,1)}), s8[4194304]{0:T(1024)(128)(4,1)S(1)}, s32[]{:S(2)}) async-start(s8[7340032]{0:T(1024)(128)(4,1)} %bitcast.51), calls=%async_computation.5 | async-start | bytes 8388608
  109.1 9.0 %slice-start.3 = ((s8[7340032]{0:T(1024)(128)(4,1)}), s8[3145728]{0:T(1024)(128)(4,1)S(1)}, s32[]{:S(2)}) async-start(s8[7340032]{0:T(1024)(128)(4,1)} %bitcast.51), calls=%async_computation.6 | async-start | bytes 6291456
  109.1 17.2 %collective-permute-start = (bf16[512,7168]{1,0:T(8,128)(2,1)}, bf16[512,7168]{1,0:T(8,128)(2,1)}, u32[]{:S(2)}, u32[]{:S(2)}) collective-permute-start(bf16[512,7168]{1,0:T(8,128)(2,1)} %bitcast.4), channel_id=1, source_target_pairs={{0,1},{1,0},{2,3},{3,2},{4,5},{5,4},{6,7},{7,6},{8,9},{9,8},{10,11... | collective-permute-start | bytes 22020104 | tf_op jit(solution)/shard_map/ppermute | solution.py:42
  126.1 51.0 %all-gather.7.cloned.1.call-start = ((), (), s32[]{:S(2)}) async-start(), calls=%async_computation.2 | async-start | bytes 2621440 | tf_op jit(solution)/shard_map/all_gather | solution.py:50
  126.4 8.5 %copy-start = (bf16[512,512]{1,0:T(8,128)(2,1)S(1)}, bf16[512,512]{1,0:T(8,128)(2,1)}, u32[]{:S(2)}) copy-start(bf16[512,512]{1,0:T(8,128)(2,1)} %fusion.16) | copy-start | bytes 1572868
  149.4 4.2 %copy-start.1 = (bf16[2048,512]{1,0:T(8,128)(2,1)S(1)}, bf16[2048,512]{1,0:T(8,128)(2,1)}, u32[]{:S(2)}) copy-start(bf16[2048,512]{1,0:T(8,128)(2,1)} %all-gather.5.cloned.1.call-done) | copy-start | bytes 6291460
  177.1 3.9 %copy-start.2 = (bf16[2048,512]{1,0:T(8,128)(2,1)S(1)}, bf16[2048,512]{1,0:T(8,128)(2,1)}, u32[]{:S(2)}) copy-start(bf16[2048,512]{1,0:T(8,128)(2,1)} %all-gather.7.cloned.1.call-done) | copy-start | bytes 6291460
Sparse Core Ops, SparseCore 0:
  126.2 23.1 all-gather.4
  151.1 26.0 all-gather.6

commit v3 on v1

--- a/solution.py
+++ b/solution.py
@@ -39,20 +39,36 @@
         slot_rows, ("expert", "xh"), split_axis=0, concat_axis=0, tiled=True
     )
     slot_block = slot_block.reshape(expert_count * half_count * capacity, width_model)
-    slot_block = lax.all_gather(slot_block, "core", axis=0, tiled=True)
-    gate_pre = jnp.dot(slot_block, w_gate[0], preferred_element_type=jnp.float32)
-    up_pre = jnp.dot(slot_block, w_up[0], preferred_element_type=jnp.float32)
-    own_keys = (jax.nn.silu(gate_pre) * up_pre).astype(jnp.bfloat16)
+    partner = lax.ppermute(slot_block, "core", [(c, (c + 1) % core_count) for c in range(core_count)])
     factor = 1.0 / (expert_count * capacity)
-    key_gram = (
-        jnp.einsum(
-            "rf,rg->fg",
-            own_keys,
-            lax.all_gather(own_keys, ("xh", "core"), axis=1, tiled=True),
-            preferred_element_type=jnp.float32,
+    swap_half = [(h, (h + 1) % half_count) for h in range(half_count)]
+    swap_core = [(c, (c + 1) % core_count) for c in range(core_count)]
+    replica_count = half_count * core_count
+    swap_both = [(r, r ^ (replica_count - 1)) for r in range(replica_count)]
+    blocks = [[None] * 4, [None] * 4]
+    for i, rows in enumerate((slot_block, partner)):
+        gate_pre = jnp.dot(rows, w_gate[0], preferred_element_type=jnp.float32)
+        up_pre = jnp.dot(rows, w_up[0], preferred_element_type=jnp.float32)
+        keys = (jax.nn.silu(gate_pre) * up_pre).astype(jnp.bfloat16)
+        blocks[i][0] = keys
+        blocks[i][2] = lax.ppermute(keys, "xh", swap_half)
+        blocks[1 - i][1] = lax.ppermute(keys, "core", swap_core)
+        blocks[1 - i][3] = lax.ppermute(keys, ("xh", "core"), swap_both)
+    on_second_core = lax.axis_index("core") == 1
+    on_second_half = lax.axis_index("xh") == 1
+
+    def absolute(rel):
+        by_core = [jnp.where(on_second_core, rel[k ^ 1], rel[k]) for k in range(4)]
+        by_half = [jnp.where(on_second_half, by_core[k ^ 2], by_core[k]) for k in range(4)]
+        return jnp.concatenate(by_half, axis=1)
+
+    key_gram = None
+    for i in range(2):
+        part = jnp.einsum(
+            "rf,rg->fg", blocks[i][0], absolute(blocks[i]), preferred_element_type=jnp.float32
         )
-        * factor
-    )
+        key_gram = part if key_gram is None else key_gram + part
+    key_gram = key_gram * factor
     return key_gram[None]
 
 

time: 215 us -> 181 us (0.84)
  waiting for transfers between devices: 68.3 us -> 30.4 us
  between operations: 14.1 us -> 0.75 us
  starting transfers between devices: 0.04 us -> 9.55 us
  matrix products: 35.3 us -> 42.9 us
    all_gather x2 -> x0, waiting for transfers between devices: 68.3 us -> none  [the longest x1 39.9 us: body(): lax.all_gather(own_keys, ('xh', 'core'), axis=1, tiled=True)]
    ppermute x0 -> x7, waiting for transfers between devices: none -> 30.4 us  [the longest x2 19 us: body(): blocks[i][2] = lax.ppermute(keys, 'xh', swap_half)]
    ppermute x0 -> x7, starting transfers between devices: none -> 9.55 us  [the longest x2 3.39 us: body(): blocks[1 - i][3] = lax.ppermute(keys, ('xh', 'core'), swap_both)]
    dot_general x3 -> x6, matrix products: 31 us -> 38.6 us  [the longest x2 16.5 us: body(): up_pre = jnp.dot(rows, w_up[0], preferred_element_type=jnp.float32)]
  transfers between devices with their start and end apart: 2 -> 7, of which waited for: 2 -> 3; matrix products, arithmetic and copies ran while one was open for 0% -> 18% of each run, Pallas kernels for 0% -> 0%
where the time goes in v3:
time: 181 us
  blocking collectives  96.2 us (53%)
  matrix products  42.9 us (24%)
  waiting for transfers between devices  30.4 us (17%)
  starting transfers between devices  9.55 us (5%)
    all_to_all x1, blocking collectives, body(): lax.all_to_all(slot_rows, ('expert', 'xh'), split_axis=0, concat_axis=0,...  96.2 us
    ppermute x2, waiting for transfers between devices, body(): blocks[i][2] = lax.ppermute(keys, 'xh', swap_half)  19 us
    dot_general x2, matrix products, body(): up_pre = jnp.dot(rows, w_up[0], preferred_element_type=jnp.float32)  16.5 us
    dot_general x2, matrix products, body(): gate_pre = jnp.dot(rows, w_gate[0], preferred_element_type=jnp.float32)  14.8 us
    ppermute x2, waiting for transfers between devices, body(): blocks[1 - i][3] = lax.ppermute(keys, ('xh', 'core'), swap_both)  11.4 us
    dot_general x2, matrix products, body(): jnp.einsum('rf,rg->fg', blocks[i][0], absolute(blocks[i]), preferred_elem...  7.23 us
    dot_general x1, matrix products, body(): jnp.dot(onehot.astype(tokens.dtype), tokens, preferred_element_type=jnp.f...  4.11 us
  transfers between devices with their start and end apart: 7, of which 3 were waited for; matrix products, arithmetic and copies ran while one was open for 18% of the time, Pallas kernels for 0%

profile of v3, /device:TPU:1, one launch (start us, length us, event | category | flops | bytes accessed | tf_op | source)
XLA Modules:
  0.0 181.0 jit_solution(18135701400545746917)
XLA Ops:
  0.0 0.7 fusion.30
  1.4 0.2 convolution_convert_fusion.1
  1.6 0.1 fusion.31
  1.7 4.1 %fusion = bf16[64,8,7168]{2,1,0:T(8,128)(2,1)S(1)} fusion(pred[512,256]{1,0:T(8,128)(4,1)S(1)} %bitcast.37, bf16[256,7168]{1,0:T(8,128)(2,1)} %param.5), kind=kOutput, calls=%fused_computation.1 | convolution fusion | flops 1882718208 | bytes 11141120 | tf_op jit(solution)/shard_map/dot_general | solution.py:34
  5.8 96.2 %all_to_all.5 = bf16[64,8,7168]{2,1,0:T(8,128)(2,1)S(1)} all-to-all(bf16[64,8,7168]{2,1,0:T(8,128)(2,1)S(1)} %fusion), channel_id=1, replica_groups=mesh['expert'=32,'xh'=2,'core'=2] {'expert','xh'}, dimensions={0} | all-to-all | bytes 14680064 | tf_op jit(solution)/shard_map/all_to_all | solution.py:38
  102.0 2.6 %collective-permute-start = (bf16[512,7168]{1,0:T(8,128)(2,1)S(1)}, bf16[512,7168]{1,0:T(8,128)(2,1)}, u32[]{:S(2)}, u32[]{:S(2)}) collective-permute-start(bf16[512,7168]{1,0:T(8,128)(2,1)S(1)} %bitcast.36), channel_id=1, source_target_pairs={{0,1},{1,0},{2,3},{3,2},{4,5},{5,4},{6,7},{7,6},{8,9},{9,8},{10,11... | collective-permute-start | bytes 22020104 | tf_op jit(solution)/shard_map/ppermute | solution.py:42
  104.6 6.4 %fusion.7 = f32[512,512]{0,1:T(8,128)S(1)} fusion(bf16[1,7168,512]{2,1,0:T(8,128)(2,1)} %param.8, bf16[64,8,7168]{2,1,0:T(8,128)(2,1)S(1)} %all_to_all.5), kind=kOutput, calls=%fused_computation.8 | convolution fusion | flops 3758096384 | bytes 15728640 | tf_op jit(solution)/shard_map/dot_general | solution.py:50
  111.0 7.3 %fusion.27 = bf16[512,512]{0,1:T(8,128)(2,1)S(1)} fusion(bf16[1,7168,512]{2,1,0:T(8,128)(2,1)} %param.9, f32[512,512]{0,1:T(8,128)S(1)} %fusion.7, bf16[64,8,7168]{2,1,0:T(8,128)(2,1)S(1)} %all_to_all.5), kind=kOutput, calls=%fused_computation.27 | convolution fusion | flops 3759669248 | bytes 16252928 | tf_op jit(solution)/shard_map/dot_general | solution.py:51
  118.3 0.7 collective-permute-start.4
  119.0 0.5 collective-permute-start.6
  119.5 0.0 collective-permute-done
  119.5 8.4 %fusion.5 = f32[512,512]{0,1:T(8,128)S(1)} fusion(bf16[512,7168]{1,0:T(8,128)(2,1)} %collective-permute-done, bf16[1,7168,512]{2,1,0:T(8,128)(2,1)} %param.8), kind=kOutput, calls=%fused_computation.6 | convolution fusion | flops 3758096384 | bytes 15728640 | tf_op jit(solution)/shard_map/dot_general | solution.py:50
  128.0 9.3 %multiply_convert_fusion = bf16[512,512]{0,1:T(8,128)(2,1)S(1)} fusion(f32[512,512]{0,1:T(8,128)S(1)} %fusion.5, bf16[512,7168]{1,0:T(8,128)(2,1)} %collective-permute-done, bf16[1,7168,512]{2,1,0:T(8,128)(2,1)} %param.9), kind=kOutput, calls=%fused_computation.29 | convolution fusion | flops 3759669248 | bytes 16252928 | tf_op jit(solution)/shard_map/dot_general | solution.py:51
  137.2 2.3 %collective-permute-start.5 = (bf16[512,512]{0,1:T(8,128)(2,1)S(1)}, bf16[512,512]{0,1:T(8,128)(2,1)S(1)}, u32[]{:S(2)}, u32[]{:S(2)}) collective-permute-start(bf16[512,512]{0,1:T(8,128)(2,1)S(1)} %multiply_convert_fusion), channel_id=1, source_target_pairs={{0,2},{2,0},{1,3},{3,1},{4,6},{6,4},{5,7},{7,5},{8,10},{10,8},{9,1... | collective-permute-start | bytes 1572872 | tf_op jit(solution)/shard_map/ppermute | solution.py:54
  139.6 0.7 collective-permute-start.2
  140.3 2.7 %collective-permute-start.1 = (bf16[512,512]{0,1:T(8,128)(2,1)S(1)}, bf16[512,512]{0,1:T(8,128)(2,1)S(1)}, u32[]{:S(2)}, u32[]{:S(2)}) collective-permute-start(bf16[512,512]{0,1:T(8,128)(2,1)S(1)} %multiply_convert_fusion), channel_id=1, source_target_pairs={{0,3},{1,2},{2,1},{3,0},{4,7},{5,6},{6,5},{7,4},{8,11},{9,10},{10,... | collective-permute-start | bytes 1572872 | tf_op jit(solution)/shard_map/ppermute | solution.py:56
  143.0 0.0 collective-permute-done.4
  143.0 0.0 collective-permute-start.3
  143.0 0.0 collective-permute-done.6
  143.0 9.3 %collective-permute-done.5 = bf16[512,512]{0,1:T(8,128)(2,1)S(1)} collective-permute-done((bf16[512,512]{0,1:T(8,128)(2,1)S(1)}, bf16[512,512]{0,1:T(8,128)(2,1)S(1)}, u32[]{:S(2)}, u32[]{:S(2)}) %collective-permute-start.5) | collective-permute-done | bytes 524320 | tf_op jit(solution)/shard_map/ppermute | solution.py:54
  152.3 0.2 broadcast_select_fusion.11
  152.5 1.3 fusion.16
  153.8 9.7 %collective-permute-done.2 = bf16[512,512]{0,1:T(8,128)(2,1)S(1)} collective-permute-done((bf16[512,512]{0,1:T(8,128)(2,1)S(1)}, bf16[512,512]{0,1:T(8,128)(2,1)S(1)}, u32[]{:S(2)}, u32[]{:S(2)}) %collective-permute-start.2) | collective-permute-done | bytes 524320 | tf_op jit(solution)/shard_map/ppermute | solution.py:54
  163.5 11.4 %collective-permute-done.1 = bf16[512,512]{0,1:T(8,128)(2,1)S(1)} collective-permute-done((bf16[512,512]{0,1:T(8,128)(2,1)S(1)}, bf16[512,512]{0,1:T(8,128)(2,1)S(1)}, u32[]{:S(2)}, u32[]{:S(2)}) %collective-permute-start.1) | collective-permute-done | bytes 524320 | tf_op jit(solution)/shard_map/ppermute | solution.py:56
  174.9 0.0 collective-permute-done.3
  174.9 0.2 broadcast_select_fusion.15
  175.1 5.9 %multiply_bitcast_fusion = f32[1,512,2048]{2,1,0:T(8,128)} fusion(f32[512,2048]{1,0:T(8,128)S(1)} %fusion.16, bf16[512,512]{0,1:T(8,128)(2,1)S(1)} %fusion.27, bf16[512,512]{0,1:T(8,128)(2,1)S(1)} %get-tuple-element.8, bf16[512,512]{0,1:T(8,128)(2,1)S(1)} %get-tuple-element.7, bf16[512,512]{0,1:T(8,128)(2,1)S(1)} %get-tuple-element.6, ...), kind=kOutput, calls=%fused_computation.10 | convolution fusion | flops 1084227584 | bytes 11010048 | tf_op jit(solution)/shard_map/rf,rg->fg/dot_general | solution.py:67
  (3 shorter events, 0.1 us)
Async XLA Ops:
  102.0 17.5 %collective-permute-start = (bf16[512,7168]{1,0:T(8,128)(2,1)S(1)}, bf16[512,7168]{1,0:T(8,128)(2,1)}, u32[]{:S(2)}, u32[]{:S(2)}) collective-permute-start(bf16[512,7168]{1,0:T(8,128)(2,1)S(1)} %bitcast.36), channel_id=1, source_target_pairs={{0,1},{1,0},{2,3},{3,2},{4,5},{5,4},{6,7},{7,6},{8,9},{9,8},{10,11... | collective-permute-start | bytes 22020104 | tf_op jit(solution)/shard_map/ppermute | solution.py:42
  118.3 24.7 %collective-permute-start.4 = (bf16[512,512]{0,1:T(8,128)(2,1)S(1)}, bf16[512,512]{0,1:T(8,128)(2,1)S(1)}, u32[]{:S(2)}, u32[]{:S(2)}) collective-permute-start(bf16[512,512]{0,1:T(8,128)(2,1)S(1)} %fusion.27), channel_id=1, source_target_pairs={{0,3},{1,2},{2,1},{3,0},{4,7},{5,6},{6,5},{7,4},{8,11},{9,10},{10,... | collective-permute-start | bytes 1572872 | tf_op jit(solution)/shard_map/ppermute | solution.py:56
  119.0 24.0 %collective-permute-start.6 = (bf16[512,512]{0,1:T(8,128)(2,1)S(1)}, bf16[512,512]{0,1:T(8,128)(2,1)S(1)}, u32[]{:S(2)}, u32[]{:S(2)}) collective-permute-start(bf16[512,512]{0,1:T(8,128)(2,1)S(1)} %fusion.27), channel_id=1, source_target_pairs={{0,1},{1,0},{2,3},{3,2},{4,5},{5,4},{6,7},{7,6},{8,9},{9,8},{10,11... | collective-permute-start | bytes 1572872 | tf_op jit(solution)/shard_map/ppermute | solution.py:55
  137.2 15.1 %collective-permute-start.5 = (bf16[512,512]{0,1:T(8,128)(2,1)S(1)}, bf16[512,512]{0,1:T(8,128)(2,1)S(1)}, u32[]{:S(2)}, u32[]{:S(2)}) collective-permute-start(bf16[512,512]{0,1:T(8,128)(2,1)S(1)} %multiply_convert_fusion), channel_id=1, source_target_pairs={{0,2},{2,0},{1,3},{3,1},{4,6},{6,4},{5,7},{7,5},{8,10},{10,8},{9,1... | collective-permute-start | bytes 1572872 | tf_op jit(solution)/shard_map/ppermute | solution.py:54
  139.6 24.0 %collective-permute-start.2 = (bf16[512,512]{0,1:T(8,128)(2,1)S(1)}, bf16[512,512]{0,1:T(8,128)(2,1)S(1)}, u32[]{:S(2)}, u32[]{:S(2)}) collective-permute-start(bf16[512,512]{0,1:T(8,128)(2,1)S(1)} %fusion.27), channel_id=1, source_target_pairs={{0,2},{2,0},{1,3},{3,1},{4,6},{6,4},{5,7},{7,5},{8,10},{10,8},{9,1... | collective-permute-start | bytes 1572872 | tf_op jit(solution)/shard_map/ppermute | solution.py:54
  140.3 34.7 %collective-permute-start.1 = (bf16[512,512]{0,1:T(8,128)(2,1)S(1)}, bf16[512,512]{0,1:T(8,128)(2,1)S(1)}, u32[]{:S(2)}, u32[]{:S(2)}) collective-permute-start(bf16[512,512]{0,1:T(8,128)(2,1)S(1)} %multiply_convert_fusion), channel_id=1, source_target_pairs={{0,3},{1,2},{2,1},{3,0},{4,7},{5,6},{6,5},{7,4},{8,11},{9,10},{10,... | collective-permute-start | bytes 1572872 | tf_op jit(solution)/shard_map/ppermute | solution.py:56
  143.0 31.9 %collective-permute-start.3 = (bf16[512,512]{0,1:T(8,128)(2,1)S(1)}, bf16[512,512]{0,1:T(8,128)(2,1)S(1)}, u32[]{:S(2)}, u32[]{:S(2)}) collective-permute-start(bf16[512,512]{0,1:T(8,128)(2,1)S(1)} %multiply_convert_fusion), channel_id=1, source_target_pairs={{0,1},{1,0},{2,3},{3,2},{4,5},{5,4},{6,7},{7,6},{8,9},{9,8},{10,11... | collective-permute-start | bytes 1572872 | tf_op jit(solution)/shard_map/ppermute | solution.py:55

commit v4 on v3

--- a/solution.py
+++ b/solution.py
@@ -5,6 +5,7 @@
 
 N_ROUTED = 256
 TOP = 8
+CHUNKS = 2
 
 
 def slot_onehot(routes, real_count, expert_total, capacity):
@@ -35,25 +36,30 @@
         onehot.astype(tokens.dtype), tokens, preferred_element_type=jnp.float32
     ).astype(tokens.dtype)
     slot_rows = slot_rows.reshape(expert_count * half_count, capacity, width_model)
-    slot_block = lax.all_to_all(
-        slot_rows, ("expert", "xh"), split_axis=0, concat_axis=0, tiled=True
-    )
-    slot_block = slot_block.reshape(expert_count * half_count * capacity, width_model)
-    partner = lax.ppermute(slot_block, "core", [(c, (c + 1) % core_count) for c in range(core_count)])
     factor = 1.0 / (expert_count * capacity)
     swap_half = [(h, (h + 1) % half_count) for h in range(half_count)]
     swap_core = [(c, (c + 1) % core_count) for c in range(core_count)]
     replica_count = half_count * core_count
     swap_both = [(r, r ^ (replica_count - 1)) for r in range(replica_count)]
-    blocks = [[None] * 4, [None] * 4]
-    for i, rows in enumerate((slot_block, partner)):
+    per_chunk = capacity // CHUNKS
+    own = []
+    for q in range(CHUNKS):
+        piece = lax.all_to_all(
+            slot_rows[:, q * per_chunk:(q + 1) * per_chunk], ("expert", "xh"),
+            split_axis=0, concat_axis=0, tiled=True,
+        )
+        own.append(piece.reshape(expert_count * half_count * per_chunk, width_model))
+    partner = [lax.ppermute(piece, "core", swap_core) for piece in own]
+    blocks = {(q, s): [None] * 4 for q in range(CHUNKS) for s in range(2)}
+    work = [(q, 0, own[q]) for q in range(CHUNKS)] + [(q, 1, partner[q]) for q in range(CHUNKS)]
+    for q, s, rows in work:
         gate_pre = jnp.dot(rows, w_gate[0], preferred_element_type=jnp.float32)
         up_pre = jnp.dot(rows, w_up[0], preferred_element_type=jnp.float32)
         keys = (jax.nn.silu(gate_pre) * up_pre).astype(jnp.bfloat16)
-        blocks[i][0] = keys
-        blocks[i][2] = lax.ppermute(keys, "xh", swap_half)
-        blocks[1 - i][1] = lax.ppermute(keys, "core", swap_core)
-        blocks[1 - i][3] = lax.ppermute(keys, ("xh", "core"), swap_both)
+        blocks[(q, s)][0] = keys
+        blocks[(q, s)][2] = lax.ppermute(keys, "xh", swap_half)
+        blocks[(q, 1 - s)][1] = lax.ppermute(keys, "core", swap_core)
+        blocks[(q, 1 - s)][3] = lax.ppermute(keys, ("xh", "core"), swap_both)
     on_second_core = lax.axis_index("core") == 1
     on_second_half = lax.axis_index("xh") == 1
 
@@ -63,9 +69,10 @@
         return jnp.concatenate(by_half, axis=1)
 
     key_gram = None
-    for i in range(2):
+    for q, s, _ in work:
         part = jnp.einsum(
-            "rf,rg->fg", blocks[i][0], absolute(blocks[i]), preferred_element_type=jnp.float32
+            "rf,rg->fg", blocks[(q, s)][0], absolute(blocks[(q, s)]),
+            preferred_element_type=jnp.float32,
         )
         key_gram = part if key_gram is None else key_gram + part
     key_gram = key_gram * factor

time: 181 us -> 205 us (1.13)
  blocking collectives: 96.2 us -> 56.9 us
  waiting for transfers between devices: 30.4 us -> 55.9 us
  local copies, waits for them, and re-layouts: 0.04 us -> 25.1 us
  starting transfers between devices: 9.55 us -> 26.8 us
  matrix products: 42.9 us -> 37.5 us
    all_to_all x1, blocking collectives: 96.2 us -> 56.9 us  [body(): lax.all_to_all(slot_rows[:, q * per_chunk:(q + 1) * per_chunk], ('expert'...]
    all_to_all x0 -> x1, waiting for transfers between devices: none -> 34.8 us  [body(): lax.all_to_all(slot_rows[:, q * per_chunk:(q + 1) * per_chunk], ('expert'...]
    reshape x0 -> x2, local copies, waits for them, and re-layouts: none -> 13.6 us  [body(): piece.reshape(expert_count * half_count * per_chunk, width_model)]
    ppermute x7 -> x14, starting transfers between devices: 9.55 us -> 20.9 us  [the longest x2 7.24 us: body(): partner = [lax.ppermute(piece, 'core', swap_core) for piece in own]]
    slice x0 -> x1, local copies, waits for them, and re-layouts: none -> 11.2 us  [body(): slot_rows[:, q * per_chunk:(q + 1) * per_chunk]]
    ppermute x7 -> x14, waiting for transfers between devices: 30.4 us -> 21.1 us  [the longest x4 11.7 us: body(): blocks[q, s][2] = lax.ppermute(keys, 'xh', swap_half)]
    all_to_all x0 -> x1, starting transfers between devices: none -> 5.95 us  [body(): lax.all_to_all(slot_rows[:, q * per_chunk:(q + 1) * per_chunk], ('expert'...]
    dot_general x2 -> x4, matrix products: 16.5 us -> 10.6 us  [body(): up_pre = jnp.dot(rows, w_up[0], preferred_element_type=jnp.float32)]
  transfers between devices with their start and end apart: 7 -> 15, of which waited for: 3 -> 5; matrix products, arithmetic and copies ran while one was open for 18% -> 20% of each run, Pallas kernels for 0% -> 0%
where the time goes in v4:
time: 205 us; the launch traced here: 204 us
  blocking collectives  56.9 us (28%)
  waiting for transfers between devices  55.9 us (27%)
  matrix products  37.5 us (18%)
  starting transfers between devices  26.8 us (13%)
  local copies, waits for them, and re-layouts  25.1 us (12%)
    all_to_all x1, blocking collectives, body(): lax.all_to_all(slot_rows[:, q * per_chunk:(q + 1) * per_chunk], ('expert'...  56.9 us
    all_to_all x1, waiting for transfers between devices, body(): lax.all_to_all(slot_rows[:, q * per_chunk:(q + 1) * per_chunk], ('expert'...  34.8 us
    dot_general x4, matrix products, body(): gate_pre = jnp.dot(rows, w_gate[0], preferred_element_type=jnp.float32)  14.7 us
    reshape x2, local copies, waits for them, and re-layouts, body(): piece.reshape(expert_count * half_count * per_chunk, width_model)  13.6 us
    ppermute x4, waiting for transfers between devices, body(): blocks[q, s][2] = lax.ppermute(keys, 'xh', swap_half)  11.7 us
    slice x1, local copies, waits for them, and re-layouts, body(): slot_rows[:, q * per_chunk:(q + 1) * per_chunk]  11.2 us
    dot_general x4, matrix products, body(): up_pre = jnp.dot(rows, w_up[0], preferred_element_type=jnp.float32)  10.6 us
    ppermute x4, waiting for transfers between devices, body(): blocks[q, 1 - s][3] = lax.ppermute(keys, ('xh', 'core'), swap_both)  9.43 us
  transfers between devices with their start and end apart: 15, of which 5 were waited for; matrix products, arithmetic and copies ran while one was open for 20% of the time, Pallas kernels for 0%

profile of v4, /device:TPU:1, one launch (start us, length us, event | category | flops | bytes accessed | tf_op | source)
XLA Modules:
  0.0 204.4 jit_solution(1242017801520782946)
XLA Ops:
  0.0 0.7 fusion.60
  1.4 0.2 convolution_convert_fusion.1
  1.6 0.1 fusion.61
  1.7 7.1 %fusion = bf16[64,8,7168]{2,1,0:T(8,128)(2,1)} fusion(pred[512,256]{1,0:T(8,128)(4,1)S(1)} %bitcast.53, bf16[256,7168]{1,0:T(8,128)(2,1)} %param.5), kind=kOutput, calls=%fused_computation.1 | convolution fusion | flops 1882718208 | bytes 11141120 | tf_op jit(solution)/shard_map/dot_general | solution.py:35
  8.8 11.2 %fusion.68 = (bf16[64,4,7168]{2,1,0:T(4,128)(2,1)}, bf16[64,4,7168]{2,1,0:T(4,128)(2,1)}) fusion(bf16[64,8,7168]{2,1,0:T(8,128)(2,1)} %fusion), kind=kLoop, calls=%fused_computation.102 | loop fusion | bytes 14680064 | tf_op jit(solution)/shard_map/slice | solution.py:48
  20.0 56.9 %all_to_all.10 = bf16[64,4,7168]{2,1,0:T(4,128)(2,1)} all-to-all(bf16[64,4,7168]{2,1,0:T(4,128)(2,1)} %get-tuple-element.5), channel_id=1, replica_groups=mesh['expert'=32,'xh'=2,'core'=2] {'expert','xh'}, dimensions={0} | all-to-all | bytes 7340032 | tf_op jit(solution)/shard_map/all_to_all | solution.py:47
  76.9 6.0 %all-to-all-start = ((bf16[64,4,7168]{2,1,0:T(4,128)(2,1)}), bf16[64,4,7168]{2,1,0:T(4,128)(2,1)}, u32[]{:S(2)}, u32[]{:S(2)}) async-start(bf16[64,4,7168]{2,1,0:T(4,128)(2,1)} %get-tuple-element.6), calls=%async_computation | async-start | bytes 7340032 | tf_op jit(solution)/shard_map/all_to_all | solution.py:47
  82.8 6.7 %reshape.29 = bf16[256,7168]{1,0:T(8,128)(2,1)} reshape(bf16[64,4,7168]{2,1,0:T(4,128)(2,1)} %all_to_all.10) | data formatting | bytes 7340032 | tf_op jit(solution)/shard_map/reshape | solution.py:51
  89.6 2.2 %collective-permute-start.4 = (bf16[256,7168]{1,0:T(8,128)(2,1)}, bf16[256,7168]{1,0:T(8,128)(2,1)}, u32[]{:S(2)}, u32[]{:S(2)}) collective-permute-start(bf16[256,7168]{1,0:T(8,128)(2,1)} %reshape.29), channel_id=1, source_target_pairs={{0,1},{1,0},{2,3},{3,2},{4,5},{5,4},{6,7},{7,6},{8,9},{9,8},{10,11... | collective-permute-start | bytes 11010056 | tf_op jit(solution)/shard_map/ppermute | solution.py:52
  91.8 34.8 %all-to-all-done = bf16[64,4,7168]{2,1,0:T(4,128)(2,1)} async-done(((bf16[64,4,7168]{2,1,0:T(4,128)(2,1)}), bf16[64,4,7168]{2,1,0:T(4,128)(2,1)}, u32[]{:S(2)}, u32[]{:S(2)}) %all-to-all-start) | async-done | bytes 3670048 | tf_op jit(solution)/shard_map/all_to_all | solution.py:47
  126.6 0.0 slice-start.2
  126.6 6.9 %reshape.28 = bf16[256,7168]{1,0:T(8,128)(2,1)} reshape(bf16[64,4,7168]{2,1,0:T(4,128)(2,1)} %all-to-all-done) | data formatting | bytes 7340032 | tf_op jit(solution)/shard_map/reshape | solution.py:51
  133.5 0.0 copy-start.1
  133.5 5.0 %collective-permute-start = (bf16[256,7168]{1,0:T(8,128)(2,1)}, bf16[256,7168]{1,0:T(8,128)(2,1)S(1)}, u32[]{:S(2)}, u32[]{:S(2)}) collective-permute-start(bf16[256,7168]{1,0:T(8,128)(2,1)} %reshape.28), channel_id=1, source_target_pairs={{0,1},{1,0},{2,3},{3,2},{4,5},{5,4},{6,7},{7,6},{8,9},{9,8},{10,11... | collective-permute-start | bytes 11010056 | tf_op jit(solution)/shard_map/ppermute | solution.py:52
  138.5 6.4 %fusion.15 = f32[256,512]{1,0:T(8,128)S(1)} fusion(bf16[256,7168]{1,0:T(8,128)(2,1)} %reshape.28, bf16[1,7168,512]{2,1,0:T(8,128)(2,1)} %param.8), kind=kOutput, calls=%fused_computation.16 | convolution fusion | flops 1879048192 | bytes 11534336 | tf_op jit(solution)/shard_map/dot_general | solution.py:56
  144.9 0.0 slice-done.2
  144.9 0.0 copy-done.1
  144.9 0.0 slice-done.3
  145.0 0.0 copy-start
  145.0 0.0 slice-start.1
  145.0 2.2 %fusion.26 = bf16[256,512]{1,0:T(8,128)(2,1)S(1)} fusion(bf16[256,7168]{1,0:T(8,128)(2,1)S(1)} %copy-done.1, bf16[1,7168,512]{2,1,0:T(8,128)(2,1)S(1)} %bitcast.57, f32[256,512]{1,0:T(8,128)S(1)} %fusion.15), kind=kOutput, calls=%fused_computation.22 | convolution fusion | flops 1879834624 | bytes 11796480 | tf_op jit(solution)/shard_map/dot_general | solution.py:57
  147.2 0.3 collective-permute-start.2
  147.4 0.3 collective-permute-start.10
  147.7 0.0 slice-done
  147.7 0.0 copy-done
  147.7 0.2 slice-done.1
  148.0 2.0 fusion.11
  150.0 2.2 %fusion.23 = bf16[256,512]{1,0:T(8,128)(2,1)S(1)} fusion(bf16[256,7168]{1,0:T(8,128)(2,1)S(1)} %copy-done, bf16[1,7168,512]{2,1,0:T(8,128)(2,1)S(1)} %bitcast.57, f32[256,512]{1,0:T(8,128)S(1)} %fusion.11), kind=kOutput, calls=%fused_computation.21 | convolution fusion | flops 1879834624 | bytes 11796480 | tf_op jit(solution)/shard_map/dot_general | solution.py:57
  152.2 2.8 %collective-permute-start.6 = (bf16[256,512]{1,0:T(8,128)(2,1)S(1)}, bf16[256,512]{1,0:T(8,128)(2,1)S(1)}, u32[]{:S(2)}, u32[]{:S(2)}) collective-permute-start(bf16[256,512]{1,0:T(8,128)(2,1)S(1)} %fusion.23), channel_id=1, source_target_pairs={{0,2},{2,0},{1,3},{3,1},{4,6},{6,4},{5,7},{7,5},{8,10},{10,8},{9,1... | collective-permute-start | bytes 786440 | tf_op jit(solution)/shard_map/ppermute | solution.py:60
  155.0 0.0 collective-permute-done.4
  155.0 4.2 %fusion.9 = f32[256,512]{1,0:T(8,128)S(1)} fusion(bf16[256,7168]{1,0:T(8,128)(2,1)} %collective-permute-done.4, bf16[1,7168,512]{2,1,0:T(8,128)(2,1)S(1)} %bitcast.55), kind=kOutput, calls=%fused_computation.10 | convolution fusion | flops 1879048192 | bytes 11534336 | tf_op jit(solution)/shard_map/dot_general | solution.py:56
  159.2 4.1 %multiply_convert_fusion = bf16[256,512]{1,0:T(8,128)(2,1)S(1)} fusion(f32[256,512]{1,0:T(8,128)S(1)} %fusion.9, bf16[256,7168]{1,0:T(8,128)(2,1)} %collective-permute-done.4, bf16[1,7168,512]{2,1,0:T(8,128)(2,1)S(1)} %bitcast.57), kind=kOutput, calls=%fused_computation.55 | convolution fusion | flops 1879834624 | bytes 11796480 | tf_op jit(solution)/shard_map/dot_general | solution.py:57
  163.3 0.9 collective-permute-start.5
  164.2 0.0 collective-permute-done
  164.2 0.0 collective-permute-start.7
  164.2 2.0 %fusion.13 = f32[256,512]{1,0:T(8,128)S(1)} fusion(bf16[256,7168]{1,0:T(8,128)(2,1)S(1)} %collective-permute-done, bf16[1,7168,512]{2,1,0:T(8,128)(2,1)S(1)} %bitcast.55), kind=kOutput, calls=%fused_computation.14 | convolution fusion | flops 1879048192 | bytes 11534336 | tf_op jit(solution)/shard_map/dot_general | solution.py:56
  166.3 2.2 %multiply_convert_fusion.1 = bf16[256,512]{1,0:T(8,128)(2,1)S(1)} fusion(f32[256,512]{1,0:T(8,128)S(1)} %fusion.13, bf16[256,7168]{1,0:T(8,128)(2,1)S(1)} %collective-permute-done, bf16[1,7168,512]{2,1,0:T(8,128)(2,1)S(1)} %bitcast.57), kind=kOutput, calls=%fused_computation.56 | convolution fusion | flops 1879834624 | bytes 11796480 | tf_op jit(solution)/shard_map/dot_general | solution.py:57
  168.4 0.0 collective-permute-done.6
  168.5 3.0 %collective-permute-start.8 = (bf16[256,512]{1,0:T(8,128)(2,1)S(1)}, bf16[256,512]{1,0:T(8,128)(2,1)S(1)}, u32[]{:S(2)}, u32[]{:S(2)}) collective-permute-start(bf16[256,512]{1,0:T(8,128)(2,1)S(1)} %fusion.26), channel_id=1, source_target_pairs={{0,3},{1,2},{2,1},{3,0},{4,7},{5,6},{6,5},{7,4},{8,11},{9,10},{10,... | collective-permute-start | bytes 786440 | tf_op jit(solution)/shard_map/ppermute | solution.py:62
  171.5 2.4 %collective-permute-done.5 = bf16[256,512]{1,0:T(8,128)(2,1)S(1)} collective-permute-done((bf16[256,512]{1,0:T(8,128)(2,1)S(1)}, bf16[256,512]{1,0:T(8,128)(2,1)S(1)}, u32[]{:S(2)}, u32[]{:S(2)}) %collective-permute-start.5) | collective-permute-done | bytes 262176 | tf_op jit(solution)/shard_map/ppermute | solution.py:62
  173.8 0.5 collective-permute-start.1
  174.3 0.0 collective-permute-done.7
  174.3 0.1 collective-permute-start.3
  174.4 0.1 broadcast_select_fusion.27
  174.5 0.7 fusion.37
  175.3 0.0 collective-permute-done.2
  175.3 2.7 %collective-permute-start.11 = (bf16[256,512]{1,0:T(8,128)(2,1)S(1)}, bf16[256,512]{1,0:T(8,128)(2,1)S(1)}, u32[]{:S(2)}, u32[]{:S(2)}) collective-permute-start(bf16[256,512]{1,0:T(8,128)(2,1)S(1)} %fusion.23), channel_id=1, source_target_pairs={{0,3},{1,2},{2,1},{3,0},{4,7},{5,6},{6,5},{7,4},{8,11},{9,10},{10,... | collective-permute-start | bytes 786440 | tf_op jit(solution)/shard_map/ppermute | solution.py:62
  178.0 7.1 %collective-permute-done.1 = bf16[256,512]{1,0:T(8,128)(2,1)S(1)} collective-permute-done((bf16[256,512]{1,0:T(8,128)(2,1)S(1)}, bf16[256,512]{1,0:T(8,128)(2,1)S(1)}, u32[]{:S(2)}, u32[]{:S(2)}) %collective-permute-start.1) | collective-permute-done | bytes 262176 | tf_op jit(solution)/shard_map/ppermute | solution.py:62
  185.1 0.0 collective-permute-start.13
  185.1 0.0 collective-permute-done.3
  185.1 2.1 %collective-permute-start.9 = (bf16[256,512]{1,0:T(8,128)(2,1)S(1)}, bf16[256,512]{1,0:T(8,128)(2,1)S(1)}, u32[]{:S(2)}, u32[]{:S(2)}) collective-permute-start(bf16[256,512]{1,0:T(8,128)(2,1)S(1)} %multiply_convert_fusion.1), channel_id=1, source_target_pairs={{0,2},{2,0},{1,3},{3,1},{4,6},{6,4},{5,7},{7,5},{8,10},{10,8},{9,1... | collective-permute-start | bytes 786440 | tf_op jit(solution)/shard_map/ppermute | solution.py:60
  187.1 0.1 broadcast_select_fusion.31
  187.2 0.7 fusion.29
  188.0 0.0 collective-permute-done.10
  188.0 1.0 collective-permute-start.12
  189.0 0.0 collective-permute-done.8
  189.0 6.9 %collective-permute-done.9 = bf16[256,512]{1,0:T(8,128)(2,1)S(1)} collective-permute-done((bf16[256,512]{1,0:T(8,128)(2,1)S(1)}, bf16[256,512]{1,0:T(8,128)(2,1)S(1)}, u32[]{:S(2)}, u32[]{:S(2)}) %collective-permute-start.9) | collective-permute-done | bytes 262176 | tf_op jit(solution)/shard_map/ppermute | solution.py:60
  195.8 0.1 broadcast_select_fusion.23
  195.9 0.7 fusion.45
  196.7 0.0 collective-permute-done.11
  196.7 0.0 collective-permute-done.13
  196.7 4.8 %collective-permute-done.12 = bf16[256,512]{1,0:T(8,128)(2,1)S(1)} collective-permute-done((bf16[256,512]{1,0:T(8,128)(2,1)S(1)}, bf16[256,512]{1,0:T(8,128)(2,1)S(1)}, u32[]{:S(2)}, u32[]{:S(2)}) %collective-permute-start.12) | collective-permute-done | bytes 262176 | tf_op jit(solution)/shard_map/ppermute | solution.py:60
  201.5 0.1 broadcast_select_fusion.19
  201.6 2.9 %multiply_bitcast_fusion = f32[1,512,2048]{2,1,0:T(8,128)} fusion(f32[512,2048]{1,0:T(8,128)S(1)} %fusion.45, f32[512,2048]{1,0:T(8,128)S(1)} %fusion.29, f32[512,2048]{1,0:T(8,128)S(1)} %fusion.37, bf16[256,512]{1,0:T(8,128)(2,1)S(1)} %multiply_convert_fusion, bf16[256,512]{1,0:T(8,128)(2,1)S(1)} %get-tuple-element.10, ...), kind=kOutput, calls=%fused_computation.18 | convolution fusion | flops 545259520 | bytes 18087936 | tf_op jit(solution)/shard_map/rf,rg->fg/dot_general | solution.py:73
  (7 shorter events, 0.1 us)
Async XLA Ops:
  76.9 49.7 %all-to-all-start = ((bf16[64,4,7168]{2,1,0:T(4,128)(2,1)}), bf16[64,4,7168]{2,1,0:T(4,128)(2,1)}, u32[]{:S(2)}, u32[]{:S(2)}) async-start(bf16[64,4,7168]{2,1,0:T(4,128)(2,1)} %get-tuple-element.6), calls=%async_computation | async-start | bytes 7340032 | tf_op jit(solution)/shard_map/all_to_all | solution.py:47
  89.6 65.5 %collective-permute-start.4 = (bf16[256,7168]{1,0:T(8,128)(2,1)}, bf16[256,7168]{1,0:T(8,128)(2,1)}, u32[]{:S(2)}, u32[]{:S(2)}) collective-permute-start(bf16[256,7168]{1,0:T(8,128)(2,1)} %reshape.29), channel_id=1, source_target_pairs={{0,1},{1,0},{2,3},{3,2},{4,5},{5,4},{6,7},{7,6},{8,9},{9,8},{10,11... | collective-permute-start | bytes 11010056 | tf_op jit(solution)/shard_map/ppermute | solution.py:52
  126.6 18.3 %slice-start.2 = ((s8[7340032]{0:T(1024)(128)(4,1)}), s8[3145728]{0:T(1024)(128)(4,1)S(1)}, s32[]{:S(2)}) async-start(s8[7340032]{0:T(1024)(128)(4,1)} %bitcast.56), calls=%async_computation.4 | async-start | bytes 6291456
  133.5 11.4 %copy-start.1 = (bf16[256,7168]{1,0:T(8,128)(2,1)S(1)}, bf16[256,7168]{1,0:T(8,128)(2,1)}, u32[]{:S(2)}) copy-start(bf16[256,7168]{1,0:T(8,128)(2,1)} %reshape.28) | copy-start | bytes 11010052
  133.5 11.5 %slice-start.3 = ((s8[7340032]{0:T(1024)(128)(4,1)}), s8[4194304]{0:T(1024)(128)(4,1)S(1)}, s32[]{:S(2)}) async-start(s8[7340032]{0:T(1024)(128)(4,1)} %bitcast.56), calls=%async_computation.5 | async-start | bytes 8388608
  133.5 30.7 %collective-permute-start = (bf16[256,7168]{1,0:T(8,128)(2,1)}, bf16[256,7168]{1,0:T(8,128)(2,1)S(1)}, u32[]{:S(2)}, u32[]{:S(2)}) collective-permute-start(bf16[256,7168]{1,0:T(8,128)(2,1)} %reshape.28), channel_id=1, source_target_pairs={{0,1},{1,0},{2,3},{3,2},{4,5},{5,4},{6,7},{7,6},{8,9},{9,8},{10,11... | collective-permute-start | bytes 11010056 | tf_op jit(solution)/shard_map/ppermute | solution.py:52
  138.5 9.2 %slice-start = ((s8[7340032]{0:T(1024)(128)(4,1)}), s8[4194304]{0:T(1024)(128)(4,1)S(1)}, s32[]{:S(2)}) async-start(s8[7340032]{0:T(1024)(128)(4,1)} %bitcast.54), calls=%async_computation.2 | async-start | bytes 8388608
  145.0 2.8 %copy-start = (bf16[256,7168]{1,0:T(8,128)(2,1)S(1)}, bf16[256,7168]{1,0:T(8,128)(2,1)}, u32[]{:S(2)}) copy-start(bf16[256,7168]{1,0:T(8,128)(2,1)} %reshape.29) | copy-start | bytes 11010052
  145.0 3.0 %slice-start.1 = ((s8[7340032]{0:T(1024)(128)(4,1)}), s8[3145728]{0:T(1024)(128)(4,1)S(1)}, s32[]{:S(2)}) async-start(s8[7340032]{0:T(1024)(128)(4,1)} %bitcast.54), calls=%async_computation.3 | async-start | bytes 6291456
  147.2 28.1 %collective-permute-start.2 = (bf16[256,512]{1,0:T(8,128)(2,1)S(1)}, bf16[256,512]{1,0:T(8,128)(2,1)S(1)}, u32[]{:S(2)}, u32[]{:S(2)}) collective-permute-start(bf16[256,512]{1,0:T(8,128)(2,1)S(1)} %fusion.26), channel_id=1, source_target_pairs={{0,2},{2,0},{1,3},{3,1},{4,6},{6,4},{5,7},{7,5},{8,10},{10,8},{9,1... | collective-permute-start | bytes 786440 | tf_op jit(solution)/shard_map/ppermute | solution.py:60
  147.4 40.5 %collective-permute-start.10 = (bf16[256,512]{1,0:T(8,128)(2,1)S(1)}, bf16[256,512]{1,0:T(8,128)(2,1)S(1)}, u32[]{:S(2)}, u32[]{:S(2)}) collective-permute-start(bf16[256,512]{1,0:T(8,128)(2,1)S(1)} %fusion.26), channel_id=1, source_target_pairs={{0,1},{1,0},{2,3},{3,2},{4,5},{5,4},{6,7},{7,6},{8,9},{9,8},{10,11... | collective-permute-start | bytes 786440 | tf_op jit(solution)/shard_map/ppermute | solution.py:61
  152.2 16.2 %collective-permute-start.6 = (bf16[256,512]{1,0:T(8,128)(2,1)S(1)}, bf16[256,512]{1,0:T(8,128)(2,1)S(1)}, u32[]{:S(2)}, u32[]{:S(2)}) collective-permute-start(bf16[256,512]{1,0:T(8,128)(2,1)S(1)} %fusion.23), channel_id=1, source_target_pairs={{0,2},{2,0},{1,3},{3,1},{4,6},{6,4},{5,7},{7,5},{8,10},{10,8},{9,1... | collective-permute-start | bytes 786440 | tf_op jit(solution)/shard_map/ppermute | solution.py:60
  163.3 10.5 %collective-permute-start.5 = (bf16[256,512]{1,0:T(8,128)(2,1)S(1)}, bf16[256,512]{1,0:T(8,128)(2,1)S(1)}, u32[]{:S(2)}, u32[]{:S(2)}) collective-permute-start(bf16[256,512]{1,0:T(8,128)(2,1)S(1)} %multiply_convert_fusion), channel_id=1, source_target_pairs={{0,3},{1,2},{2,1},{3,0},{4,7},{5,6},{6,5},{7,4},{8,11},{9,10},{10,... | collective-permute-start | bytes 786440 | tf_op jit(solution)/shard_map/ppermute | solution.py:62
  164.2 10.1 %collective-permute-start.7 = (bf16[256,512]{1,0:T(8,128)(2,1)S(1)}, bf16[256,512]{1,0:T(8,128)(2,1)S(1)}, u32[]{:S(2)}, u32[]{:S(2)}) collective-permute-start(bf16[256,512]{1,0:T(8,128)(2,1)S(1)} %multiply_convert_fusion), channel_id=1, source_target_pairs={{0,1},{1,0},{2,3},{3,2},{4,5},{5,4},{6,7},{7,6},{8,9},{9,8},{10,11... | collective-permute-start | bytes 786440 | tf_op jit(solution)/shard_map/ppermute | solution.py:61
  168.5 20.5 %collective-permute-start.8 = (bf16[256,512]{1,0:T(8,128)(2,1)S(1)}, bf16[256,512]{1,0:T(8,128)(2,1)S(1)}, u32[]{:S(2)}, u32[]{:S(2)}) collective-permute-start(bf16[256,512]{1,0:T(8,128)(2,1)S(1)} %fusion.26), channel_id=1, source_target_pairs={{0,3},{1,2},{2,1},{3,0},{4,7},{5,6},{6,5},{7,4},{8,11},{9,10},{10,... | collective-permute-start | bytes 786440 | tf_op jit(solution)/shard_map/ppermute | solution.py:62
  173.8 11.2 %collective-permute-start.1 = (bf16[256,512]{1,0:T(8,128)(2,1)S(1)}, bf16[256,512]{1,0:T(8,128)(2,1)S(1)}, u32[]{:S(2)}, u32[]{:S(2)}) collective-permute-start(bf16[256,512]{1,0:T(8,128)(2,1)S(1)} %multiply_convert_fusion.1), channel_id=1, source_target_pairs={{0,3},{1,2},{2,1},{3,0},{4,7},{5,6},{6,5},{7,4},{8,11},{9,10},{10,... | collective-permute-start | bytes 786440 | tf_op jit(solution)/shard_map/ppermute | solution.py:62
  174.3 10.7 %collective-permute-start.3 = (bf16[256,512]{1,0:T(8,128)(2,1)S(1)}, bf16[256,512]{1,0:T(8,128)(2,1)S(1)}, u32[]{:S(2)}, u32[]{:S(2)}) collective-permute-start(bf16[256,512]{1,0:T(8,128)(2,1)S(1)} %multiply_convert_fusion.1), channel_id=1, source_target_pairs={{0,1},{1,0},{2,3},{3,2},{4,5},{5,4},{6,7},{7,6},{8,9},{9,8},{10,11... | collective-permute-start | bytes 786440 | tf_op jit(solution)/shard_map/ppermute | solution.py:61
  175.3 21.4 %collective-permute-start.11 = (bf16[256,512]{1,0:T(8,128)(2,1)S(1)}, bf16[256,512]{1,0:T(8,128)(2,1)S(1)}, u32[]{:S(2)}, u32[]{:S(2)}) collective-permute-start(bf16[256,512]{1,0:T(8,128)(2,1)S(1)} %fusion.23), channel_id=1, source_target_pairs={{0,3},{1,2},{2,1},{3,0},{4,7},{5,6},{6,5},{7,4},{8,11},{9,10},{10,... | collective-permute-start | bytes 786440 | tf_op jit(solution)/shard_map/ppermute | solution.py:62
  185.1 11.6 %collective-permute-start.13 = (bf16[256,512]{1,0:T(8,128)(2,1)S(1)}, bf16[256,512]{1,0:T(8,128)(2,1)S(1)}, u32[]{:S(2)}, u32[]{:S(2)}) collective-permute-start(bf16[256,512]{1,0:T(8,128)(2,1)S(1)} %fusion.23), channel_id=1, source_target_pairs={{0,1},{1,0},{2,3},{3,2},{4,5},{5,4},{6,7},{7,6},{8,9},{9,8},{10,11... | collective-permute-start | bytes 786440 | tf_op jit(solution)/shard_map/ppermute | solution.py:61
  185.1 10.8 %collective-permute-start.9 = (bf16[256,512]{1,0:T(8,128)(2,1)S(1)}, bf16[256,512]{1,0:T(8,128)(2,1)S(1)}, u32[]{:S(2)}, u32[]{:S(2)}) collective-permute-start(bf16[256,512]{1,0:T(8,128)(2,1)S(1)} %multiply_convert_fusion.1), channel_id=1, source_target_pairs={{0,2},{2,0},{1,3},{3,1},{4,6},{6,4},{5,7},{7,5},{8,10},{10,8},{9,1... | collective-permute-start | bytes 786440 | tf_op jit(solution)/shard_map/ppermute | solution.py:60
  188.0 13.5 %collective-permute-start.12 = (bf16[256,512]{1,0:T(8,128)(2,1)S(1)}, bf16[256,512]{1,0:T(8,128)(2,1)S(1)}, u32[]{:S(2)}, u32[]{:S(2)}) collective-permute-start(bf16[256,512]{1,0:T(8,128)(2,1)S(1)} %multiply_convert_fusion), channel_id=1, source_target_pairs={{0,2},{2,0},{1,3},{3,1},{4,6},{6,4},{5,7},{7,5},{8,10},{10,8},{9,1... | collective-permute-start | bytes 786440 | tf_op jit(solution)/shard_map/ppermute | solution.py:60

commit v5 on v1

--- a/solution.py
+++ b/solution.py
@@ -39,19 +39,29 @@
         slot_rows, ("expert", "xh"), split_axis=0, concat_axis=0, tiled=True
     )
     slot_block = slot_block.reshape(expert_count * half_count * capacity, width_model)
-    slot_block = lax.all_gather(slot_block, "core", axis=0, tiled=True)
-    gate_pre = jnp.dot(slot_block, w_gate[0], preferred_element_type=jnp.float32)
-    up_pre = jnp.dot(slot_block, w_up[0], preferred_element_type=jnp.float32)
-    own_keys = (jax.nn.silu(gate_pre) * up_pre).astype(jnp.bfloat16)
+    partner = lax.ppermute(slot_block, "core", [(c, (c + 1) % core_count) for c in range(core_count)])
     factor = 1.0 / (expert_count * capacity)
+    replica_count = half_count * core_count
+    halves = []
+    for rows in (slot_block, partner):
+        gate_pre = jnp.dot(rows, w_gate[0], preferred_element_type=jnp.float32)
+        up_pre = jnp.dot(rows, w_up[0], preferred_element_type=jnp.float32)
+        halves.append((jax.nn.silu(gate_pre) * up_pre).astype(jnp.bfloat16))
+    in_order = jnp.concatenate(halves, axis=0)
+    swapped = jnp.concatenate(halves[::-1], axis=0)
+    canonical = jnp.where(lax.axis_index("core") == 0, in_order, swapped)
+    sent = jnp.broadcast_to(in_order[None], (replica_count,) + in_order.shape)
+    received = lax.all_to_all(sent, ("xh", "core"), split_axis=0, concat_axis=0, tiled=True)
+    rows_half = in_order.shape[0] // 2
+    columns = []
+    for replica in range(replica_count):
+        block = received[replica]
+        if replica % core_count == 1:
+            block = jnp.concatenate([block[rows_half:], block[:rows_half]], axis=0)
+        columns.append(block)
+    every = jnp.concatenate(columns, axis=1)
     key_gram = (
-        jnp.einsum(
-            "rf,rg->fg",
-            own_keys,
-            lax.all_gather(own_keys, ("xh", "core"), axis=1, tiled=True),
-            preferred_element_type=jnp.float32,
-        )
-        * factor
+        jnp.einsum("rf,rg->fg", canonical, every, preferred_element_type=jnp.float32) * factor
     )
     return key_gram[None]
 

time: 215 us -> 195 us (0.907)
  waiting for transfers between devices: 68.3 us -> 52.2 us
  between operations: 14.1 us -> 0.78 us
  starting transfers between devices: 0.04 us -> 7.78 us
  local copies, waits for them, and re-layouts: 0.04 us -> 5.72 us
  matrix products: 35.3 us -> 30.4 us
    all_gather x2 -> x0, waiting for transfers between devices: 68.3 us -> none  [the longest x1 39.9 us: body(): lax.all_gather(own_keys, ('xh', 'core'), axis=1, tiled=True)]
    all_to_all x0 -> x1, waiting for transfers between devices: none -> 48.8 us  [body(): lax.all_to_all(sent, ('xh', 'core'), split_axis=0, concat_axis=0, tiled=T...]
    all_to_all x0 -> x1, starting transfers between devices: none -> 5.18 us  [body(): lax.all_to_all(sent, ('xh', 'core'), split_axis=0, concat_axis=0, tiled=T...]
    dot_general x3 -> x5, matrix products: 31 us -> 26 us  [the longest x2 11.2 us: body(): up_pre = jnp.dot(rows, w_up[0], preferred_element_type=jnp.float32)]
    ppermute x0 -> x1, waiting for transfers between devices: none -> 3.41 us  [body(): lax.ppermute(slot_block, 'core', [(c, (c + 1) % core_count) for c in rang...]
    ppermute x0 -> x1, starting transfers between devices: none -> 2.6 us  [body(): lax.ppermute(slot_block, 'core', [(c, (c + 1) % core_count) for c in rang...]
    broadcast_in_dim x0 -> x1, local copies, waits for them, and re-layouts: none -> 2.34 us  [body(): sent = jnp.broadcast_to(in_order[None], (replica_count,) + in_order.shape)]
  transfers between devices with their start and end apart: 2 -> 2, of which waited for: 2 -> 2; matrix products, arithmetic and copies ran while one was open for 0% -> 4% of each run, Pallas kernels for 0% -> 0%
where the time goes in v5:
time: 195 us; the launch traced here: 194 us
  blocking collectives  96.5 us (49%)
  waiting for transfers between devices  52.2 us (27%)
  matrix products  30.4 us (16%)
  starting transfers between devices  7.78 us (4%)
  local copies, waits for them, and re-layouts  5.72 us (3%)
    all_to_all x1, blocking collectives, body(): lax.all_to_all(slot_rows, ('expert', 'xh'), split_axis=0, concat_axis=0,...  96.5 us
    all_to_all x1, waiting for transfers between devices, body(): lax.all_to_all(sent, ('xh', 'core'), split_axis=0, concat_axis=0, tiled=T...  48.8 us
    dot_general x2, matrix products, body(): up_pre = jnp.dot(rows, w_up[0], preferred_element_type=jnp.float32)  11.2 us
    dot_general x2, matrix products, body(): gate_pre = jnp.dot(rows, w_gate[0], preferred_element_type=jnp.float32)  10.3 us
    all_to_all x1, starting transfers between devices, body(): lax.all_to_all(sent, ('xh', 'core'), split_axis=0, concat_axis=0, tiled=T...  5.18 us
    dot_general x1, matrix products, body(): jnp.einsum('rf,rg->fg', canonical, every, preferred_element_type=jnp.floa...  4.51 us
    dot_general x1, matrix products, body(): jnp.dot(onehot.astype(tokens.dtype), tokens, preferred_element_type=jnp.f...  4.26 us
  transfers between devices with their start and end apart: 2, of which 2 were waited for; matrix products, arithmetic and copies ran while one was open for 4% of the time, Pallas kernels for 0%

profile of v5, /device:TPU:1, one launch (start us, length us, event | category | flops | bytes accessed | tf_op | source)
XLA Modules:
  0.0 194.3 jit_solution(7779377896322808061)
XLA Ops:
  0.7 0.7 fusion.32
  1.4 0.2 convolution_convert_fusion.1
  1.6 0.1 fusion.33
  1.7 0.0 slice-start
  1.7 4.3 %fusion = bf16[64,8,7168]{2,1,0:T(8,128)(2,1)S(1)} fusion(pred[512,256]{1,0:T(8,128)(4,1)S(1)} %bitcast.47, bf16[256,7168]{1,0:T(8,128)(2,1)} %param.5), kind=kOutput, calls=%fused_computation.1 | convolution fusion | flops 1882718208 | bytes 11141120 | tf_op jit(solution)/shard_map/dot_general | solution.py:34
  6.0 0.0 slice-start.1
  6.0 96.5 %all_to_all.10 = bf16[64,8,7168]{2,1,0:T(8,128)(2,1)S(1)} all-to-all(bf16[64,8,7168]{2,1,0:T(8,128)(2,1)S(1)} %fusion), channel_id=1, replica_groups=mesh['expert'=32,'xh'=2,'core'=2] {'expert','xh'}, dimensions={0} | all-to-all | bytes 14680064 | tf_op jit(solution)/shard_map/all_to_all | solution.py:38
  102.5 0.0 slice-start.2
  102.5 0.0 slice-start.3
  102.5 2.6 %collective-permute-start = (bf16[512,7168]{1,0:T(8,128)(2,1)S(1)}, bf16[512,7168]{1,0:T(8,128)(2,1)}, u32[]{:S(2)}, u32[]{:S(2)}) collective-permute-start(bf16[512,7168]{1,0:T(8,128)(2,1)S(1)} %bitcast.46), channel_id=1, source_target_pairs={{0,1},{1,0},{2,3},{3,2},{4,5},{5,4},{6,7},{7,6},{8,9},{9,8},{10,11... | collective-permute-start | bytes 22020104 | tf_op jit(solution)/shard_map/ppermute | solution.py:42
  105.1 0.0 slice-done
  105.1 0.0 slice-done.1
  105.1 3.9 %fusion.7 = f32[512,512]{1,0:T(8,128)S(1)} fusion(bf16[1,7168,512]{2,1,0:T(8,128)(2,1)S(1)} %bitcast.49, bf16[64,8,7168]{2,1,0:T(8,128)(2,1)S(1)} %all_to_all.10), kind=kOutput, calls=%fused_computation.8 | convolution fusion | flops 3758096384 | bytes 15728640 | tf_op jit(solution)/shard_map/dot_general | solution.py:47
  109.0 0.0 slice-done.2
  109.0 0.0 slice-done.3
  109.1 4.0 %fusion.26 = bf16[512,512]{1,0:T(8,128)(2,1)S(1)} fusion(bf16[1,7168,512]{2,1,0:T(8,128)(2,1)S(1)} %bitcast.51, f32[512,512]{1,0:T(8,128)S(1)} %fusion.7, bf16[64,8,7168]{2,1,0:T(8,128)(2,1)S(1)} %all_to_all.10), kind=kOutput, calls=%fused_computation.24 | convolution fusion | flops 3759669248 | bytes 16252928 | tf_op jit(solution)/shard_map/dot_general | solution.py:48
  113.1 3.4 %collective-permute-done = bf16[512,7168]{1,0:T(8,128)(2,1)} collective-permute-done((bf16[512,7168]{1,0:T(8,128)(2,1)S(1)}, bf16[512,7168]{1,0:T(8,128)(2,1)}, u32[]{:S(2)}, u32[]{:S(2)}) %collective-permute-start) | collective-permute-done | bytes 7340064 | tf_op jit(solution)/shard_map/ppermute | solution.py:42
  116.5 6.4 %fusion.5 = f32[512,512]{1,0:T(8,128)S(1)} fusion(bf16[512,7168]{1,0:T(8,128)(2,1)} %collective-permute-done, bf16[1,7168,512]{2,1,0:T(8,128)(2,1)S(1)} %bitcast.49), kind=kOutput, calls=%fused_computation.6 | convolution fusion | flops 3758096384 | bytes 15728640 | tf_op jit(solution)/shard_map/dot_general | solution.py:47
  122.9 7.2 %multiply_convert_fusion = bf16[512,512]{1,0:T(8,128)(2,1)S(1)} fusion(f32[512,512]{1,0:T(8,128)S(1)} %fusion.5, bf16[512,7168]{1,0:T(8,128)(2,1)} %collective-permute-done, bf16[1,7168,512]{2,1,0:T(8,128)(2,1)S(1)} %bitcast.51), kind=kOutput, calls=%fused_computation.32 | convolution fusion | flops 3759669248 | bytes 16252928 | tf_op jit(solution)/shard_map/dot_general | solution.py:48
  130.1 0.1 pad_maximum_fusion
  130.1 2.3 %broadcast_in_dim.7 = bf16[4,1024,512]{2,1,0:T(8,128)(2,1)} broadcast(bf16[1024,512]{1,0:T(8,128)(2,1)S(1)} %pad_maximum_fusion), dimensions={1,2} | broadcast | bytes 5242880 | tf_op jit(solution)/shard_map/broadcast_in_dim | solution.py:53
  132.5 5.2 %all-to-all-start.1 = ((bf16[4,1024,512]{2,1,0:T(8,128)(2,1)}), bf16[4,1024,512]{2,1,0:T(8,128)(2,1)}, u32[]{:S(2)}, u32[]{:S(2)}) async-start(bf16[4,1024,512]{2,1,0:T(8,128)(2,1)} %broadcast_in_dim.7), calls=%async_computation.1 | async-start | bytes 8388608 | tf_op jit(solution)/shard_map/all_to_all | solution.py:54
  137.7 48.8 %all-to-all-done.1 = bf16[4,1024,512]{2,1,0:T(8,128)(2,1)} async-done(((bf16[4,1024,512]{2,1,0:T(8,128)(2,1)}), bf16[4,1024,512]{2,1,0:T(8,128)(2,1)}, u32[]{:S(2)}, u32[]{:S(2)}) %all-to-all-start.1) | async-done | bytes 4194336 | tf_op jit(solution)/shard_map/all_to_all | solution.py:54
  186.4 1.7 slice_bitcast_fusion.5
  188.1 1.7 slice_bitcast_fusion.1
  189.8 4.5 %multiply_bitcast_fusion = f32[1,512,2048]{2,1,0:T(8,128)} fusion(bf16[512,512]{1,0:T(8,128)(2,1)S(1)} %get-tuple-element.8, bf16[512,512]{1,0:T(8,128)(2,1)S(1)} %get-tuple-element.9, bf16[1024,512]{1,0:T(8,128)(2,1)S(1)} %get-tuple-element.6, bf16[512,512]{1,0:T(8,128)(2,1)S(1)} %get-tuple-element.10, bf16[512,512]{1,0:T(8,128)(2,1)S(1)} %get-tuple-element.7, ...), kind=kOutput, calls=%fused_computation.22 | convolution fusion | flops 2178416640 | bytes 9437185 | tf_op jit(solution)/shard_map/rf,rg->fg/dot_general | solution.py:64
  (5 shorter events, 0.1 us)
Async XLA Ops:
  1.7 103.4 %slice-start = ((s8[7340032]{0:T(1024)(128)(4,1)}), s8[4194304]{0:T(1024)(128)(4,1)S(1)}, s32[]{:S(2)}) async-start(s8[7340032]{0:T(1024)(128)(4,1)} %bitcast.48), calls=%async_computation.2 | async-start | bytes 8388608
  6.0 99.1 %slice-start.1 = ((s8[7340032]{0:T(1024)(128)(4,1)}), s8[3145728]{0:T(1024)(128)(4,1)S(1)}, s32[]{:S(2)}) async-start(s8[7340032]{0:T(1024)(128)(4,1)} %bitcast.48), calls=%async_computation.3 | async-start | bytes 6291456
  102.5 6.6 %slice-start.2 = ((s8[7340032]{0:T(1024)(128)(4,1)}), s8[4194304]{0:T(1024)(128)(4,1)S(1)}, s32[]{:S(2)}) async-start(s8[7340032]{0:T(1024)(128)(4,1)} %bitcast.50), calls=%async_computation.4 | async-start | bytes 8388608
  102.5 6.6 %slice-start.3 = ((s8[7340032]{0:T(1024)(128)(4,1)}), s8[3145728]{0:T(1024)(128)(4,1)S(1)}, s32[]{:S(2)}) async-start(s8[7340032]{0:T(1024)(128)(4,1)} %bitcast.50), calls=%async_computation.5 | async-start | bytes 6291456
  102.5 14.0 %collective-permute-start = (bf16[512,7168]{1,0:T(8,128)(2,1)S(1)}, bf16[512,7168]{1,0:T(8,128)(2,1)}, u32[]{:S(2)}, u32[]{:S(2)}) collective-permute-start(bf16[512,7168]{1,0:T(8,128)(2,1)S(1)} %bitcast.46), channel_id=1, source_target_pairs={{0,1},{1,0},{2,3},{3,2},{4,5},{5,4},{6,7},{7,6},{8,9},{9,8},{10,11... | collective-permute-start | bytes 22020104 | tf_op jit(solution)/shard_map/ppermute | solution.py:42
  132.5 54.0 %all-to-all-start.1 = ((bf16[4,1024,512]{2,1,0:T(8,128)(2,1)}), bf16[4,1024,512]{2,1,0:T(8,128)(2,1)}, u32[]{:S(2)}, u32[]{:S(2)}) async-start(bf16[4,1024,512]{2,1,0:T(8,128)(2,1)} %broadcast_in_dim.7), calls=%async_computation.1 | async-start | bytes 8388608 | tf_op jit(solution)/shard_map/all_to_all | solution.py:54

commit v6 on v3

--- a/solution.py
+++ b/solution.py
@@ -1,6 +1,7 @@
 import jax
 import jax.numpy as jnp
 from jax import lax
+from jax.experimental.layout import Layout, with_layout_constraint
 from jax.sharding import Mesh, NamedSharding, PartitionSpec as P
 
 N_ROUTED = 256
@@ -50,6 +51,7 @@
         gate_pre = jnp.dot(rows, w_gate[0], preferred_element_type=jnp.float32)
         up_pre = jnp.dot(rows, w_up[0], preferred_element_type=jnp.float32)
         keys = (jax.nn.silu(gate_pre) * up_pre).astype(jnp.bfloat16)
+        keys = with_layout_constraint(keys, Layout(major_to_minor=(0, 1)))
         blocks[i][0] = keys
         blocks[i][2] = lax.ppermute(keys, "xh", swap_half)
         blocks[1 - i][1] = lax.ppermute(keys, "core", swap_core)

time: 181 us -> 171 us (0.945)
  matrix products: 42.9 us -> 30.5 us
  waiting for transfers between devices: 30.4 us -> 33.8 us
    dot_general x2, matrix products: 16.5 us -> 11.2 us  [body(): up_pre = jnp.dot(rows, w_up[0], preferred_element_type=jnp.float32)]
    dot_general x2, matrix products: 14.8 us -> 10.3 us  [body(): gate_pre = jnp.dot(rows, w_gate[0], preferred_element_type=jnp.float32)]
    dot_general x2, matrix products: 7.23 us -> 4.57 us  [body(): jnp.einsum('rf,rg->fg', blocks[i][0], absolute(blocks[i]), preferred_elem...]
    ppermute x1, waiting for transfers between devices: 0.01 us -> 2.18 us  [body(): lax.ppermute(slot_block, 'core', [(c, (c + 1) % core_count) for c in rang...]
  transfers between devices with their start and end apart: 7 -> 7, of which waited for: 3 -> 4; matrix products, arithmetic and copies ran while one was open for 18% -> 13% of each run, Pallas kernels for 0% -> 0%
where the time goes in v6:
time: 171 us
  blocking collectives  96.5 us (56%)
  waiting for transfers between devices  33.8 us (20%)
  matrix products  30.5 us (18%)
  starting transfers between devices  8.41 us (5%)
    all_to_all x1, blocking collectives, body(): lax.all_to_all(slot_rows, ('expert', 'xh'), split_axis=0, concat_axis=0,...  96.5 us
    ppermute x2, waiting for transfers between devices, body(): blocks[i][2] = lax.ppermute(keys, 'xh', swap_half)  19.8 us
    ppermute x2, waiting for transfers between devices, body(): blocks[1 - i][3] = lax.ppermute(keys, ('xh', 'core'), swap_both)  11.8 us
    dot_general x2, matrix products, body(): up_pre = jnp.dot(rows, w_up[0], preferred_element_type=jnp.float32)  11.2 us
    dot_general x2, matrix products, body(): gate_pre = jnp.dot(rows, w_gate[0], preferred_element_type=jnp.float32)  10.3 us
    dot_general x2, matrix products, body(): jnp.einsum('rf,rg->fg', blocks[i][0], absolute(blocks[i]), preferred_elem...  4.57 us
    dot_general x1, matrix products, body(): jnp.dot(onehot.astype(tokens.dtype), tokens, preferred_element_type=jnp.f...  4.26 us
  transfers between devices with their start and end apart: 7, of which 4 were waited for; matrix products, arithmetic and copies ran while one was open for 13% of the time, Pallas kernels for 0%

profile of v6, /device:TPU:1, one launch (start us, length us, event | category | flops | bytes accessed | tf_op | source)
XLA Modules:
  0.0 171.2 jit_solution(14682526246038989317)
XLA Ops:
  0.0 0.7 fusion.30
  1.4 0.2 convolution_convert_fusion.1
  1.6 0.1 fusion.31
  1.7 0.0 slice-start
  1.7 4.3 %fusion = bf16[64,8,7168]{2,1,0:T(8,128)(2,1)S(1)} fusion(pred[512,256]{1,0:T(8,128)(4,1)S(1)} %bitcast.37, bf16[256,7168]{1,0:T(8,128)(2,1)} %param.5), kind=kOutput, calls=%fused_computation.1 | convolution fusion | flops 1882718208 | bytes 11141120 | tf_op jit(solution)/shard_map/dot_general | solution.py:35
  6.0 0.0 slice-start.1
  6.0 96.5 %all_to_all.5 = bf16[64,8,7168]{2,1,0:T(8,128)(2,1)S(1)} all-to-all(bf16[64,8,7168]{2,1,0:T(8,128)(2,1)S(1)} %fusion), channel_id=1, replica_groups=mesh['expert'=32,'xh'=2,'core'=2] {'expert','xh'}, dimensions={0} | all-to-all | bytes 14680064 | tf_op jit(solution)/shard_map/all_to_all | solution.py:39
  102.5 0.0 slice-start.2
  102.5 0.0 slice-start.3
  102.5 2.6 %collective-permute-start = (bf16[512,7168]{1,0:T(8,128)(2,1)S(1)}, bf16[512,7168]{1,0:T(8,128)(2,1)}, u32[]{:S(2)}, u32[]{:S(2)}) collective-permute-start(bf16[512,7168]{1,0:T(8,128)(2,1)S(1)} %bitcast.36), channel_id=1, source_target_pairs={{0,1},{1,0},{2,3},{3,2},{4,5},{5,4},{6,7},{7,6},{8,9},{9,8},{10,11... | collective-permute-start | bytes 22020104 | tf_op jit(solution)/shard_map/ppermute | solution.py:43
  105.1 0.0 slice-done
  105.1 0.0 slice-done.1
  105.1 3.9 %fusion.7 = f32[512,512]{1,0:T(8,128)S(1)} fusion(bf16[1,7168,512]{2,1,0:T(8,128)(2,1)S(1)} %bitcast.39, bf16[64,8,7168]{2,1,0:T(8,128)(2,1)S(1)} %all_to_all.5), kind=kOutput, calls=%fused_computation.8 | convolution fusion | flops 3758096384 | bytes 15728640 | tf_op jit(solution)/shard_map/dot_general | solution.py:51
  109.0 0.0 slice-done.2
  109.0 0.0 slice-done.3
  109.1 4.0 %fusion.27 = bf16[512,512]{1,0:T(8,128)(2,1)S(1)} fusion(bf16[1,7168,512]{2,1,0:T(8,128)(2,1)S(1)} %bitcast.41, f32[512,512]{1,0:T(8,128)S(1)} %fusion.7, bf16[64,8,7168]{2,1,0:T(8,128)(2,1)S(1)} %all_to_all.5), kind=kOutput, calls=%fused_computation.27 | convolution fusion | flops 3759669248 | bytes 16252928 | tf_op jit(solution)/shard_map/dot_general | solution.py:52
  113.1 0.7 collective-permute-start.4
  113.8 0.5 collective-permute-start.6
  114.3 2.2 %collective-permute-done = bf16[512,7168]{1,0:T(8,128)(2,1)} collective-permute-done((bf16[512,7168]{1,0:T(8,128)(2,1)S(1)}, bf16[512,7168]{1,0:T(8,128)(2,1)}, u32[]{:S(2)}, u32[]{:S(2)}) %collective-permute-start) | collective-permute-done | bytes 7340064 | tf_op jit(solution)/shard_map/ppermute | solution.py:43
  116.5 6.4 %fusion.5 = f32[512,512]{1,0:T(8,128)S(1)} fusion(bf16[512,7168]{1,0:T(8,128)(2,1)} %collective-permute-done, bf16[1,7168,512]{2,1,0:T(8,128)(2,1)S(1)} %bitcast.39), kind=kOutput, calls=%fused_computation.6 | convolution fusion | flops 3758096384 | bytes 15728640 | tf_op jit(solution)/shard_map/dot_general | solution.py:51
  122.9 7.2 %multiply_convert_fusion = bf16[512,512]{1,0:T(8,128)(2,1)S(1)} fusion(f32[512,512]{1,0:T(8,128)S(1)} %fusion.5, bf16[512,7168]{1,0:T(8,128)(2,1)} %collective-permute-done, bf16[1,7168,512]{2,1,0:T(8,128)(2,1)S(1)} %bitcast.41), kind=kOutput, calls=%fused_computation.29 | convolution fusion | flops 3759669248 | bytes 16252928 | tf_op jit(solution)/shard_map/dot_general | solution.py:52
  130.1 0.8 collective-permute-start.5
  130.9 2.2 %collective-permute-start.2 = (bf16[512,512]{1,0:T(8,128)(2,1)S(1)}, bf16[512,512]{1,0:T(8,128)(2,1)S(1)}, u32[]{:S(2)}, u32[]{:S(2)}) collective-permute-start(bf16[512,512]{1,0:T(8,128)(2,1)S(1)} %fusion.27), channel_id=1, source_target_pairs={{0,2},{2,0},{1,3},{3,1},{4,6},{6,4},{5,7},{7,5},{8,10},{10,8},{9,1... | collective-permute-start | bytes 1572872 | tf_op jit(solution)/shard_map/ppermute | solution.py:56
  133.1 1.6 collective-permute-start.1
  134.7 0.0 collective-permute-done.4
  134.7 0.0 collective-permute-start.3
  134.7 0.0 collective-permute-done.6
  134.7 10.1 %collective-permute-done.5 = bf16[512,512]{1,0:T(8,128)(2,1)S(1)} collective-permute-done((bf16[512,512]{1,0:T(8,128)(2,1)S(1)}, bf16[512,512]{1,0:T(8,128)(2,1)S(1)}, u32[]{:S(2)}, u32[]{:S(2)}) %collective-permute-start.5) | collective-permute-done | bytes 524320 | tf_op jit(solution)/shard_map/ppermute | solution.py:56
  144.7 0.2 broadcast_select_fusion.11
  144.9 1.3 fusion.16
  146.2 9.8 %collective-permute-done.2 = bf16[512,512]{1,0:T(8,128)(2,1)S(1)} collective-permute-done((bf16[512,512]{1,0:T(8,128)(2,1)S(1)}, bf16[512,512]{1,0:T(8,128)(2,1)S(1)}, u32[]{:S(2)}, u32[]{:S(2)}) %collective-permute-start.2) | collective-permute-done | bytes 524320 | tf_op jit(solution)/shard_map/ppermute | solution.py:56
  156.0 11.8 %collective-permute-done.1 = bf16[512,512]{1,0:T(8,128)(2,1)S(1)} collective-permute-done((bf16[512,512]{1,0:T(8,128)(2,1)S(1)}, bf16[512,512]{1,0:T(8,128)(2,1)S(1)}, u32[]{:S(2)}, u32[]{:S(2)}) %collective-permute-start.1) | collective-permute-done | bytes 524320 | tf_op jit(solution)/shard_map/ppermute | solution.py:58
  167.8 0.0 collective-permute-done.3
  167.8 0.2 broadcast_select_fusion.15
  167.9 3.3 %multiply_bitcast_fusion = f32[1,512,2048]{2,1,0:T(8,128)} fusion(f32[512,2048]{1,0:T(8,128)S(1)} %fusion.16, bf16[512,512]{1,0:T(8,128)(2,1)S(1)} %fusion.27, bf16[512,512]{1,0:T(8,128)(2,1)S(1)} %get-tuple-element.8, bf16[512,512]{1,0:T(8,128)(2,1)S(1)} %get-tuple-element.7, bf16[512,512]{1,0:T(8,128)(2,1)S(1)} %get-tuple-element.6, ...), kind=kOutput, calls=%fused_computation.10 | convolution fusion | flops 1084227584 | bytes 11010048 | tf_op jit(solution)/shard_map/rf,rg->fg/dot_general | solution.py:69
  (5 shorter events, 0.1 us)
Async XLA Ops:
  1.7 103.4 %slice-start = ((s8[7340032]{0:T(1024)(128)(4,1)}), s8[4194304]{0:T(1024)(128)(4,1)S(1)}, s32[]{:S(2)}) async-start(s8[7340032]{0:T(1024)(128)(4,1)} %bitcast.38), calls=%async_computation.1 | async-start | bytes 8388608
  6.0 99.1 %slice-start.1 = ((s8[7340032]{0:T(1024)(128)(4,1)}), s8[3145728]{0:T(1024)(128)(4,1)S(1)}, s32[]{:S(2)}) async-start(s8[7340032]{0:T(1024)(128)(4,1)} %bitcast.38), calls=%async_computation.2 | async-start | bytes 6291456
  102.5 6.5 %slice-start.2 = ((s8[7340032]{0:T(1024)(128)(4,1)}), s8[4194304]{0:T(1024)(128)(4,1)S(1)}, s32[]{:S(2)}) async-start(s8[7340032]{0:T(1024)(128)(4,1)} %bitcast.40), calls=%async_computation.3 | async-start | bytes 8388608
  102.5 6.5 %slice-start.3 = ((s8[7340032]{0:T(1024)(128)(4,1)}), s8[3145728]{0:T(1024)(128)(4,1)S(1)}, s32[]{:S(2)}) async-start(s8[7340032]{0:T(1024)(128)(4,1)} %bitcast.40), calls=%async_computation.4 | async-start | bytes 6291456
  102.5 14.0 %collective-permute-start = (bf16[512,7168]{1,0:T(8,128)(2,1)S(1)}, bf16[512,7168]{1,0:T(8,128)(2,1)}, u32[]{:S(2)}, u32[]{:S(2)}) collective-permute-start(bf16[512,7168]{1,0:T(8,128)(2,1)S(1)} %bitcast.36), channel_id=1, source_target_pairs={{0,1},{1,0},{2,3},{3,2},{4,5},{5,4},{6,7},{7,6},{8,9},{9,8},{10,11... | collective-permute-start | bytes 22020104 | tf_op jit(solution)/shard_map/ppermute | solution.py:43
  113.1 21.6 %collective-permute-start.4 = (bf16[512,512]{1,0:T(8,128)(2,1)S(1)}, bf16[512,512]{1,0:T(8,128)(2,1)S(1)}, u32[]{:S(2)}, u32[]{:S(2)}) collective-permute-start(bf16[512,512]{1,0:T(8,128)(2,1)S(1)} %fusion.27), channel_id=1, source_target_pairs={{0,3},{1,2},{2,1},{3,0},{4,7},{5,6},{6,5},{7,4},{8,11},{9,10},{10,... | collective-permute-start | bytes 1572872 | tf_op jit(solution)/shard_map/ppermute | solution.py:58
  113.8 20.9 %collective-permute-start.6 = (bf16[512,512]{1,0:T(8,128)(2,1)S(1)}, bf16[512,512]{1,0:T(8,128)(2,1)S(1)}, u32[]{:S(2)}, u32[]{:S(2)}) collective-permute-start(bf16[512,512]{1,0:T(8,128)(2,1)S(1)} %fusion.27), channel_id=1, source_target_pairs={{0,1},{1,0},{2,3},{3,2},{4,5},{5,4},{6,7},{7,6},{8,9},{9,8},{10,11... | collective-permute-start | bytes 1572872 | tf_op jit(solution)/shard_map/ppermute | solution.py:57
  130.1 14.7 %collective-permute-start.5 = (bf16[512,512]{1,0:T(8,128)(2,1)S(1)}, bf16[512,512]{1,0:T(8,128)(2,1)S(1)}, u32[]{:S(2)}, u32[]{:S(2)}) collective-permute-start(bf16[512,512]{1,0:T(8,128)(2,1)S(1)} %multiply_convert_fusion), channel_id=1, source_target_pairs={{0,2},{2,0},{1,3},{3,1},{4,6},{6,4},{5,7},{7,5},{8,10},{10,8},{9,1... | collective-permute-start | bytes 1572872 | tf_op jit(solution)/shard_map/ppermute | solution.py:56
  130.9 25.1 %collective-permute-start.2 = (bf16[512,512]{1,0:T(8,128)(2,1)S(1)}, bf16[512,512]{1,0:T(8,128)(2,1)S(1)}, u32[]{:S(2)}, u32[]{:S(2)}) collective-permute-start(bf16[512,512]{1,0:T(8,128)(2,1)S(1)} %fusion.27), channel_id=1, source_target_pairs={{0,2},{2,0},{1,3},{3,1},{4,6},{6,4},{5,7},{7,5},{8,10},{10,8},{9,1... | collective-permute-start | bytes 1572872 | tf_op jit(solution)/shard_map/ppermute | solution.py:56
  133.1 34.7 %collective-permute-start.1 = (bf16[512,512]{1,0:T(8,128)(2,1)S(1)}, bf16[512,512]{1,0:T(8,128)(2,1)S(1)}, u32[]{:S(2)}, u32[]{:S(2)}) collective-permute-start(bf16[512,512]{1,0:T(8,128)(2,1)S(1)} %multiply_convert_fusion), channel_id=1, source_target_pairs={{0,3},{1,2},{2,1},{3,0},{4,7},{5,6},{6,5},{7,4},{8,11},{9,10},{10,... | collective-permute-start | bytes 1572872 | tf_op jit(solution)/shard_map/ppermute | solution.py:58
  134.7 33.1 %collective-permute-start.3 = (bf16[512,512]{1,0:T(8,128)(2,1)S(1)}, bf16[512,512]{1,0:T(8,128)(2,1)S(1)}, u32[]{:S(2)}, u32[]{:S(2)}) collective-permute-start(bf16[512,512]{1,0:T(8,128)(2,1)S(1)} %multiply_convert_fusion), channel_id=1, source_target_pairs={{0,1},{1,0},{2,3},{3,2},{4,5},{5,4},{6,7},{7,6},{8,9},{9,8},{10,11... | collective-permute-start | bytes 1572872 | tf_op jit(solution)/shard_map/ppermute | solution.py:57

commit v7 on v6

--- a/solution.py
+++ b/solution.py
@@ -45,17 +45,18 @@
     swap_half = [(h, (h + 1) % half_count) for h in range(half_count)]
     swap_core = [(c, (c + 1) % core_count) for c in range(core_count)]
     replica_count = half_count * core_count
-    swap_both = [(r, r ^ (replica_count - 1)) for r in range(replica_count)]
-    blocks = [[None] * 4, [None] * 4]
-    for i, rows in enumerate((slot_block, partner)):
+    own_keys, far_keys = [], []
+    for rows in (slot_block, partner):
         gate_pre = jnp.dot(rows, w_gate[0], preferred_element_type=jnp.float32)
         up_pre = jnp.dot(rows, w_up[0], preferred_element_type=jnp.float32)
         keys = (jax.nn.silu(gate_pre) * up_pre).astype(jnp.bfloat16)
         keys = with_layout_constraint(keys, Layout(major_to_minor=(0, 1)))
-        blocks[i][0] = keys
-        blocks[i][2] = lax.ppermute(keys, "xh", swap_half)
-        blocks[1 - i][1] = lax.ppermute(keys, "core", swap_core)
-        blocks[1 - i][3] = lax.ppermute(keys, ("xh", "core"), swap_both)
+        own_keys.append(keys)
+        far_keys.append(lax.ppermute(keys, "xh", swap_half))
+    relayed = lax.ppermute(jnp.stack(own_keys + far_keys), "core", swap_core)
+    blocks = [
+        [own_keys[i], relayed[1 - i], far_keys[i], relayed[3 - i]] for i in range(2)
+    ]
     on_second_core = lax.axis_index("core") == 1
     on_second_half = lax.axis_index("xh") == 1
 

time: 171 us -> 152 us (0.89)
  waiting for transfers between devices: 33.8 us -> 20.5 us
  matrix products: 30.5 us -> 24.9 us
  starting transfers between devices: 8.41 us -> 5.46 us
  other arithmetic: 1.18 us -> 3.97 us
    ppermute x6 -> x3, waiting for transfers between devices: 31.6 us -> 18.2 us  [the longest x2 14.2 us: body(): far_keys.append(lax.ppermute(keys, 'xh', swap_half))]
    dot_general x2, matrix products: 11.2 us -> 8.05 us  [body(): up_pre = jnp.dot(rows, w_up[0], preferred_element_type=jnp.float32)]
    ppermute x6 -> x3, starting transfers between devices: 5.85 us -> 2.85 us  [the longest x2 1.78 us: body(): far_keys.append(lax.ppermute(keys, 'xh', swap_half))]
    dot_general x2, matrix products: 10.3 us -> 7.88 us  [body(): gate_pre = jnp.dot(rows, w_gate[0], preferred_element_type=jnp.float32)]
  transfers between devices with their start and end apart: 7 -> 4, of which waited for: 4 -> 4; matrix products, arithmetic and copies ran while one was open for 13% -> 10% of each run, Pallas kernels for 0% -> 0%
where the time goes in v7:
time: 152 us
  blocking collectives  96.5 us (63%)
  matrix products  24.9 us (16%)
  waiting for transfers between devices  20.5 us (13%)
  starting transfers between devices  5.46 us (4%)
  other arithmetic  3.97 us (3%)
    all_to_all x1, blocking collectives, body(): lax.all_to_all(slot_rows, ('expert', 'xh'), split_axis=0, concat_axis=0,...  96.5 us
    ppermute x2, waiting for transfers between devices, body(): far_keys.append(lax.ppermute(keys, 'xh', swap_half))  14.2 us
    dot_general x2, matrix products, body(): up_pre = jnp.dot(rows, w_up[0], preferred_element_type=jnp.float32)  8.05 us
    dot_general x2, matrix products, body(): gate_pre = jnp.dot(rows, w_gate[0], preferred_element_type=jnp.float32)  7.88 us
    dot_general x2, matrix products, body(): jnp.einsum('rf,rg->fg', blocks[i][0], absolute(blocks[i]), preferred_elem...  4.57 us
    dot_general x1, matrix products, body(): jnp.dot(onehot.astype(tokens.dtype), tokens, preferred_element_type=jnp.f...  4.26 us
    ppermute x1, waiting for transfers between devices, body(): relayed = lax.ppermute(jnp.stack(own_keys + far_keys), 'core', swap_core)  3.99 us
  transfers between devices with their start and end apart: 4, of which 4 were waited for; matrix products, arithmetic and copies ran while one was open for 10% of the time, Pallas kernels for 0%

profile of v7, /device:TPU:1, one launch (start us, length us, event | category | flops | bytes accessed | tf_op | source)
XLA Modules:
  0.0 152.2 jit_solution(12562399548443399124)
XLA Ops:
  0.7 0.7 fusion.30
  1.4 0.2 convolution_convert_fusion.1
  1.6 0.1 fusion.31
  1.7 0.0 slice-start
  1.7 4.3 %fusion = bf16[64,8,7168]{2,1,0:T(8,128)(2,1)S(1)} fusion(pred[512,256]{1,0:T(8,128)(4,1)S(1)} %bitcast.101, bf16[256,7168]{1,0:T(8,128)(2,1)} %param.5), kind=kOutput, calls=%fused_computation.1 | convolution fusion | flops 1882718208 | bytes 11141120 | tf_op jit(solution)/shard_map/dot_general | solution.py:35
  6.0 0.0 slice-start.1
  6.0 96.5 %all_to_all.5 = bf16[64,8,7168]{2,1,0:T(8,128)(2,1)S(1)} all-to-all(bf16[64,8,7168]{2,1,0:T(8,128)(2,1)S(1)} %fusion), channel_id=1, replica_groups=mesh['expert'=32,'xh'=2,'core'=2] {'expert','xh'}, dimensions={0} | all-to-all | bytes 14680064 | tf_op jit(solution)/shard_map/all_to_all | solution.py:39
  102.5 0.0 slice-start.2
  102.5 0.0 slice-start.3
  102.5 2.6 %collective-permute-start = (bf16[512,7168]{1,0:T(8,128)(2,1)S(1)}, bf16[512,7168]{1,0:T(8,128)(2,1)S(1)}, u32[]{:S(2)}, u32[]{:S(2)}) collective-permute-start(bf16[512,7168]{1,0:T(8,128)(2,1)S(1)} %bitcast.96), channel_id=1, source_target_pairs={{0,1},{1,0},{2,3},{3,2},{4,5},{5,4},{6,7},{7,6},{8,9},{9,8},{10,11... | collective-permute-start | bytes 22020104 | tf_op jit(solution)/shard_map/ppermute | solution.py:43
  105.1 0.0 slice-done
  105.1 0.0 slice-done.1
  105.1 3.9 %fusion.7 = f32[512,512]{1,0:T(8,128)S(1)} fusion(bf16[1,7168,512]{2,1,0:T(8,128)(2,1)S(1)} %bitcast.103, bf16[64,8,7168]{2,1,0:T(8,128)(2,1)S(1)} %all_to_all.5), kind=kOutput, calls=%fused_computation.8 | convolution fusion | flops 3758096384 | bytes 15728640 | tf_op jit(solution)/shard_map/dot_general | solution.py:50
  109.0 0.0 slice-done.2
  109.0 0.0 slice-done.3
  109.1 4.0 %fusion.27 = bf16[512,512]{1,0:T(8,128)(2,1)S(1)} fusion(bf16[1,7168,512]{2,1,0:T(8,128)(2,1)S(1)} %bitcast.105, f32[512,512]{1,0:T(8,128)S(1)} %fusion.7, bf16[64,8,7168]{2,1,0:T(8,128)(2,1)S(1)} %all_to_all.5), kind=kOutput, calls=%fused_computation.28 | convolution fusion | flops 3759669248 | bytes 16252928 | tf_op jit(solution)/shard_map/dot_general | solution.py:51
  113.1 1.0 collective-permute-start.1
  114.1 2.3 %collective-permute-done = bf16[512,7168]{1,0:T(8,128)(2,1)S(1)} collective-permute-done((bf16[512,7168]{1,0:T(8,128)(2,1)S(1)}, bf16[512,7168]{1,0:T(8,128)(2,1)S(1)}, u32[]{:S(2)}, u32[]{:S(2)}) %collective-permute-start) | collective-permute-done | bytes 7340064 | tf_op jit(solution)/shard_map/ppermute | solution.py:43
  116.4 3.9 %fusion.5 = f32[512,512]{1,0:T(8,128)S(1)} fusion(bf16[512,7168]{1,0:T(8,128)(2,1)S(1)} %collective-permute-done, bf16[1,7168,512]{2,1,0:T(8,128)(2,1)S(1)} %bitcast.103), kind=kOutput, calls=%fused_computation.6 | convolution fusion | flops 3758096384 | bytes 15728640 | tf_op jit(solution)/shard_map/dot_general | solution.py:50
  120.3 4.0 %multiply_convert_fusion = bf16[512,512]{1,0:T(8,128)(2,1)S(1)} fusion(f32[512,512]{1,0:T(8,128)S(1)} %fusion.5, bf16[512,7168]{1,0:T(8,128)(2,1)S(1)} %collective-permute-done, bf16[1,7168,512]{2,1,0:T(8,128)(2,1)S(1)} %bitcast.105), kind=kOutput, calls=%fused_computation.30 | convolution fusion | flops 3759669248 | bytes 16252928 | tf_op jit(solution)/shard_map/dot_general | solution.py:51
  124.3 0.0 copy-start
  124.4 0.8 collective-permute-start.2
  125.2 3.2 %collective-permute-done.1 = bf16[512,512]{1,0:T(8,128)(2,1)S(1)} collective-permute-done((bf16[512,512]{1,0:T(8,128)(2,1)S(1)}, bf16[512,512]{1,0:T(8,128)(2,1)S(1)}, u32[]{:S(2)}, u32[]{:S(2)}) %collective-permute-start.1) | collective-permute-done | bytes 524320 | tf_op jit(solution)/shard_map/ppermute | solution.py:55
  128.3 11.0 %collective-permute-done.2 = bf16[512,512]{1,0:T(8,128)(2,1)S(1)} collective-permute-done((bf16[512,512]{1,0:T(8,128)(2,1)S(1)}, bf16[512,512]{1,0:T(8,128)(2,1)S(1)}, u32[]{:S(2)}, u32[]{:S(2)}) %collective-permute-start.2) | collective-permute-done | bytes 524320 | tf_op jit(solution)/shard_map/ppermute | solution.py:55
  139.4 0.0 copy-start.2
  139.4 0.0 copy-done
  139.4 1.6 %pad_maximum_fusion = bf16[4,512,512]{2,1,0:T(8,128)(2,1)} fusion(bf16[1,512,512]{2,1,0:T(8,128)(2,1)S(1)} %bitcast.100, bf16[1,512,512]{2,1,0:T(8,128)(2,1)S(1)} %bitcast.98, bf16[1,512,512]{2,1,0:T(8,128)(2,1)S(1)} %bitcast.99, bf16[1,512,512]{2,1,0:T(8,128)(2,1)S(1)} %bitcast.97), kind=kLoop, calls=%fused_computation.11 | loop fusion | flops 3145728 | bytes 4194304 | tf_op jit(solution)/shard_map/stack | solution.py:56
  140.9 0.0 copy-done.2
  140.9 1.1 collective-permute-start.3
  142.0 0.0 copy-start.1
  142.0 4.0 %collective-permute-done.3 = bf16[4,512,512]{2,1,0:T(8,128)(2,1)S(1)} collective-permute-done((bf16[4,512,512]{2,1,0:T(8,128)(2,1)}, bf16[4,512,512]{2,1,0:T(8,128)(2,1)S(1)}, u32[]{:S(2)}, u32[]{:S(2)}) %collective-permute-start.3) | collective-permute-done | bytes 2097184 | tf_op jit(solution)/shard_map/ppermute | solution.py:56
  146.0 1.4 broadcast_select_fusion.11
  147.4 0.0 copy-done.1
  147.4 1.3 fusion.16
  148.7 0.2 broadcast_select_fusion.15
  148.9 3.3 %multiply_bitcast_fusion = f32[1,512,2048]{2,1,0:T(8,128)} fusion(f32[512,2048]{1,0:T(8,128)S(1)} %fusion.16, bf16[512,512]{1,0:T(8,128)(2,1)S(1)} %fusion.27, bf16[512,512]{1,0:T(8,128)(2,1)S(1)} %get-tuple-element.8, bf16[512,512]{1,0:T(8,128)(2,1)S(1)} %get-tuple-element.7, bf16[512,512]{1,0:T(8,128)(2,1)S(1)} %get-tuple-element.6, ...), kind=kOutput, calls=%fused_computation.10 | convolution fusion | flops 1084227584 | bytes 11010048 | tf_op jit(solution)/shard_map/rf,rg->fg/dot_general | solution.py:70
  (5 shorter events, 0.1 us)
Async XLA Ops:
  1.7 103.4 %slice-start = ((s8[7340032]{0:T(1024)(128)(4,1)}), s8[4194304]{0:T(1024)(128)(4,1)S(1)}, s32[]{:S(2)}) async-start(s8[7340032]{0:T(1024)(128)(4,1)} %bitcast.102), calls=%async_computation.1 | async-start | bytes 8388608
  6.0 99.1 %slice-start.1 = ((s8[7340032]{0:T(1024)(128)(4,1)}), s8[3145728]{0:T(1024)(128)(4,1)S(1)}, s32[]{:S(2)}) async-start(s8[7340032]{0:T(1024)(128)(4,1)} %bitcast.102), calls=%async_computation.2 | async-start | bytes 6291456
  102.5 6.6 %slice-start.2 = ((s8[7340032]{0:T(1024)(128)(4,1)}), s8[4194304]{0:T(1024)(128)(4,1)S(1)}, s32[]{:S(2)}) async-start(s8[7340032]{0:T(1024)(128)(4,1)} %bitcast.104), calls=%async_computation.3 | async-start | bytes 8388608
  102.5 6.6 %slice-start.3 = ((s8[7340032]{0:T(1024)(128)(4,1)}), s8[3145728]{0:T(1024)(128)(4,1)S(1)}, s32[]{:S(2)}) async-start(s8[7340032]{0:T(1024)(128)(4,1)} %bitcast.104), calls=%async_computation.4 | async-start | bytes 6291456
  102.5 13.9 %collective-permute-start = (bf16[512,7168]{1,0:T(8,128)(2,1)S(1)}, bf16[512,7168]{1,0:T(8,128)(2,1)S(1)}, u32[]{:S(2)}, u32[]{:S(2)}) collective-permute-start(bf16[512,7168]{1,0:T(8,128)(2,1)S(1)} %bitcast.96), channel_id=1, source_target_pairs={{0,1},{1,0},{2,3},{3,2},{4,5},{5,4},{6,7},{7,6},{8,9},{9,8},{10,11... | collective-permute-start | bytes 22020104 | tf_op jit(solution)/shard_map/ppermute | solution.py:43
  113.1 15.2 %collective-permute-start.1 = (bf16[512,512]{1,0:T(8,128)(2,1)S(1)}, bf16[512,512]{1,0:T(8,128)(2,1)S(1)}, u32[]{:S(2)}, u32[]{:S(2)}) collective-permute-start(bf16[512,512]{1,0:T(8,128)(2,1)S(1)} %fusion.27), channel_id=1, source_target_pairs={{0,2},{2,0},{1,3},{3,1},{4,6},{6,4},{5,7},{7,5},{8,10},{10,8},{9,1... | collective-permute-start | bytes 1572872 | tf_op jit(solution)/shard_map/ppermute | solution.py:55
  124.3 15.0 %copy-start = (bf16[512,512]{1,0:T(8,128)(2,1)}, bf16[512,512]{1,0:T(8,128)(2,1)S(1)}, u32[]{:S(2)}) copy-start(bf16[512,512]{1,0:T(8,128)(2,1)S(1)} %multiply_convert_fusion) | copy-start | bytes 1572868
  124.4 15.0 %collective-permute-start.2 = (bf16[512,512]{1,0:T(8,128)(2,1)S(1)}, bf16[512,512]{1,0:T(8,128)(2,1)S(1)}, u32[]{:S(2)}, u32[]{:S(2)}) collective-permute-start(bf16[512,512]{1,0:T(8,128)(2,1)S(1)} %multiply_convert_fusion), channel_id=1, source_target_pairs={{0,2},{2,0},{1,3},{3,1},{4,6},{6,4},{5,7},{7,5},{8,10},{10,8},{9,1... | collective-permute-start | bytes 1572872 | tf_op jit(solution)/shard_map/ppermute | solution.py:55
  139.4 1.6 %copy-start.2 = (bf16[512,512]{1,0:T(8,128)(2,1)}, bf16[512,512]{1,0:T(8,128)(2,1)S(1)}, u32[]{:S(2)}) copy-start(bf16[512,512]{1,0:T(8,128)(2,1)S(1)} %collective-permute-done.2) | copy-start | bytes 1572868
  140.9 5.1 %collective-permute-start.3 = (bf16[4,512,512]{2,1,0:T(8,128)(2,1)}, bf16[4,512,512]{2,1,0:T(8,128)(2,1)S(1)}, u32[]{:S(2)}, u32[]{:S(2)}) collective-permute-start(bf16[4,512,512]{2,1,0:T(8,128)(2,1)} %pad_maximum_fusion), channel_id=1, source_target_pairs={{0,1},{1,0},{2,3},{3,2},{4,5},{5,4},{6,7},{7,6},{8,9},{9,8},{10,11... | collective-permute-start | bytes 6291464 | tf_op jit(solution)/shard_map/ppermute | solution.py:56
  142.0 5.4 %copy-start.1 = (bf16[512,512]{1,0:T(8,128)(2,1)S(1)}, bf16[512,512]{1,0:T(8,128)(2,1)}, u32[]{:S(2)}) copy-start(bf16[512,512]{1,0:T(8,128)(2,1)} %copy-done) | copy-start | bytes 1572868

commit v8 on v7

--- a/solution.py
+++ b/solution.py
@@ -45,6 +45,20 @@
     swap_half = [(h, (h + 1) % half_count) for h in range(half_count)]
     swap_core = [(c, (c + 1) % core_count) for c in range(core_count)]
     replica_count = half_count * core_count
+    ring = half_count * 2
+    expert_inner = expert_count // 2
+
+    def step(shift):
+        pairs = []
+        for expert in range(expert_count):
+            for half in range(half_count):
+                x = half * 2 + expert // expert_inner
+                moved = (x + shift) % ring
+                target = (moved % 2) * expert_inner + expert % expert_inner
+                pairs.append((expert * half_count + half, target * half_count + moved // 2))
+        return pairs
+
+    step_up, step_down = step(1), step(-1)
     own_keys, far_keys = [], []
     for rows in (slot_block, partner):
         gate_pre = jnp.dot(rows, w_gate[0], preferred_element_type=jnp.float32)
@@ -52,7 +66,13 @@
         keys = (jax.nn.silu(gate_pre) * up_pre).astype(jnp.bfloat16)
         keys = with_layout_constraint(keys, Layout(major_to_minor=(0, 1)))
         own_keys.append(keys)
-        far_keys.append(lax.ppermute(keys, "xh", swap_half))
+        rows_half = keys.shape[0] // 2
+        forward = keys[:rows_half]
+        backward = keys[rows_half:]
+        for _ in range(half_count):
+            forward = lax.ppermute(forward, ("expert", "xh"), step_up)
+            backward = lax.ppermute(backward, ("expert", "xh"), step_down)
+        far_keys.append(jnp.concatenate([forward, backward], axis=0))
     relayed = lax.ppermute(jnp.stack(own_keys + far_keys), "core", swap_core)
     blocks = [
         [own_keys[i], relayed[1 - i], far_keys[i], relayed[3 - i]] for i in range(2)

time: 152 us -> 165 us (1.086)
  starting transfers between devices: 5.46 us -> 13.8 us
  matrix products: 24.9 us -> 30.5 us
  waiting for transfers between devices: 20.5 us -> 17.5 us
    ppermute x2 -> x8, starting transfers between devices: 1.78 us -> 9.92 us  [the longest x4 9.35 us: body(): backward = lax.ppermute(backward, ('expert', 'xh'), step_down)]
    dot_general x2, matrix products: 8.05 us -> 11.2 us  [body(): up_pre = jnp.dot(rows, w_up[0], preferred_element_type=jnp.float32)]
    dot_general x2, matrix products: 7.88 us -> 10.3 us  [body(): gate_pre = jnp.dot(rows, w_gate[0], preferred_element_type=jnp.float32)]
    ppermute x2 -> x8, waiting for transfers between devices: 14.2 us -> 11.8 us  [the longest x4 11.8 us: body(): forward = lax.ppermute(forward, ('expert', 'xh'), step_up)]
  transfers between devices with their start and end apart: 4 -> 10, of which waited for: 4 -> 5; matrix products, arithmetic and copies ran while one was open for 10% -> 13% of each run, Pallas kernels for 0% -> 0%
where the time goes in v8:
time: 165 us; the launch traced here: 164 us
  blocking collectives  96.5 us (58%)
  matrix products  30.5 us (18%)
  waiting for transfers between devices  17.5 us (11%)
  starting transfers between devices  13.8 us (8%)
  other arithmetic  5.17 us (3%)
    all_to_all x1, blocking collectives, body(): lax.all_to_all(slot_rows, ('expert', 'xh'), split_axis=0, concat_axis=0,...  96.5 us
    ppermute x4, waiting for transfers between devices, body(): forward = lax.ppermute(forward, ('expert', 'xh'), step_up)  11.8 us
    dot_general x2, matrix products, body(): up_pre = jnp.dot(rows, w_up[0], preferred_element_type=jnp.float32)  11.2 us
    dot_general x2, matrix products, body(): gate_pre = jnp.dot(rows, w_gate[0], preferred_element_type=jnp.float32)  10.3 us
    ppermute x4, starting transfers between devices, body(): backward = lax.ppermute(backward, ('expert', 'xh'), step_down)  9.35 us
    dot_general x2, matrix products, body(): jnp.einsum('rf,rg->fg', blocks[i][0], absolute(blocks[i]), preferred_elem...  4.57 us
    dot_general x1, matrix products, body(): jnp.dot(onehot.astype(tokens.dtype), tokens, preferred_element_type=jnp.f...  4.26 us
    ppermute x1, waiting for transfers between devices, body(): relayed = lax.ppermute(jnp.stack(own_keys + far_keys), 'core', swap_core)  4.13 us
  transfers between devices with their start and end apart: 10, of which 5 were waited for; matrix products, arithmetic and copies ran while one was open for 13% of the time, Pallas kernels for 0%

profile of v8, /device:TPU:1, one launch (start us, length us, event | category | flops | bytes accessed | tf_op | source)
XLA Modules:
  0.0 164.4 jit_solution(9126932418343172568)
XLA Ops:
  0.7 0.7 fusion.30
  1.4 0.2 convolution_convert_fusion.1
  1.6 0.1 fusion.31
  1.7 0.0 slice-start
  1.7 4.3 %fusion = bf16[64,8,7168]{2,1,0:T(8,128)(2,1)S(1)} fusion(pred[512,256]{1,0:T(8,128)(4,1)S(1)} %bitcast.101, bf16[256,7168]{1,0:T(8,128)(2,1)} %param.5), kind=kOutput, calls=%fused_computation.1 | convolution fusion | flops 1882718208 | bytes 11141120 | tf_op jit(solution)/shard_map/dot_general | solution.py:35
  6.0 0.0 slice-start.1
  6.0 96.5 %all_to_all.5 = bf16[64,8,7168]{2,1,0:T(8,128)(2,1)S(1)} all-to-all(bf16[64,8,7168]{2,1,0:T(8,128)(2,1)S(1)} %fusion), channel_id=1, replica_groups=mesh['expert'=32,'xh'=2,'core'=2] {'expert','xh'}, dimensions={0} | all-to-all | bytes 14680064 | tf_op jit(solution)/shard_map/all_to_all | solution.py:39
  102.5 0.0 slice-start.2
  102.5 0.0 slice-start.3
  102.5 2.6 %collective-permute-start = (bf16[512,7168]{1,0:T(8,128)(2,1)S(1)}, bf16[512,7168]{1,0:T(8,128)(2,1)}, u32[]{:S(2)}, u32[]{:S(2)}) collective-permute-start(bf16[512,7168]{1,0:T(8,128)(2,1)S(1)} %bitcast.96), channel_id=1, source_target_pairs={{0,1},{1,0},{2,3},{3,2},{4,5},{5,4},{6,7},{7,6},{8,9},{9,8},{10,11... | collective-permute-start | bytes 22020104 | tf_op jit(solution)/shard_map/ppermute | solution.py:43
  105.1 0.0 slice-done
  105.1 0.0 slice-done.1
  105.1 3.9 %fusion.7 = f32[512,512]{1,0:T(8,128)S(1)} fusion(bf16[1,7168,512]{2,1,0:T(8,128)(2,1)S(1)} %bitcast.103, bf16[64,8,7168]{2,1,0:T(8,128)(2,1)S(1)} %all_to_all.5), kind=kOutput, calls=%fused_computation.8 | convolution fusion | flops 3758096384 | bytes 15728640 | tf_op jit(solution)/shard_map/dot_general | solution.py:64
  109.0 0.0 slice-done.2
  109.0 0.0 slice-done.3
  109.1 4.0 %fusion.27 = bf16[512,512]{1,0:T(8,128)(2,1)S(1)} fusion(bf16[1,7168,512]{2,1,0:T(8,128)(2,1)S(1)} %bitcast.105, f32[512,512]{1,0:T(8,128)S(1)} %fusion.7, bf16[64,8,7168]{2,1,0:T(8,128)(2,1)S(1)} %all_to_all.5), kind=kOutput, calls=%fused_computation.28 | convolution fusion | flops 3759669248 | bytes 16252928 | tf_op jit(solution)/shard_map/dot_general | solution.py:65
  113.1 1.8 %collective-permute-start.3 = (bf16[256,512]{1,0:T(8,128)(2,1)S(1)}, bf16[256,512]{1,0:T(8,128)(2,1)S(1)}, u32[]{:S(2)}, u32[]{:S(2)}) collective-permute-start(bf16[256,512]{1,0:T(8,128)(2,1)S(1)} %get-tuple-element.15), channel_id=1, source_target_pairs={{0,66},{2,64},{4,70},{6,68},{8,74},{10,72},{12,78},{14,76},{16,82}... | collective-permute-start | bytes 786440 | tf_op jit(solution)/shard_map/ppermute | solution.py:74
  115.0 0.0 collective-permute-start.1
  115.0 1.5 collective-permute-done
  116.5 6.4 %fusion.5 = f32[512,512]{1,0:T(8,128)S(1)} fusion(bf16[512,7168]{1,0:T(8,128)(2,1)} %collective-permute-done, bf16[1,7168,512]{2,1,0:T(8,128)(2,1)S(1)} %bitcast.103), kind=kOutput, calls=%fused_computation.6 | convolution fusion | flops 3758096384 | bytes 15728640 | tf_op jit(solution)/shard_map/dot_general | solution.py:64
  122.9 7.2 %multiply_convert_fusion = bf16[512,512]{1,0:T(8,128)(2,1)S(1)} fusion(f32[512,512]{1,0:T(8,128)S(1)} %fusion.5, bf16[512,7168]{1,0:T(8,128)(2,1)} %collective-permute-done, bf16[1,7168,512]{2,1,0:T(8,128)(2,1)S(1)} %bitcast.105), kind=kOutput, calls=%fused_computation.30 | convolution fusion | flops 3759669248 | bytes 16252928 | tf_op jit(solution)/shard_map/dot_general | solution.py:65
  130.1 0.6 collective-permute-start.5
  130.7 2.2 %collective-permute-start.7 = (bf16[256,512]{1,0:T(8,128)(2,1)S(1)}, bf16[256,512]{1,0:T(8,128)(2,1)S(1)}, u32[]{:S(2)}, u32[]{:S(2)}) collective-permute-start(bf16[256,512]{1,0:T(8,128)(2,1)S(1)} %get-tuple-element.13), channel_id=1, source_target_pairs={{0,66},{2,64},{4,70},{6,68},{8,74},{10,72},{12,78},{14,76},{16,82}... | collective-permute-start | bytes 786440 | tf_op jit(solution)/shard_map/ppermute | solution.py:74
  132.8 0.0 collective-permute-done.1
  132.8 0.0 collective-permute-start.2
  132.9 0.0 collective-permute-done.3
  132.9 2.7 %collective-permute-start.4 = (bf16[256,512]{1,0:T(8,128)(2,1)S(1)}, bf16[256,512]{1,0:T(8,128)(2,1)S(1)}, u32[]{:S(2)}, u32[]{:S(2)}) collective-permute-start(bf16[256,512]{1,0:T(8,128)(2,1)S(1)} %collective-permute-done.3), channel_id=1, source_target_pairs={{0,66},{2,64},{4,70},{6,68},{8,74},{10,72},{12,78},{14,76},{16,82}... | collective-permute-start | bytes 786440 | tf_op jit(solution)/shard_map/ppermute | solution.py:74
  135.5 3.3 %collective-permute-done.5 = bf16[256,512]{1,0:T(8,128)(2,1)S(1)} collective-permute-done((bf16[256,512]{1,0:T(8,128)(2,1)S(1)}, bf16[256,512]{1,0:T(8,128)(2,1)S(1)}, u32[]{:S(2)}, u32[]{:S(2)}) %collective-permute-start.5) | collective-permute-done | bytes 262176 | tf_op jit(solution)/shard_map/ppermute | solution.py:73
  138.9 0.0 collective-permute-start.6
  138.9 0.0 collective-permute-done.7
  138.9 2.7 %collective-permute-start.8 = (bf16[256,512]{1,0:T(8,128)(2,1)S(1)}, bf16[256,512]{1,0:T(8,128)(2,1)S(1)}, u32[]{:S(2)}, u32[]{:S(2)}) collective-permute-start(bf16[256,512]{1,0:T(8,128)(2,1)S(1)} %collective-permute-done.7), channel_id=1, source_target_pairs={{0,66},{2,64},{4,70},{6,68},{8,74},{10,72},{12,78},{14,76},{16,82}... | collective-permute-start | bytes 786440 | tf_op jit(solution)/shard_map/ppermute | solution.py:74
  141.6 2.9 %collective-permute-done.2 = bf16[256,512]{1,0:T(8,128)(2,1)S(1)} collective-permute-done((bf16[256,512]{1,0:T(8,128)(2,1)S(1)}, bf16[256,512]{1,0:T(8,128)(2,1)S(1)}, u32[]{:S(2)}, u32[]{:S(2)}) %collective-permute-start.2) | collective-permute-done | bytes 262176 | tf_op jit(solution)/shard_map/ppermute | solution.py:73
  144.5 0.0 collective-permute-done.4
  144.6 5.6 %collective-permute-done.6 = bf16[256,512]{1,0:T(8,128)(2,1)S(1)} collective-permute-done((bf16[256,512]{1,0:T(8,128)(2,1)S(1)}, bf16[256,512]{1,0:T(8,128)(2,1)S(1)}, u32[]{:S(2)}, u32[]{:S(2)}) %collective-permute-start.6) | collective-permute-done | bytes 262176 | tf_op jit(solution)/shard_map/ppermute | solution.py:73
  150.1 0.0 collective-permute-done.8
  150.2 1.6 pad_maximum_fusion
  151.8 1.2 collective-permute-start.9
  153.0 4.1 %collective-permute-done.9 = bf16[4,512,512]{2,1,0:T(8,128)(2,1)} collective-permute-done((bf16[4,512,512]{2,1,0:T(8,128)(2,1)}, bf16[4,512,512]{2,1,0:T(8,128)(2,1)}, u32[]{:S(2)}, u32[]{:S(2)}) %collective-permute-start.9) | collective-permute-done | bytes 2097184 | tf_op jit(solution)/shard_map/ppermute | solution.py:76
  157.1 1.4 broadcast_select_fusion.15
  158.5 1.3 fusion.9
  159.8 1.4 broadcast_select_fusion.11
  161.1 3.3 %multiply_bitcast_fusion = f32[1,512,2048]{2,1,0:T(8,128)} fusion(f32[512,2048]{1,0:T(8,128)S(1)} %fusion.9, bf16[512,512]{1,0:T(8,128)(2,1)S(1)} %multiply_convert_fusion, bf16[512,512]{1,0:T(8,128)(2,1)S(1)} %get-tuple-element.8, bf16[512,512]{1,0:T(8,128)(2,1)S(1)} %get-tuple-element.7, bf16[512,512]{1,0:T(8,128)(2,1)S(1)} %get-tuple-element.6, ...), kind=kOutput, calls=%fused_computation.10 | convolution fusion | flops 1084227584 | bytes 11010048 | tf_op jit(solution)/shard_map/rf,rg->fg/dot_general | solution.py:90
  (11 shorter events, 0.2 us)
Async XLA Ops:
  1.7 103.4 %slice-start = ((s8[7340032]{0:T(1024)(128)(4,1)}), s8[4194304]{0:T(1024)(128)(4,1)S(1)}, s32[]{:S(2)}) async-start(s8[7340032]{0:T(1024)(128)(4,1)} %bitcast.102), calls=%async_computation.1 | async-start | bytes 8388608
  6.0 99.1 %slice-start.1 = ((s8[7340032]{0:T(1024)(128)(4,1)}), s8[3145728]{0:T(1024)(128)(4,1)S(1)}, s32[]{:S(2)}) async-start(s8[7340032]{0:T(1024)(128)(4,1)} %bitcast.102), calls=%async_computation.2 | async-start | bytes 6291456
  102.5 6.6 %slice-start.2 = ((s8[7340032]{0:T(1024)(128)(4,1)}), s8[4194304]{0:T(1024)(128)(4,1)S(1)}, s32[]{:S(2)}) async-start(s8[7340032]{0:T(1024)(128)(4,1)} %bitcast.104), calls=%async_computation.3 | async-start | bytes 8388608
  102.5 6.6 %slice-start.3 = ((s8[7340032]{0:T(1024)(128)(4,1)}), s8[3145728]{0:T(1024)(128)(4,1)S(1)}, s32[]{:S(2)}) async-start(s8[7340032]{0:T(1024)(128)(4,1)} %bitcast.104), calls=%async_computation.4 | async-start | bytes 6291456
  102.5 14.0 %collective-permute-start = (bf16[512,7168]{1,0:T(8,128)(2,1)S(1)}, bf16[512,7168]{1,0:T(8,128)(2,1)}, u32[]{:S(2)}, u32[]{:S(2)}) collective-permute-start(bf16[512,7168]{1,0:T(8,128)(2,1)S(1)} %bitcast.96), channel_id=1, source_target_pairs={{0,1},{1,0},{2,3},{3,2},{4,5},{5,4},{6,7},{7,6},{8,9},{9,8},{10,11... | collective-permute-start | bytes 22020104 | tf_op jit(solution)/shard_map/ppermute | solution.py:43
  113.1 19.7 %collective-permute-start.3 = (bf16[256,512]{1,0:T(8,128)(2,1)S(1)}, bf16[256,512]{1,0:T(8,128)(2,1)S(1)}, u32[]{:S(2)}, u32[]{:S(2)}) collective-permute-start(bf16[256,512]{1,0:T(8,128)(2,1)S(1)} %get-tuple-element.15), channel_id=1, source_target_pairs={{0,66},{2,64},{4,70},{6,68},{8,74},{10,72},{12,78},{14,76},{16,82}... | collective-permute-start | bytes 786440 | tf_op jit(solution)/shard_map/ppermute | solution.py:74
  115.0 17.9 %collective-permute-start.1 = (bf16[256,512]{1,0:T(8,128)(2,1)S(1)}, bf16[256,512]{1,0:T(8,128)(2,1)S(1)}, u32[]{:S(2)}, u32[]{:S(2)}) collective-permute-start(bf16[256,512]{1,0:T(8,128)(2,1)S(1)} %get-tuple-element.16), channel_id=1, source_target_pairs={{0,64},{2,66},{4,68},{6,70},{8,72},{10,74},{12,76},{14,78},{16,80}... | collective-permute-start | bytes 786440 | tf_op jit(solution)/shard_map/ppermute | solution.py:73
  130.1 8.8 %collective-permute-start.5 = (bf16[256,512]{1,0:T(8,128)(2,1)S(1)}, bf16[256,512]{1,0:T(8,128)(2,1)S(1)}, u32[]{:S(2)}, u32[]{:S(2)}) collective-permute-start(bf16[256,512]{1,0:T(8,128)(2,1)S(1)} %get-tuple-element.14), channel_id=1, source_target_pairs={{0,64},{2,66},{4,68},{6,70},{8,72},{10,74},{12,76},{14,78},{16,80}... | collective-permute-start | bytes 786440 | tf_op jit(solution)/shard_map/ppermute | solution.py:73
  130.7 8.2 %collective-permute-start.7 = (bf16[256,512]{1,0:T(8,128)(2,1)S(1)}, bf16[256,512]{1,0:T(8,128)(2,1)S(1)}, u32[]{:S(2)}, u32[]{:S(2)}) collective-permute-start(bf16[256,512]{1,0:T(8,128)(2,1)S(1)} %get-tuple-element.13), channel_id=1, source_target_pairs={{0,66},{2,64},{4,70},{6,68},{8,74},{10,72},{12,78},{14,76},{16,82}... | collective-permute-start | bytes 786440 | tf_op jit(solution)/shard_map/ppermute | solution.py:74
  132.8 11.6 %collective-permute-start.2 = (bf16[256,512]{1,0:T(8,128)(2,1)S(1)}, bf16[256,512]{1,0:T(8,128)(2,1)S(1)}, u32[]{:S(2)}, u32[]{:S(2)}) collective-permute-start(bf16[256,512]{1,0:T(8,128)(2,1)S(1)} %collective-permute-done.1), channel_id=1, source_target_pairs={{0,64},{2,66},{4,68},{6,70},{8,72},{10,74},{12,76},{14,78},{16,80}... | collective-permute-start | bytes 786440 | tf_op jit(solution)/shard_map/ppermute | solution.py:73
  132.9 11.7 %collective-permute-start.4 = (bf16[256,512]{1,0:T(8,128)(2,1)S(1)}, bf16[256,512]{1,0:T(8,128)(2,1)S(1)}, u32[]{:S(2)}, u32[]{:S(2)}) collective-permute-start(bf16[256,512]{1,0:T(8,128)(2,1)S(1)} %collective-permute-done.3), channel_id=1, source_target_pairs={{0,66},{2,64},{4,70},{6,68},{8,74},{10,72},{12,78},{14,76},{16,82}... | collective-permute-start | bytes 786440 | tf_op jit(solution)/shard_map/ppermute | solution.py:74
  138.9 11.2 %collective-permute-start.6 = (bf16[256,512]{1,0:T(8,128)(2,1)S(1)}, bf16[256,512]{1,0:T(8,128)(2,1)S(1)}, u32[]{:S(2)}, u32[]{:S(2)}) collective-permute-start(bf16[256,512]{1,0:T(8,128)(2,1)S(1)} %collective-permute-done.5), channel_id=1, source_target_pairs={{0,64},{2,66},{4,68},{6,70},{8,72},{10,74},{12,76},{14,78},{16,80}... | collective-permute-start | bytes 786440 | tf_op jit(solution)/shard_map/ppermute | solution.py:73
  138.9 11.3 %collective-permute-start.8 = (bf16[256,512]{1,0:T(8,128)(2,1)S(1)}, bf16[256,512]{1,0:T(8,128)(2,1)S(1)}, u32[]{:S(2)}, u32[]{:S(2)}) collective-permute-start(bf16[256,512]{1,0:T(8,128)(2,1)S(1)} %collective-permute-done.7), channel_id=1, source_target_pairs={{0,66},{2,64},{4,70},{6,68},{8,74},{10,72},{12,78},{14,76},{16,82}... | collective-permute-start | bytes 786440 | tf_op jit(solution)/shard_map/ppermute | solution.py:74
  151.8 5.4 %collective-permute-start.9 = (bf16[4,512,512]{2,1,0:T(8,128)(2,1)}, bf16[4,512,512]{2,1,0:T(8,128)(2,1)}, u32[]{:S(2)}, u32[]{:S(2)}) collective-permute-start(bf16[4,512,512]{2,1,0:T(8,128)(2,1)} %pad_maximum_fusion), channel_id=1, source_target_pairs={{0,1},{1,0},{2,3},{3,2},{4,5},{5,4},{6,7},{7,6},{8,9},{9,8},{10,11... | collective-permute-start | bytes 6291464 | tf_op jit(solution)/shard_map/ppermute | solution.py:76

commit v9 on v7

--- a/solution.py
+++ b/solution.py
@@ -59,19 +59,18 @@
     ]
     on_second_core = lax.axis_index("core") == 1
     on_second_half = lax.axis_index("xh") == 1
-
-    def absolute(rel):
-        by_core = [jnp.where(on_second_core, rel[k ^ 1], rel[k]) for k in range(4)]
-        by_half = [jnp.where(on_second_half, by_core[k ^ 2], by_core[k]) for k in range(4)]
-        return jnp.concatenate(by_half, axis=1)
-
-    key_gram = None
-    for i in range(2):
-        part = jnp.einsum(
-            "rf,rg->fg", blocks[i][0], absolute(blocks[i]), preferred_element_type=jnp.float32
-        )
-        key_gram = part if key_gram is None else key_gram + part
-    key_gram = key_gram * factor
+    relative = []
+    for k in range(replica_count):
+        part = None
+        for i in range(2):
+            term = jnp.einsum(
+                "rf,rg->fg", blocks[i][0], blocks[i][k], preferred_element_type=jnp.float32
+            )
+            part = term if part is None else part + term
+        relative.append(with_layout_constraint(part, Layout(major_to_minor=(0, 1))))
+    by_core = [jnp.where(on_second_core, relative[k ^ 1], relative[k]) for k in range(4)]
+    by_half = [jnp.where(on_second_half, by_core[k ^ 2], by_core[k]) for k in range(4)]
+    key_gram = jnp.concatenate(by_half, axis=1) * factor
     return key_gram[None]
 
 

time: 152 us -> 154 us (1.013)
  matrix products: 24.9 us -> 29.5 us
  waiting for transfers between devices: 20.5 us -> 17.5 us
    dot_general x2 -> x8, matrix products: 4.57 us -> 9.17 us  [body(): jnp.einsum('rf,rg->fg', blocks[i][0], blocks[i][k], preferred_element_typ...]
    ppermute x1, waiting for transfers between devices: 3.99 us -> 0.97 us  [body(): relayed = lax.ppermute(jnp.stack(own_keys + far_keys), 'core', swap_core)]
    mul x0 -> x1, other arithmetic: none -> 2.45 us  [body(): key_gram = jnp.concatenate(by_half, axis=1) * factor]
    select_n x2 -> x0, other arithmetic: 1.55 us -> none  [absolute(): jnp.where(on_second_half, by_core[k ^ 2], by_core[k])]
  transfers between devices with their start and end apart: 4 -> 4, of which waited for: 4 -> 4; matrix products, arithmetic and copies ran while one was open for 10% -> 12% of each run, Pallas kernels for 0% -> 0%
where the time goes in v9:
time: 154 us; the launch traced here: 153 us
  blocking collectives  96.5 us (63%)
  matrix products  29.5 us (19%)
  waiting for transfers between devices  17.5 us (11%)
  starting transfers between devices  5.52 us (4%)
  other arithmetic  3.54 us (2%)
    all_to_all x1, blocking collectives, body(): lax.all_to_all(slot_rows, ('expert', 'xh'), split_axis=0, concat_axis=0,...  96.5 us
    ppermute x2, waiting for transfers between devices, body(): far_keys.append(lax.ppermute(keys, 'xh', swap_half))  14.2 us
    dot_general x8, matrix products, body(): jnp.einsum('rf,rg->fg', blocks[i][0], blocks[i][k], preferred_element_typ...  9.17 us
    dot_general x2, matrix products, body(): up_pre = jnp.dot(rows, w_up[0], preferred_element_type=jnp.float32)  8.05 us
    dot_general x2, matrix products, body(): gate_pre = jnp.dot(rows, w_gate[0], preferred_element_type=jnp.float32)  7.88 us
    dot_general x1, matrix products, body(): jnp.dot(onehot.astype(tokens.dtype), tokens, preferred_element_type=jnp.f...  4.26 us
  transfers between devices with their start and end apart: 4, of which 4 were waited for; matrix products, arithmetic and copies ran while one was open for 12% of the time, Pallas kernels for 0%

profile of v9, /device:TPU:1, one launch (start us, length us, event | category | flops | bytes accessed | tf_op | source)
XLA Modules:
  0.0 153.4 jit_solution(7486638451445573334)
XLA Ops:
  0.0 0.7 fusion.17
  1.4 0.2 convolution_convert_fusion.1
  1.6 0.1 fusion.18
  1.7 0.0 slice-start
  1.7 4.3 %fusion = bf16[64,8,7168]{2,1,0:T(8,128)(2,1)S(1)} fusion(pred[512,256]{1,0:T(8,128)(4,1)S(1)} %bitcast.75, bf16[256,7168]{1,0:T(8,128)(2,1)} %param.5), kind=kOutput, calls=%fused_computation.1 | convolution fusion | flops 1882718208 | bytes 11141120 | tf_op jit(solution)/shard_map/dot_general | solution.py:35
  6.0 0.0 slice-start.1
  6.0 96.5 %all_to_all.5 = bf16[64,8,7168]{2,1,0:T(8,128)(2,1)S(1)} all-to-all(bf16[64,8,7168]{2,1,0:T(8,128)(2,1)S(1)} %fusion), channel_id=1, replica_groups=mesh['expert'=32,'xh'=2,'core'=2] {'expert','xh'}, dimensions={0} | all-to-all | bytes 14680064 | tf_op jit(solution)/shard_map/all_to_all | solution.py:39
  102.5 0.0 slice-start.2
  102.5 0.0 slice-start.3
  102.5 2.6 %collective-permute-start = (bf16[512,7168]{1,0:T(8,128)(2,1)S(1)}, bf16[512,7168]{1,0:T(8,128)(2,1)S(1)}, u32[]{:S(2)}, u32[]{:S(2)}) collective-permute-start(bf16[512,7168]{1,0:T(8,128)(2,1)S(1)} %bitcast.72), channel_id=1, source_target_pairs={{0,1},{1,0},{2,3},{3,2},{4,5},{5,4},{6,7},{7,6},{8,9},{9,8},{10,11... | collective-permute-start | bytes 22020104 | tf_op jit(solution)/shard_map/ppermute | solution.py:43
  105.1 0.0 slice-done
  105.1 0.0 slice-done.1
  105.1 3.9 %fusion.7 = f32[512,512]{1,0:T(8,128)S(1)} fusion(bf16[1,7168,512]{2,1,0:T(8,128)(2,1)S(1)} %bitcast.77, bf16[64,8,7168]{2,1,0:T(8,128)(2,1)S(1)} %all_to_all.5), kind=kOutput, calls=%fused_computation.8 | convolution fusion | flops 3758096384 | bytes 15728640 | tf_op jit(solution)/shard_map/dot_general | solution.py:50
  109.0 0.0 slice-done.2
  109.0 0.0 slice-done.3
  109.1 4.0 %fusion.12 = bf16[512,512]{1,0:T(8,128)(2,1)S(1)} fusion(bf16[1,7168,512]{2,1,0:T(8,128)(2,1)S(1)} %bitcast.79, f32[512,512]{1,0:T(8,128)S(1)} %fusion.7, bf16[64,8,7168]{2,1,0:T(8,128)(2,1)S(1)} %all_to_all.5), kind=kOutput, calls=%fused_computation.17 | convolution fusion | flops 3759669248 | bytes 16252928 | tf_op jit(solution)/shard_map/dot_general | solution.py:51
  113.1 1.0 collective-permute-start.1
  114.1 2.3 %collective-permute-done = bf16[512,7168]{1,0:T(8,128)(2,1)S(1)} collective-permute-done((bf16[512,7168]{1,0:T(8,128)(2,1)S(1)}, bf16[512,7168]{1,0:T(8,128)(2,1)S(1)}, u32[]{:S(2)}, u32[]{:S(2)}) %collective-permute-start) | collective-permute-done | bytes 7340064 | tf_op jit(solution)/shard_map/ppermute | solution.py:43
  116.4 3.9 %fusion.5 = f32[512,512]{1,0:T(8,128)S(1)} fusion(bf16[512,7168]{1,0:T(8,128)(2,1)S(1)} %collective-permute-done, bf16[1,7168,512]{2,1,0:T(8,128)(2,1)S(1)} %bitcast.77), kind=kOutput, calls=%fused_computation.6 | convolution fusion | flops 3758096384 | bytes 15728640 | tf_op jit(solution)/shard_map/dot_general | solution.py:50
  120.3 4.0 %multiply_convert_fusion = bf16[512,512]{1,0:T(8,128)(2,1)S(1)} fusion(f32[512,512]{1,0:T(8,128)S(1)} %fusion.5, bf16[512,7168]{1,0:T(8,128)(2,1)S(1)} %collective-permute-done, bf16[1,7168,512]{2,1,0:T(8,128)(2,1)S(1)} %bitcast.79), kind=kOutput, calls=%fused_computation.23 | convolution fusion | flops 3759669248 | bytes 16252928 | tf_op jit(solution)/shard_map/dot_general | solution.py:51
  124.3 0.8 collective-permute-start.2
  125.1 3.2 %collective-permute-done.1 = bf16[512,512]{1,0:T(8,128)(2,1)S(1)} collective-permute-done((bf16[512,512]{1,0:T(8,128)(2,1)S(1)}, bf16[512,512]{1,0:T(8,128)(2,1)S(1)}, u32[]{:S(2)}, u32[]{:S(2)}) %collective-permute-start.1) | collective-permute-done | bytes 524320 | tf_op jit(solution)/shard_map/ppermute | solution.py:55
  128.3 0.0 copy-start
  128.3 11.0 %collective-permute-done.2 = bf16[512,512]{1,0:T(8,128)(2,1)S(1)} collective-permute-done((bf16[512,512]{1,0:T(8,128)(2,1)S(1)}, bf16[512,512]{1,0:T(8,128)(2,1)S(1)}, u32[]{:S(2)}, u32[]{:S(2)}) %collective-permute-start.2) | collective-permute-done | bytes 524320 | tf_op jit(solution)/shard_map/ppermute | solution.py:55
  139.4 0.0 copy-start.2
  139.4 0.3 pad_maximum_fusion
  139.6 1.1 collective-permute-start.3
  140.8 0.0 copy-done
  140.8 0.0 copy-done.2
  140.8 0.0 copy-start.1
  140.8 0.5 fusion.24
  141.3 0.5 convolution_add_fusion
  141.7 1.5 fusion.23
  143.2 0.0 copy-done.1
  143.3 0.5 convolution_add_fusion.2
  143.7 1.0 collective-permute-done.3
  144.7 1.5 fusion.16
  146.2 1.5 fusion.15
  147.7 1.5 convolution_add_fusion.1
  149.2 1.8 %select_bitcast_fusion.3 = (f32[1,512,512]{2,1,0:T(8,128)S(1)}, f32[1,512,512]{2,1,0:T(8,128)S(1)}, f32[1,512,512]{2,1,0:T(8,128)S(1)}, f32[1,512,512]{2,1,0:T(8,128)S(1)}) fusion(pred[]{:T(512)S(6)} %eq.36, f32[512,512]{1,0:T(8,128)S(1)} %convolution_add_fusion.2, pred[]{:T(512)S(6)} %eq.37, f32[512,512]{1,0:T(8,128)S(1)} %convolution_add_fusion.1, ...), kind=kOutput, calls=%fused_computation.22 | convolution fusion | flops 270794752 | bytes 9437186 | tf_op jit(solution)/shard_map/rf,rg->fg/dot_general | solution.py:66
  151.0 2.4 %maximum_multiply_fusion = f32[1,512,2048]{2,1,0:T(8,128)} fusion(f32[1,512,512]{2,1,0:T(8,128)S(1)} %get-tuple-element.8, f32[1,512,512]{2,1,0:T(8,128)S(1)} %get-tuple-element.7, f32[1,512,512]{2,1,0:T(8,128)S(1)} %get-tuple-element.6, f32[1,512,512]{2,1,0:T(8,128)S(1)} %get-tuple-element.5), kind=kLoop, calls=%fused_computation.10 | loop fusion | flops 4194304 | bytes 8388608 | tf_op jit(solution)/shard_map/mul | solution.py:73
  (5 shorter events, 0.1 us)
Async XLA Ops:
  1.7 103.4 %slice-start = ((s8[7340032]{0:T(1024)(128)(4,1)}), s8[4194304]{0:T(1024)(128)(4,1)S(1)}, s32[]{:S(2)}) async-start(s8[7340032]{0:T(1024)(128)(4,1)} %bitcast.76), calls=%async_computation.1 | async-start | bytes 8388608
  6.0 99.1 %slice-start.1 = ((s8[7340032]{0:T(1024)(128)(4,1)}), s8[3145728]{0:T(1024)(128)(4,1)S(1)}, s32[]{:S(2)}) async-start(s8[7340032]{0:T(1024)(128)(4,1)} %bitcast.76), calls=%async_computation.2 | async-start | bytes 6291456
  102.5 6.6 %slice-start.2 = ((s8[7340032]{0:T(1024)(128)(4,1)}), s8[4194304]{0:T(1024)(128)(4,1)S(1)}, s32[]{:S(2)}) async-start(s8[7340032]{0:T(1024)(128)(4,1)} %bitcast.78), calls=%async_computation.3 | async-start | bytes 8388608
  102.5 6.6 %slice-start.3 = ((s8[7340032]{0:T(1024)(128)(4,1)}), s8[3145728]{0:T(1024)(128)(4,1)S(1)}, s32[]{:S(2)}) async-start(s8[7340032]{0:T(1024)(128)(4,1)} %bitcast.78), calls=%async_computation.4 | async-start | bytes 6291456
  102.5 13.9 %collective-permute-start = (bf16[512,7168]{1,0:T(8,128)(2,1)S(1)}, bf16[512,7168]{1,0:T(8,128)(2,1)S(1)}, u32[]{:S(2)}, u32[]{:S(2)}) collective-permute-start(bf16[512,7168]{1,0:T(8,128)(2,1)S(1)} %bitcast.72), channel_id=1, source_target_pairs={{0,1},{1,0},{2,3},{3,2},{4,5},{5,4},{6,7},{7,6},{8,9},{9,8},{10,11... | collective-permute-start | bytes 22020104 | tf_op jit(solution)/shard_map/ppermute | solution.py:43
  113.1 15.2 %collective-permute-start.1 = (bf16[512,512]{1,0:T(8,128)(2,1)S(1)}, bf16[512,512]{1,0:T(8,128)(2,1)S(1)}, u32[]{:S(2)}, u32[]{:S(2)}) collective-permute-start(bf16[512,512]{1,0:T(8,128)(2,1)S(1)} %fusion.12), channel_id=1, source_target_pairs={{0,2},{2,0},{1,3},{3,1},{4,6},{6,4},{5,7},{7,5},{8,10},{10,8},{9,1... | collective-permute-start | bytes 1572872 | tf_op jit(solution)/shard_map/ppermute | solution.py:55
  124.3 15.0 %collective-permute-start.2 = (bf16[512,512]{1,0:T(8,128)(2,1)S(1)}, bf16[512,512]{1,0:T(8,128)(2,1)S(1)}, u32[]{:S(2)}, u32[]{:S(2)}) collective-permute-start(bf16[512,512]{1,0:T(8,128)(2,1)S(1)} %multiply_convert_fusion), channel_id=1, source_target_pairs={{0,2},{2,0},{1,3},{3,1},{4,6},{6,4},{5,7},{7,5},{8,10},{10,8},{9,1... | collective-permute-start | bytes 1572872 | tf_op jit(solution)/shard_map/ppermute | solution.py:55
  128.3 12.5 %copy-start = (bf16[512,512]{1,0:T(8,128)(2,1)}, bf16[512,512]{1,0:T(8,128)(2,1)S(1)}, u32[]{:S(2)}) copy-start(bf16[512,512]{1,0:T(8,128)(2,1)S(1)} %collective-permute-done.1) | copy-start | bytes 1572868
  139.4 1.4 copy-start.2
  139.6 5.1 %collective-permute-start.3 = (bf16[4,512,512]{2,1,0:T(8,128)(2,1)S(1)}, bf16[4,512,512]{2,1,0:T(8,128)(2,1)}, u32[]{:S(2)}, u32[]{:S(2)}) collective-permute-start(bf16[4,512,512]{2,1,0:T(8,128)(2,1)S(1)} %pad_maximum_fusion), channel_id=1, source_target_pairs={{0,1},{1,0},{2,3},{3,2},{4,5},{5,4},{6,7},{7,6},{8,9},{9,8},{10,11... | collective-permute-start | bytes 6291464 | tf_op jit(solution)/shard_map/ppermute | solution.py:56
  140.8 2.5 %copy-start.1 = (bf16[512,512]{1,0:T(8,128)(2,1)S(1)}, bf16[512,512]{1,0:T(8,128)(2,1)}, u32[]{:S(2)}) copy-start(bf16[512,512]{1,0:T(8,128)(2,1)} %copy-done) | copy-start | bytes 1572868

commit v10 on v7

--- a/solution.py
+++ b/solution.py
@@ -45,14 +45,20 @@
     swap_half = [(h, (h + 1) % half_count) for h in range(half_count)]
     swap_core = [(c, (c + 1) % core_count) for c in range(core_count)]
     replica_count = half_count * core_count
+    rows_half = slot_block.shape[0] // 2
+    pieces = [[slot_block[:rows_half], slot_block[rows_half:]], [partner]]
     own_keys, far_keys = [], []
-    for rows in (slot_block, partner):
-        gate_pre = jnp.dot(rows, w_gate[0], preferred_element_type=jnp.float32)
-        up_pre = jnp.dot(rows, w_up[0], preferred_element_type=jnp.float32)
-        keys = (jax.nn.silu(gate_pre) * up_pre).astype(jnp.bfloat16)
-        keys = with_layout_constraint(keys, Layout(major_to_minor=(0, 1)))
-        own_keys.append(keys)
-        far_keys.append(lax.ppermute(keys, "xh", swap_half))
+    for group in pieces:
+        keys_here, far_here = [], []
+        for rows in group:
+            gate_pre = jnp.dot(rows, w_gate[0], preferred_element_type=jnp.float32)
+            up_pre = jnp.dot(rows, w_up[0], preferred_element_type=jnp.float32)
+            keys = (jax.nn.silu(gate_pre) * up_pre).astype(jnp.bfloat16)
+            keys = with_layout_constraint(keys, Layout(major_to_minor=(0, 1)))
+            keys_here.append(keys)
+            far_here.append(lax.ppermute(keys, "xh", swap_half))
+        own_keys.append(jnp.concatenate(keys_here, axis=0))
+        far_keys.append(jnp.concatenate(far_here, axis=0))
     relayed = lax.ppermute(jnp.stack(own_keys + far_keys), "core", swap_core)
     blocks = [
         [own_keys[i], relayed[1 - i], far_keys[i], relayed[3 - i]] for i in range(2)

time: 152 us -> 165 us (1.086)
  matrix products: 24.9 us -> 30.8 us
  waiting for transfers between devices: 20.5 us -> 23.4 us
  starting transfers between devices: 5.46 us -> 7.94 us
    dot_general x2 -> x3, matrix products: 8.05 us -> 11.3 us  [body(): up_pre = jnp.dot(rows, w_up[0], preferred_element_type=jnp.float32)]
    dot_general x2 -> x3, matrix products: 7.88 us -> 10.4 us  [body(): gate_pre = jnp.dot(rows, w_gate[0], preferred_element_type=jnp.float32)]
    ppermute x2 -> x3, starting transfers between devices: 1.78 us -> 4.11 us  [body(): far_here.append(lax.ppermute(keys, 'xh', swap_half))]
    ppermute x1, waiting for transfers between devices: 2.3 us -> 4.41 us  [body(): lax.ppermute(slot_block, 'core', [(c, (c + 1) % core_count) for c in rang...]
    ppermute x2 -> x3, waiting for transfers between devices: 14.2 us -> 15 us  [body(): far_here.append(lax.ppermute(keys, 'xh', swap_half))]
  transfers between devices with their start and end apart: 4 -> 5, of which waited for: 4 -> 3; matrix products, arithmetic and copies ran while one was open for 10% -> 13% of each run, Pallas kernels for 0% -> 0%
where the time goes in v10:
time: 165 us
  blocking collectives  96.5 us (58%)
  matrix products  30.8 us (19%)
  waiting for transfers between devices  23.4 us (14%)
  starting transfers between devices  7.94 us (5%)
  other arithmetic  4.14 us (3%)
    all_to_all x1, blocking collectives, body(): lax.all_to_all(slot_rows, ('expert', 'xh'), split_axis=0, concat_axis=0,...  96.5 us
    ppermute x3, waiting for transfers between devices, body(): far_here.append(lax.ppermute(keys, 'xh', swap_half))  15 us
    dot_general x3, matrix products, body(): up_pre = jnp.dot(rows, w_up[0], preferred_element_type=jnp.float32)  11.3 us
    dot_general x3, matrix products, body(): gate_pre = jnp.dot(rows, w_gate[0], preferred_element_type=jnp.float32)  10.4 us
    dot_general x2, matrix products, body(): jnp.einsum('rf,rg->fg', blocks[i][0], absolute(blocks[i]), preferred_elem...  4.6 us
    ppermute x1, waiting for transfers between devices, body(): lax.ppermute(slot_block, 'core', [(c, (c + 1) % core_count) for c in rang...  4.41 us
    dot_general x1, matrix products, body(): jnp.dot(onehot.astype(tokens.dtype), tokens, preferred_element_type=jnp.f...  4.26 us
    ppermute x3, starting transfers between devices, body(): far_here.append(lax.ppermute(keys, 'xh', swap_half))  4.11 us
  transfers between devices with their start and end apart: 5, of which 3 were waited for; matrix products, arithmetic and copies ran while one was open for 13% of the time, Pallas kernels for 0%

profile of v10, /device:TPU:1, one launch (start us, length us, event | category | flops | bytes accessed | tf_op | source)
XLA Modules:
  0.0 164.5 jit_solution(1255165213119599863)
XLA Ops:
  0.0 0.7 fusion.40
  1.4 0.2 convolution_convert_fusion.1
  1.6 0.1 fusion.41
  1.7 0.0 slice-start
  1.7 4.3 %fusion = bf16[64,8,7168]{2,1,0:T(8,128)(2,1)S(1)} fusion(pred[512,256]{1,0:T(8,128)(4,1)S(1)} %bitcast.120, bf16[256,7168]{1,0:T(8,128)(2,1)} %param.5), kind=kOutput, calls=%fused_computation.1 | convolution fusion | flops 1882718208 | bytes 11141120 | tf_op jit(solution)/shard_map/dot_general | solution.py:35
  6.0 0.0 slice-start.1
  6.0 96.5 %all_to_all.5 = bf16[64,8,7168]{2,1,0:T(8,128)(2,1)S(1)} all-to-all(bf16[64,8,7168]{2,1,0:T(8,128)(2,1)S(1)} %fusion), channel_id=1, replica_groups=mesh['expert'=32,'xh'=2,'core'=2] {'expert','xh'}, dimensions={0} | all-to-all | bytes 14680064 | tf_op jit(solution)/shard_map/all_to_all | solution.py:39
  102.5 0.0 slice-start.2
  102.5 0.0 slice-start.3
  102.5 2.6 %collective-permute-start = (bf16[512,7168]{1,0:T(8,128)(2,1)S(1)}, bf16[512,7168]{1,0:T(8,128)(2,1)}, u32[]{:S(2)}, u32[]{:S(2)}) collective-permute-start(bf16[512,7168]{1,0:T(8,128)(2,1)S(1)} %bitcast.116), channel_id=1, source_target_pairs={{0,1},{1,0},{2,3},{3,2},{4,5},{5,4},{6,7},{7,6},{8,9},{9,8},{10,11... | collective-permute-start | bytes 22020104 | tf_op jit(solution)/shard_map/ppermute | solution.py:43
  105.1 0.0 slice-done
  105.1 0.0 slice-done.1
  105.1 2.0 %fusion.11 = f32[256,512]{1,0:T(8,128)S(1)} fusion(bf16[1,7168,512]{2,1,0:T(8,128)(2,1)S(1)} %bitcast.122, bf16[64,8,7168]{2,1,0:T(8,128)(2,1)S(1)} %all_to_all.5), kind=kOutput, calls=%fused_computation.12 | convolution fusion | flops 1879048192 | bytes 11534336 | tf_op jit(solution)/shard_map/dot_general | solution.py:54
  107.1 0.0 slice-done.2
  107.1 0.0 slice-done.3
  107.2 2.1 %fusion.37 = bf16[256,512]{1,0:T(8,128)(2,1)S(1)} fusion(bf16[1,7168,512]{2,1,0:T(8,128)(2,1)S(1)} %bitcast.124, bf16[64,8,7168]{2,1,0:T(8,128)(2,1)S(1)} %all_to_all.5, f32[256,512]{1,0:T(8,128)S(1)} %fusion.11), kind=kOutput, calls=%fused_computation.36 | convolution fusion | flops 1879834624 | bytes 11796480 | tf_op jit(solution)/shard_map/dot_general | solution.py:55
  109.2 0.8 collective-permute-start.1
  110.0 2.0 %fusion.9 = f32[256,512]{1,0:T(8,128)S(1)} fusion(bf16[1,7168,512]{2,1,0:T(8,128)(2,1)S(1)} %bitcast.122, bf16[64,8,7168]{2,1,0:T(8,128)(2,1)S(1)} %all_to_all.5), kind=kOutput, calls=%fused_computation.10 | convolution fusion | flops 1879048192 | bytes 11534336 | tf_op jit(solution)/shard_map/dot_general | solution.py:54
  112.1 4.4 %collective-permute-done = bf16[512,7168]{1,0:T(8,128)(2,1)} collective-permute-done((bf16[512,7168]{1,0:T(8,128)(2,1)S(1)}, bf16[512,7168]{1,0:T(8,128)(2,1)}, u32[]{:S(2)}, u32[]{:S(2)}) %collective-permute-start) | collective-permute-done | bytes 7340064 | tf_op jit(solution)/shard_map/ppermute | solution.py:43
  116.5 6.4 %fusion.7 = f32[512,512]{1,0:T(8,128)S(1)} fusion(bf16[512,7168]{1,0:T(8,128)(2,1)} %collective-permute-done, bf16[1,7168,512]{2,1,0:T(8,128)(2,1)S(1)} %bitcast.122), kind=kOutput, calls=%fused_computation.8 | convolution fusion | flops 3758096384 | bytes 15728640 | tf_op jit(solution)/shard_map/dot_general | solution.py:54
  122.9 7.2 %multiply_convert_fusion = bf16[512,512]{1,0:T(8,128)(2,1)S(1)} fusion(f32[512,512]{1,0:T(8,128)S(1)} %fusion.7, bf16[512,7168]{1,0:T(8,128)(2,1)} %collective-permute-done, bf16[1,7168,512]{2,1,0:T(8,128)(2,1)S(1)} %bitcast.124), kind=kOutput, calls=%fused_computation.38 | convolution fusion | flops 3759669248 | bytes 16252928 | tf_op jit(solution)/shard_map/dot_general | solution.py:55
  130.0 1.0 collective-permute-start.3
  131.0 2.1 %fusion.34 = bf16[256,512]{1,0:T(8,128)(2,1)S(1)} fusion(bf16[1,7168,512]{2,1,0:T(8,128)(2,1)S(1)} %bitcast.124, bf16[64,8,7168]{2,1,0:T(8,128)(2,1)S(1)} %all_to_all.5, f32[256,512]{1,0:T(8,128)S(1)} %fusion.9), kind=kOutput, calls=%fused_computation.35 | convolution fusion | flops 1879834624 | bytes 11796480 | tf_op jit(solution)/shard_map/dot_general | solution.py:55
  133.1 0.0 copy-start.2
  133.1 2.3 %collective-permute-start.2 = (bf16[256,512]{1,0:T(8,128)(2,1)S(1)}, bf16[256,512]{1,0:T(8,128)(2,1)S(1)}, u32[]{:S(2)}, u32[]{:S(2)}) collective-permute-start(bf16[256,512]{1,0:T(8,128)(2,1)S(1)} %fusion.34), channel_id=1, source_target_pairs={{0,2},{2,0},{1,3},{3,1},{4,6},{6,4},{5,7},{7,5},{8,10},{10,8},{9,1... | collective-permute-start | bytes 786440 | tf_op jit(solution)/shard_map/ppermute | solution.py:59
  135.5 0.0 collective-permute-done.1
  135.5 15.0 %collective-permute-done.2 = bf16[256,512]{1,0:T(8,128)(2,1)S(1)} collective-permute-done((bf16[256,512]{1,0:T(8,128)(2,1)S(1)}, bf16[256,512]{1,0:T(8,128)(2,1)S(1)}, u32[]{:S(2)}, u32[]{:S(2)}) %collective-permute-start.2) | collective-permute-done | bytes 262176 | tf_op jit(solution)/shard_map/ppermute | solution.py:59
  150.6 0.0 collective-permute-done.3
  150.6 0.0 copy-start
  150.6 0.8 copy-done
  151.4 1.6 pad_maximum_fusion
  152.9 0.0 copy-done.2
  152.9 1.2 collective-permute-start.4
  154.2 0.0 copy-start.3
  154.2 4.0 %collective-permute-done.4 = bf16[4,512,512]{2,1,0:T(8,128)(2,1)S(1)} collective-permute-done((bf16[4,512,512]{2,1,0:T(8,128)(2,1)}, bf16[4,512,512]{2,1,0:T(8,128)(2,1)S(1)}, u32[]{:S(2)}, u32[]{:S(2)}) %collective-permute-start.4) | collective-permute-done | bytes 2097184 | tf_op jit(solution)/shard_map/ppermute | solution.py:62
  158.2 1.5 broadcast_select_fusion.15
  159.7 0.0 copy-done.3
  159.7 0.0 copy-start.1
  159.7 1.3 fusion.13
  161.0 0.0 copy-done.1
  161.0 0.2 broadcast_select_fusion.11
  161.2 3.3 %multiply_bitcast_fusion = f32[1,512,2048]{2,1,0:T(8,128)} fusion(f32[512,2048]{1,0:T(8,128)S(1)} %fusion.13, bf16[512,512]{1,0:T(8,128)(2,1)S(1)} %multiply_convert_fusion, bf16[512,512]{1,0:T(8,128)(2,1)S(1)} %get-tuple-element.8, bf16[512,512]{1,0:T(8,128)(2,1)S(1)} %get-tuple-element.7, bf16[512,512]{1,0:T(8,128)(2,1)S(1)} %get-tuple-element.6, ...), kind=kOutput, calls=%fused_computation.14 | convolution fusion | flops 1084227584 | bytes 11010048 | tf_op jit(solution)/shard_map/rf,rg->fg/dot_general | solution.py:76
  (8 shorter events, 0.1 us)
Async XLA Ops:
  1.7 103.4 %slice-start = ((s8[7340032]{0:T(1024)(128)(4,1)}), s8[4194304]{0:T(1024)(128)(4,1)S(1)}, s32[]{:S(2)}) async-start(s8[7340032]{0:T(1024)(128)(4,1)} %bitcast.121), calls=%async_computation.1 | async-start | bytes 8388608
  6.0 99.1 %slice-start.1 = ((s8[7340032]{0:T(1024)(128)(4,1)}), s8[3145728]{0:T(1024)(128)(4,1)S(1)}, s32[]{:S(2)}) async-start(s8[7340032]{0:T(1024)(128)(4,1)} %bitcast.121), calls=%async_computation.2 | async-start | bytes 6291456
  102.5 4.7 %slice-start.2 = ((s8[7340032]{0:T(1024)(128)(4,1)}), s8[4194304]{0:T(1024)(128)(4,1)S(1)}, s32[]{:S(2)}) async-start(s8[7340032]{0:T(1024)(128)(4,1)} %bitcast.123), calls=%async_computation.3 | async-start | bytes 8388608
  102.5 4.7 %slice-start.3 = ((s8[7340032]{0:T(1024)(128)(4,1)}), s8[3145728]{0:T(1024)(128)(4,1)S(1)}, s32[]{:S(2)}) async-start(s8[7340032]{0:T(1024)(128)(4,1)} %bitcast.123), calls=%async_computation.4 | async-start | bytes 6291456
  102.5 14.0 %collective-permute-start = (bf16[512,7168]{1,0:T(8,128)(2,1)S(1)}, bf16[512,7168]{1,0:T(8,128)(2,1)}, u32[]{:S(2)}, u32[]{:S(2)}) collective-permute-start(bf16[512,7168]{1,0:T(8,128)(2,1)S(1)} %bitcast.116), channel_id=1, source_target_pairs={{0,1},{1,0},{2,3},{3,2},{4,5},{5,4},{6,7},{7,6},{8,9},{9,8},{10,11... | collective-permute-start | bytes 22020104 | tf_op jit(solution)/shard_map/ppermute | solution.py:43
  109.2 26.2 %collective-permute-start.1 = (bf16[256,512]{1,0:T(8,128)(2,1)S(1)}, bf16[256,512]{1,0:T(8,128)(2,1)S(1)}, u32[]{:S(2)}, u32[]{:S(2)}) collective-permute-start(bf16[256,512]{1,0:T(8,128)(2,1)S(1)} %fusion.37), channel_id=1, source_target_pairs={{0,2},{2,0},{1,3},{3,1},{4,6},{6,4},{5,7},{7,5},{8,10},{10,8},{9,1... | collective-permute-start | bytes 786440 | tf_op jit(solution)/shard_map/ppermute | solution.py:59
  130.0 20.5 %collective-permute-start.3 = (bf16[512,512]{1,0:T(8,128)(2,1)S(1)}, bf16[512,512]{1,0:T(8,128)(2,1)S(1)}, u32[]{:S(2)}, u32[]{:S(2)}) collective-permute-start(bf16[512,512]{1,0:T(8,128)(2,1)S(1)} %multiply_convert_fusion), channel_id=1, source_target_pairs={{0,2},{2,0},{1,3},{3,1},{4,6},{6,4},{5,7},{7,5},{8,10},{10,8},{9,1... | collective-permute-start | bytes 1572872 | tf_op jit(solution)/shard_map/ppermute | solution.py:59
  133.1 19.8 %copy-start.2 = (bf16[256,512]{1,0:T(8,128)(2,1)}, bf16[256,512]{1,0:T(8,128)(2,1)S(1)}, u32[]{:S(2)}) copy-start(bf16[256,512]{1,0:T(8,128)(2,1)S(1)} %fusion.34) | copy-start | bytes 786436
  133.1 17.4 %collective-permute-start.2 = (bf16[256,512]{1,0:T(8,128)(2,1)S(1)}, bf16[256,512]{1,0:T(8,128)(2,1)S(1)}, u32[]{:S(2)}, u32[]{:S(2)}) collective-permute-start(bf16[256,512]{1,0:T(8,128)(2,1)S(1)} %fusion.34), channel_id=1, source_target_pairs={{0,2},{2,0},{1,3},{3,1},{4,6},{6,4},{5,7},{7,5},{8,10},{10,8},{9,1... | collective-permute-start | bytes 786440 | tf_op jit(solution)/shard_map/ppermute | solution.py:59
  150.6 0.8 copy-start
  152.9 5.2 %collective-permute-start.4 = (bf16[4,512,512]{2,1,0:T(8,128)(2,1)}, bf16[4,512,512]{2,1,0:T(8,128)(2,1)S(1)}, u32[]{:S(2)}, u32[]{:S(2)}) collective-permute-start(bf16[4,512,512]{2,1,0:T(8,128)(2,1)} %pad_maximum_fusion), channel_id=1, source_target_pairs={{0,1},{1,0},{2,3},{3,2},{4,5},{5,4},{6,7},{7,6},{8,9},{9,8},{10,11... | collective-permute-start | bytes 6291464 | tf_op jit(solution)/shard_map/ppermute | solution.py:62
  154.2 5.5 %copy-start.3 = (bf16[256,512]{1,0:T(8,128)(2,1)S(1)}, bf16[256,512]{1,0:T(8,128)(2,1)}, u32[]{:S(2)}) copy-start(bf16[256,512]{1,0:T(8,128)(2,1)} %copy-done.2) | copy-start | bytes 786436
  159.7 1.3 copy-start.1

commit v11 on v7

--- a/solution.py
+++ b/solution.py
@@ -30,14 +30,14 @@
     capacity = slot_total * TOP // N_ROUTED
     onehot = slot_onehot(routes, counts[0], expert_count, capacity)
     onehot = jnp.broadcast_to(
-        onehot[:, None], (expert_count, half_count, capacity, slot_total)
-    ).reshape(expert_count * half_count * capacity, slot_total)
+        onehot[None], (half_count, expert_count, capacity, slot_total)
+    ).reshape(half_count * expert_count * capacity, slot_total)
     slot_rows = jnp.dot(
         onehot.astype(tokens.dtype), tokens, preferred_element_type=jnp.float32
     ).astype(tokens.dtype)
     slot_rows = slot_rows.reshape(expert_count * half_count, capacity, width_model)
     slot_block = lax.all_to_all(
-        slot_rows, ("expert", "xh"), split_axis=0, concat_axis=0, tiled=True
+        slot_rows, ("xh", "expert"), split_axis=0, concat_axis=0, tiled=True
     )
     slot_block = slot_block.reshape(expert_count * half_count * capacity, width_model)
     partner = lax.ppermute(slot_block, "core", [(c, (c + 1) % core_count) for c in range(core_count)])

time: 152 us -> 156 us (1.026)
  blocking collectives: 96.5 us -> 100 us
  starting transfers between devices: 5.46 us -> 3.72 us
    all_to_all x1, blocking collectives: 96.5 us -> 100 us  [body(): lax.all_to_all(slot_rows, ('xh', 'expert'), split_axis=0, concat_axis=0,...]
where the time goes in v11:
time: 156 us; the launch traced here: 155 us
  blocking collectives  100 us (64%)
  matrix products  24.9 us (16%)
  waiting for transfers between devices  21.9 us (14%)
  other arithmetic  3.97 us (3%)
  starting transfers between devices  3.72 us (2%)
    all_to_all x1, blocking collectives, body(): lax.all_to_all(slot_rows, ('xh', 'expert'), split_axis=0, concat_axis=0,...  100 us
    ppermute x2, waiting for transfers between devices, body(): far_keys.append(lax.ppermute(keys, 'xh', swap_half))  14.9 us
    dot_general x2, matrix products, body(): up_pre = jnp.dot(rows, w_up[0], preferred_element_type=jnp.float32)  8.05 us
    dot_general x2, matrix products, body(): gate_pre = jnp.dot(rows, w_gate[0], preferred_element_type=jnp.float32)  7.88 us
    dot_general x2, matrix products, body(): jnp.einsum('rf,rg->fg', blocks[i][0], absolute(blocks[i]), preferred_elem...  4.57 us
    dot_general x1, matrix products, body(): jnp.dot(onehot.astype(tokens.dtype), tokens, preferred_element_type=jnp.f...  4.26 us
    ppermute x1, waiting for transfers between devices, body(): relayed = lax.ppermute(jnp.stack(own_keys + far_keys), 'core', swap_core)  3.99 us
  transfers between devices with their start and end apart: 4, of which 4 were waited for; matrix products, arithmetic and copies ran while one was open for 10% of the time, Pallas kernels for 0%

profile of v11, /device:TPU:1, one launch (start us, length us, event | category | flops | bytes accessed | tf_op | source)
XLA Modules:
  0.0 155.4 jit_solution(8891930321502931575)
XLA Ops:
  0.7 0.7 fusion.30
  1.4 0.2 convolution_convert_fusion.1
  1.6 0.1 fusion.31
  1.7 0.0 slice-start
  1.7 4.3 %fusion = bf16[64,8,7168]{2,1,0:T(8,128)(2,1)S(1)} fusion(pred[512,256]{1,0:T(8,128)(4,1)S(1)} %bitcast.101, bf16[256,7168]{1,0:T(8,128)(2,1)} %param.5), kind=kOutput, calls=%fused_computation.1 | convolution fusion | flops 1882718208 | bytes 11141120 | tf_op jit(solution)/shard_map/dot_general | solution.py:35
  6.0 0.0 slice-start.1
  6.0 100.0 %all_to_all.5 = bf16[64,8,7168]{2,1,0:T(8,128)(2,1)S(1)} all-to-all(bf16[64,8,7168]{2,1,0:T(8,128)(2,1)S(1)} %fusion), channel_id=1, replica_groups=mesh['expert'=32,'xh'=2,'core'=2] {'xh','expert'}, dimensions={0} | all-to-all | bytes 14680064 | tf_op jit(solution)/shard_map/all_to_all | solution.py:39
  106.0 0.0 slice-start.2
  106.0 0.0 slice-start.3
  106.0 2.3 %collective-permute-start = (bf16[512,7168]{1,0:T(8,128)(2,1)S(1)}, bf16[512,7168]{1,0:T(8,128)(2,1)S(1)}, u32[]{:S(2)}, u32[]{:S(2)}) collective-permute-start(bf16[512,7168]{1,0:T(8,128)(2,1)S(1)} %bitcast.96), channel_id=1, source_target_pairs={{0,1},{1,0},{2,3},{3,2},{4,5},{5,4},{6,7},{7,6},{8,9},{9,8},{10,11... | collective-permute-start | bytes 22020104 | tf_op jit(solution)/shard_map/ppermute | solution.py:43
  108.3 0.0 slice-done
  108.3 0.0 slice-done.1
  108.3 3.9 %fusion.7 = f32[512,512]{1,0:T(8,128)S(1)} fusion(bf16[1,7168,512]{2,1,0:T(8,128)(2,1)S(1)} %bitcast.103, bf16[64,8,7168]{2,1,0:T(8,128)(2,1)S(1)} %all_to_all.5), kind=kOutput, calls=%fused_computation.8 | convolution fusion | flops 3758096384 | bytes 15728640 | tf_op jit(solution)/shard_map/dot_general | solution.py:50
  112.3 0.0 slice-done.2
  112.3 0.0 slice-done.3
  112.3 4.0 %fusion.27 = bf16[512,512]{1,0:T(8,128)(2,1)S(1)} fusion(bf16[1,7168,512]{2,1,0:T(8,128)(2,1)S(1)} %bitcast.105, f32[512,512]{1,0:T(8,128)S(1)} %fusion.7, bf16[64,8,7168]{2,1,0:T(8,128)(2,1)S(1)} %all_to_all.5), kind=kOutput, calls=%fused_computation.28 | convolution fusion | flops 3759669248 | bytes 16252928 | tf_op jit(solution)/shard_map/dot_general | solution.py:51
  116.3 0.3 collective-permute-start.1
  116.6 3.0 %collective-permute-done = bf16[512,7168]{1,0:T(8,128)(2,1)S(1)} collective-permute-done((bf16[512,7168]{1,0:T(8,128)(2,1)S(1)}, bf16[512,7168]{1,0:T(8,128)(2,1)S(1)}, u32[]{:S(2)}, u32[]{:S(2)}) %collective-permute-start) | collective-permute-done | bytes 7340064 | tf_op jit(solution)/shard_map/ppermute | solution.py:43
  119.6 3.9 %fusion.5 = f32[512,512]{1,0:T(8,128)S(1)} fusion(bf16[512,7168]{1,0:T(8,128)(2,1)S(1)} %collective-permute-done, bf16[1,7168,512]{2,1,0:T(8,128)(2,1)S(1)} %bitcast.103), kind=kOutput, calls=%fused_computation.6 | convolution fusion | flops 3758096384 | bytes 15728640 | tf_op jit(solution)/shard_map/dot_general | solution.py:50
  123.5 4.0 %multiply_convert_fusion = bf16[512,512]{1,0:T(8,128)(2,1)S(1)} fusion(f32[512,512]{1,0:T(8,128)S(1)} %fusion.5, bf16[512,7168]{1,0:T(8,128)(2,1)S(1)} %collective-permute-done, bf16[1,7168,512]{2,1,0:T(8,128)(2,1)S(1)} %bitcast.105), kind=kOutput, calls=%fused_computation.30 | convolution fusion | flops 3759669248 | bytes 16252928 | tf_op jit(solution)/shard_map/dot_general | solution.py:51
  127.6 0.0 copy-start
  127.6 0.1 collective-permute-start.2
  127.7 3.9 %collective-permute-done.1 = bf16[512,512]{1,0:T(8,128)(2,1)S(1)} collective-permute-done((bf16[512,512]{1,0:T(8,128)(2,1)S(1)}, bf16[512,512]{1,0:T(8,128)(2,1)S(1)}, u32[]{:S(2)}, u32[]{:S(2)}) %collective-permute-start.1) | collective-permute-done | bytes 524320 | tf_op jit(solution)/shard_map/ppermute | solution.py:55
  131.5 11.0 %collective-permute-done.2 = bf16[512,512]{1,0:T(8,128)(2,1)S(1)} collective-permute-done((bf16[512,512]{1,0:T(8,128)(2,1)S(1)}, bf16[512,512]{1,0:T(8,128)(2,1)S(1)}, u32[]{:S(2)}, u32[]{:S(2)}) %collective-permute-start.2) | collective-permute-done | bytes 524320 | tf_op jit(solution)/shard_map/ppermute | solution.py:55
  142.6 0.0 copy-start.2
  142.6 0.0 copy-done
  142.6 1.6 %pad_maximum_fusion = bf16[4,512,512]{2,1,0:T(8,128)(2,1)} fusion(bf16[1,512,512]{2,1,0:T(8,128)(2,1)S(1)} %bitcast.100, bf16[1,512,512]{2,1,0:T(8,128)(2,1)S(1)} %bitcast.98, bf16[1,512,512]{2,1,0:T(8,128)(2,1)S(1)} %bitcast.99, bf16[1,512,512]{2,1,0:T(8,128)(2,1)S(1)} %bitcast.97), kind=kLoop, calls=%fused_computation.11 | loop fusion | flops 3145728 | bytes 4194304 | tf_op jit(solution)/shard_map/stack | solution.py:56
  144.2 0.0 copy-done.2
  144.2 1.1 collective-permute-start.3
  145.3 0.0 copy-start.1
  145.3 4.0 %collective-permute-done.3 = bf16[4,512,512]{2,1,0:T(8,128)(2,1)S(1)} collective-permute-done((bf16[4,512,512]{2,1,0:T(8,128)(2,1)}, bf16[4,512,512]{2,1,0:T(8,128)(2,1)S(1)}, u32[]{:S(2)}, u32[]{:S(2)}) %collective-permute-start.3) | collective-permute-done | bytes 2097184 | tf_op jit(solution)/shard_map/ppermute | solution.py:56
  149.2 1.4 broadcast_select_fusion.11
  150.6 0.0 copy-done.1
  150.6 1.3 fusion.16
  151.9 0.2 broadcast_select_fusion.15
  152.1 3.3 %multiply_bitcast_fusion = f32[1,512,2048]{2,1,0:T(8,128)} fusion(f32[512,2048]{1,0:T(8,128)S(1)} %fusion.16, bf16[512,512]{1,0:T(8,128)(2,1)S(1)} %fusion.27, bf16[512,512]{1,0:T(8,128)(2,1)S(1)} %get-tuple-element.8, bf16[512,512]{1,0:T(8,128)(2,1)S(1)} %get-tuple-element.7, bf16[512,512]{1,0:T(8,128)(2,1)S(1)} %get-tuple-element.6, ...), kind=kOutput, calls=%fused_computation.10 | convolution fusion | flops 1084227584 | bytes 11010048 | tf_op jit(solution)/shard_map/rf,rg->fg/dot_general | solution.py:70
  (5 shorter events, 0.1 us)
Async XLA Ops:
  1.7 106.6 %slice-start = ((s8[7340032]{0:T(1024)(128)(4,1)}), s8[4194304]{0:T(1024)(128)(4,1)S(1)}, s32[]{:S(2)}) async-start(s8[7340032]{0:T(1024)(128)(4,1)} %bitcast.102), calls=%async_computation.1 | async-start | bytes 8388608
  6.0 102.3 %slice-start.1 = ((s8[7340032]{0:T(1024)(128)(4,1)}), s8[3145728]{0:T(1024)(128)(4,1)S(1)}, s32[]{:S(2)}) async-start(s8[7340032]{0:T(1024)(128)(4,1)} %bitcast.102), calls=%async_computation.2 | async-start | bytes 6291456
  106.0 6.2 %slice-start.2 = ((s8[7340032]{0:T(1024)(128)(4,1)}), s8[4194304]{0:T(1024)(128)(4,1)S(1)}, s32[]{:S(2)}) async-start(s8[7340032]{0:T(1024)(128)(4,1)} %bitcast.104), calls=%async_computation.3 | async-start | bytes 8388608
  106.0 6.2 %slice-start.3 = ((s8[7340032]{0:T(1024)(128)(4,1)}), s8[3145728]{0:T(1024)(128)(4,1)S(1)}, s32[]{:S(2)}) async-start(s8[7340032]{0:T(1024)(128)(4,1)} %bitcast.104), calls=%async_computation.4 | async-start | bytes 6291456
  106.0 13.6 %collective-permute-start = (bf16[512,7168]{1,0:T(8,128)(2,1)S(1)}, bf16[512,7168]{1,0:T(8,128)(2,1)S(1)}, u32[]{:S(2)}, u32[]{:S(2)}) collective-permute-start(bf16[512,7168]{1,0:T(8,128)(2,1)S(1)} %bitcast.96), channel_id=1, source_target_pairs={{0,1},{1,0},{2,3},{3,2},{4,5},{5,4},{6,7},{7,6},{8,9},{9,8},{10,11... | collective-permute-start | bytes 22020104 | tf_op jit(solution)/shard_map/ppermute | solution.py:43
  116.3 15.2 %collective-permute-start.1 = (bf16[512,512]{1,0:T(8,128)(2,1)S(1)}, bf16[512,512]{1,0:T(8,128)(2,1)S(1)}, u32[]{:S(2)}, u32[]{:S(2)}) collective-permute-start(bf16[512,512]{1,0:T(8,128)(2,1)S(1)} %fusion.27), channel_id=1, source_target_pairs={{0,2},{2,0},{1,3},{3,1},{4,6},{6,4},{5,7},{7,5},{8,10},{10,8},{9,1... | collective-permute-start | bytes 1572872 | tf_op jit(solution)/shard_map/ppermute | solution.py:55
  127.6 15.0 %copy-start = (bf16[512,512]{1,0:T(8,128)(2,1)}, bf16[512,512]{1,0:T(8,128)(2,1)S(1)}, u32[]{:S(2)}) copy-start(bf16[512,512]{1,0:T(8,128)(2,1)S(1)} %multiply_convert_fusion) | copy-start | bytes 1572868
  127.6 15.0 %collective-permute-start.2 = (bf16[512,512]{1,0:T(8,128)(2,1)S(1)}, bf16[512,512]{1,0:T(8,128)(2,1)S(1)}, u32[]{:S(2)}, u32[]{:S(2)}) collective-permute-start(bf16[512,512]{1,0:T(8,128)(2,1)S(1)} %multiply_convert_fusion), channel_id=1, source_target_pairs={{0,2},{2,0},{1,3},{3,1},{4,6},{6,4},{5,7},{7,5},{8,10},{10,8},{9,1... | collective-permute-start | bytes 1572872 | tf_op jit(solution)/shard_map/ppermute | solution.py:55
  142.6 1.6 %copy-start.2 = (bf16[512,512]{1,0:T(8,128)(2,1)}, bf16[512,512]{1,0:T(8,128)(2,1)S(1)}, u32[]{:S(2)}) copy-start(bf16[512,512]{1,0:T(8,128)(2,1)S(1)} %collective-permute-done.2) | copy-start | bytes 1572868
  144.2 5.1 %collective-permute-start.3 = (bf16[4,512,512]{2,1,0:T(8,128)(2,1)}, bf16[4,512,512]{2,1,0:T(8,128)(2,1)S(1)}, u32[]{:S(2)}, u32[]{:S(2)}) collective-permute-start(bf16[4,512,512]{2,1,0:T(8,128)(2,1)} %pad_maximum_fusion), channel_id=1, source_target_pairs={{0,1},{1,0},{2,3},{3,2},{4,5},{5,4},{6,7},{7,6},{8,9},{9,8},{10,11... | collective-permute-start | bytes 6291464 | tf_op jit(solution)/shard_map/ppermute | solution.py:56
  145.3 5.4 %copy-start.1 = (bf16[512,512]{1,0:T(8,128)(2,1)S(1)}, bf16[512,512]{1,0:T(8,128)(2,1)}, u32[]{:S(2)}) copy-start(bf16[512,512]{1,0:T(8,128)(2,1)} %copy-done) | copy-start | bytes 1572868

commit v12 on v7

--- a/solution.py
+++ b/solution.py
@@ -40,16 +40,23 @@
         slot_rows, ("expert", "xh"), split_axis=0, concat_axis=0, tiled=True
     )
     slot_block = slot_block.reshape(expert_count * half_count * capacity, width_model)
-    partner = lax.ppermute(slot_block, "core", [(c, (c + 1) % core_count) for c in range(core_count)])
+    rows_half = slot_block.shape[0] // 2
+    partner = [
+        lax.ppermute(piece, "core", [(c, (c + 1) % core_count) for c in range(core_count)])
+        for piece in (slot_block[:rows_half], slot_block[rows_half:])
+    ]
     factor = 1.0 / (expert_count * capacity)
     swap_half = [(h, (h + 1) % half_count) for h in range(half_count)]
     swap_core = [(c, (c + 1) % core_count) for c in range(core_count)]
     replica_count = half_count * core_count
     own_keys, far_keys = [], []
-    for rows in (slot_block, partner):
-        gate_pre = jnp.dot(rows, w_gate[0], preferred_element_type=jnp.float32)
-        up_pre = jnp.dot(rows, w_up[0], preferred_element_type=jnp.float32)
-        keys = (jax.nn.silu(gate_pre) * up_pre).astype(jnp.bfloat16)
+    for group in ([slot_block], partner):
+        pieces = []
+        for rows in group:
+            gate_pre = jnp.dot(rows, w_gate[0], preferred_element_type=jnp.float32)
+            up_pre = jnp.dot(rows, w_up[0], preferred_element_type=jnp.float32)
+            pieces.append((jax.nn.silu(gate_pre) * up_pre).astype(jnp.bfloat16))
+        keys = jnp.concatenate(pieces, axis=0)
         keys = with_layout_constraint(keys, Layout(major_to_minor=(0, 1)))
         own_keys.append(keys)
         far_keys.append(lax.ppermute(keys, "xh", swap_half))

time: 152 us -> 158 us (1.039)
  matrix products: 24.9 us -> 31.2 us
  waiting for transfers between devices: 20.5 us -> 16 us
  starting transfers between devices: 5.46 us -> 7.7 us
    dot_general x2 -> x3, matrix products: 7.88 us -> 14.1 us  [body(): gate_pre = jnp.dot(rows, w_gate[0], preferred_element_type=jnp.float32)]
    ppermute x1 -> x2, waiting for transfers between devices: 2.3 us -> 0.01 us  [body(): lax.ppermute(piece, 'core', [(c, (c + 1) % core_count) for c in range(cor...]
    ppermute x2, waiting for transfers between devices: 14.2 us -> 12 us  [body(): far_keys.append(lax.ppermute(keys, 'xh', swap_half))]
    dot_general x2 -> x3, matrix products: 8.05 us -> 8.23 us  [body(): up_pre = jnp.dot(rows, w_up[0], preferred_element_type=jnp.float32)]
  transfers between devices with their start and end apart: 4 -> 5, of which waited for: 4 -> 2; matrix products, arithmetic and copies ran while one was open for 10% -> 14% of each run, Pallas kernels for 0% -> 0%
where the time goes in v12:
time: 158 us
  blocking collectives  96.2 us (61%)
  matrix products  31.2 us (20%)
  waiting for transfers between devices  16 us (10%)
  starting transfers between devices  7.7 us (5%)
  other arithmetic  4.31 us (3%)
    all_to_all x1, blocking collectives, body(): lax.all_to_all(slot_rows, ('expert', 'xh'), split_axis=0, concat_axis=0,...  96.2 us
    dot_general x3, matrix products, body(): gate_pre = jnp.dot(rows, w_gate[0], preferred_element_type=jnp.float32)  14.1 us
    ppermute x2, waiting for transfers between devices, body(): far_keys.append(lax.ppermute(keys, 'xh', swap_half))  12 us
    dot_general x3, matrix products, body(): up_pre = jnp.dot(rows, w_up[0], preferred_element_type=jnp.float32)  8.23 us
    dot_general x2, matrix products, body(): jnp.einsum('rf,rg->fg', blocks[i][0], absolute(blocks[i]), preferred_elem...  4.6 us
    dot_general x1, matrix products, body(): jnp.dot(onehot.astype(tokens.dtype), tokens, preferred_element_type=jnp.f...  4.11 us
    ppermute x1, waiting for transfers between devices, body(): relayed = lax.ppermute(jnp.stack(own_keys + far_keys), 'core', swap_core)  3.99 us
    ppermute x2, starting transfers between devices, body(): far_keys.append(lax.ppermute(keys, 'xh', swap_half))  3.32 us
  transfers between devices with their start and end apart: 5, of which 2 were waited for; matrix products, arithmetic and copies ran while one was open for 14% of the time, Pallas kernels for 0%

profile of v12, /device:TPU:1, one launch (start us, length us, event | category | flops | bytes accessed | tf_op | source)
XLA Modules:
  0.0 157.6 jit_solution(15889773652562631003)
XLA Ops:
  0.7 0.7 fusion.40
  1.4 0.2 convolution_convert_fusion.1
  1.6 0.1 fusion.41
  1.7 4.1 %fusion = bf16[64,8,7168]{2,1,0:T(8,128)(2,1)S(1)} fusion(pred[512,256]{1,0:T(8,128)(4,1)S(1)} %bitcast.115, bf16[256,7168]{1,0:T(8,128)(2,1)} %param.5), kind=kOutput, calls=%fused_computation.1 | convolution fusion | flops 1882718208 | bytes 11141120 | tf_op jit(solution)/shard_map/dot_general | solution.py:35
  5.8 96.2 %all_to_all.5 = bf16[64,8,7168]{2,1,0:T(8,128)(2,1)S(1)} all-to-all(bf16[64,8,7168]{2,1,0:T(8,128)(2,1)S(1)} %fusion), channel_id=1, replica_groups=mesh['expert'=32,'xh'=2,'core'=2] {'expert','xh'}, dimensions={0} | all-to-all | bytes 14680064 | tf_op jit(solution)/shard_map/all_to_all | solution.py:39
  102.1 0.5 slice_bitcast_fusion.1
  102.6 2.6 %collective-permute-start = (bf16[256,7168]{1,0:T(8,128)(2,1)S(1)}, bf16[256,7168]{1,0:T(8,128)(2,1)S(1)}, u32[]{:S(2)}, u32[]{:S(2)}) collective-permute-start(bf16[256,7168]{1,0:T(8,128)(2,1)S(1)} %get-tuple-element.5), channel_id=1, source_target_pairs={{0,1},{1,0},{2,3},{3,2},{4,5},{5,4},{6,7},{7,6},{8,9},{9,8},{10,11... | collective-permute-start | bytes 11010056 | tf_op jit(solution)/shard_map/ppermute | solution.py:45
  105.2 0.0 slice-start.2
  105.2 0.0 slice-start.3
  105.2 0.1 collective-permute-start.1
  105.3 6.6 %fusion.11 = f32[512,512]{1,0:T(8,128)S(1)} fusion(bf16[1,7168,512]{2,1,0:T(8,128)(2,1)} %param.8, bf16[64,8,7168]{2,1,0:T(8,128)(2,1)S(1)} %all_to_all.5), kind=kOutput, calls=%fused_computation.12 | convolution fusion | flops 3758096384 | bytes 15728640 | tf_op jit(solution)/shard_map/dot_general | solution.py:56
  111.9 0.0 slice-done.2
  111.9 0.0 slice-done.3
  111.9 4.1 %fusion.35 = bf16[512,512]{1,0:T(8,128)(2,1)S(1)} fusion(bf16[1,7168,512]{2,1,0:T(8,128)(2,1)S(1)} %bitcast.119, bf16[64,8,7168]{2,1,0:T(8,128)(2,1)S(1)} %all_to_all.5, f32[512,512]{1,0:T(8,128)S(1)} %fusion.11), kind=kOutput, calls=%fused_computation.36 | convolution fusion | flops 3759669248 | bytes 16252928 | tf_op jit(solution)/shard_map/dot_general | solution.py:57
  116.0 1.0 collective-permute-start.2
  117.0 0.0 collective-permute-done
  117.0 0.0 slice-start
  117.0 5.4 %fusion.9 = f32[256,512]{1,0:T(8,128)S(1)} fusion(bf16[256,7168]{1,0:T(8,128)(2,1)S(1)} %collective-permute-done, bf16[1,7168,512]{2,1,0:T(8,128)(2,1)} %param.8), kind=kOutput, calls=%fused_computation.10 | convolution fusion | flops 1879048192 | bytes 11534336 | tf_op jit(solution)/shard_map/dot_general | solution.py:56
  122.4 0.0 slice-start.1
  122.4 2.1 %multiply_convert_fusion.1 = bf16[256,512]{1,0:T(8,128)(2,1)S(1)} fusion(f32[256,512]{1,0:T(8,128)S(1)} %fusion.9, bf16[256,7168]{1,0:T(8,128)(2,1)S(1)} %collective-permute-done, bf16[1,7168,512]{2,1,0:T(8,128)(2,1)S(1)} %bitcast.119), kind=kOutput, calls=%fused_computation.44 | convolution fusion | flops 1879834624 | bytes 11796480 | tf_op jit(solution)/shard_map/dot_general | solution.py:57
  124.5 0.0 collective-permute-done.1
  124.5 0.0 slice-done
  124.5 0.0 slice-done.1
  124.5 2.1 %fusion.7 = f32[256,512]{1,0:T(8,128)S(1)} fusion(bf16[256,7168]{1,0:T(8,128)(2,1)S(1)} %collective-permute-done.1, bf16[1,7168,512]{2,1,0:T(8,128)(2,1)S(1)} %bitcast.117), kind=kOutput, calls=%fused_computation.8 | convolution fusion | flops 1879048192 | bytes 11534336 | tf_op jit(solution)/shard_map/dot_general | solution.py:56
  126.7 2.1 %multiply_convert_fusion = bf16[256,512]{1,0:T(8,128)(2,1)S(1)} fusion(f32[256,512]{1,0:T(8,128)S(1)} %fusion.7, bf16[256,7168]{1,0:T(8,128)(2,1)S(1)} %collective-permute-done.1, bf16[1,7168,512]{2,1,0:T(8,128)(2,1)S(1)} %bitcast.119), kind=kOutput, calls=%fused_computation.43 | convolution fusion | flops 1879834624 | bytes 11796480 | tf_op jit(solution)/shard_map/dot_general | solution.py:57
  128.8 0.0 copy-start.1
  128.8 0.1 fusion.46
  128.9 2.3 %collective-permute-start.3 = (bf16[512,512]{1,0:T(8,128)(2,1)S(1)}, bf16[512,512]{1,0:T(8,128)(2,1)S(1)}, u32[]{:S(2)}, u32[]{:S(2)}) collective-permute-start(bf16[512,512]{1,0:T(8,128)(2,1)S(1)} %get-tuple-element.16), channel_id=1, source_target_pairs={{0,2},{2,0},{1,3},{3,1},{4,6},{6,4},{5,7},{7,5},{8,10},{10,8},{9,1... | collective-permute-start | bytes 1572872 | tf_op jit(solution)/shard_map/ppermute | solution.py:62
  131.2 0.0 collective-permute-done.2
  131.2 12.0 %collective-permute-done.3 = bf16[512,512]{1,0:T(8,128)(2,1)S(1)} collective-permute-done((bf16[512,512]{1,0:T(8,128)(2,1)S(1)}, bf16[512,512]{1,0:T(8,128)(2,1)S(1)}, u32[]{:S(2)}, u32[]{:S(2)}) %collective-permute-start.3) | collective-permute-done | bytes 524320 | tf_op jit(solution)/shard_map/ppermute | solution.py:62
  143.2 0.0 copy-start
  143.2 0.8 copy-done
  144.0 1.6 %pad_maximum_fusion = bf16[4,512,512]{2,1,0:T(8,128)(2,1)} fusion(bf16[1,512,512]{2,1,0:T(8,128)(2,1)S(1)} %bitcast.114, bf16[1,512,512]{2,1,0:T(8,128)(2,1)S(1)} %bitcast.113, bf16[1,512,512]{2,1,0:T(8,128)(2,1)S(1)} %get-tuple-element.15, bf16[1,512,512]{2,1,0:T(8,128)(2,1)S(1)} %bitcast.112), kind=kLoop, calls=%fused_computation.19 | loop fusion | flops 3145728 | bytes 4194304 | tf_op jit(solution)/shard_map/stack | solution.py:63
  145.5 0.0 copy-done.1
  145.5 1.6 %collective-permute-start.4 = (bf16[4,512,512]{2,1,0:T(8,128)(2,1)}, bf16[4,512,512]{2,1,0:T(8,128)(2,1)S(1)}, u32[]{:S(2)}, u32[]{:S(2)}) collective-permute-start(bf16[4,512,512]{2,1,0:T(8,128)(2,1)} %pad_maximum_fusion), channel_id=1, source_target_pairs={{0,1},{1,0},{2,3},{3,2},{4,5},{5,4},{6,7},{7,6},{8,9},{9,8},{10,11... | collective-permute-start | bytes 6291464 | tf_op jit(solution)/shard_map/ppermute | solution.py:63
  147.2 0.0 copy-start.2
  147.2 4.0 %collective-permute-done.4 = bf16[4,512,512]{2,1,0:T(8,128)(2,1)S(1)} collective-permute-done((bf16[4,512,512]{2,1,0:T(8,128)(2,1)}, bf16[4,512,512]{2,1,0:T(8,128)(2,1)S(1)}, u32[]{:S(2)}, u32[]{:S(2)}) %collective-permute-start.4) | collective-permute-done | bytes 2097184 | tf_op jit(solution)/shard_map/ppermute | solution.py:63
  151.2 1.6 %broadcast_select_fusion.11 = (bf16[512,512]{1,0:T(8,128)(2,1)S(1)}, bf16[512,512]{1,0:T(8,128)(2,1)S(1)}, bf16[512,512]{1,0:T(8,128)(2,1)S(1)}, bf16[512,512]{1,0:T(8,128)(2,1)S(1)}) fusion(pred[]{:T(512)S(6)} %eq.42, bf16[512,512]{1,0:T(8,128)(2,1)} %copy-done, bf16[4,512,512]{2,1,0:T(8,128)(2,1)S(1)} %collective-permute-done.4, pred[]{:T(512)S(6)} %eq.43, ...), kind=kLoop, calls=%fused_computation.56 | loop fusion | flops 3145728 | bytes 4194306 | tf_op jit(solution)/shard_map/jit(_where)/select_n | solution.py:72
  152.8 0.0 copy-done.2
  152.8 1.3 fusion.22
  154.1 0.2 broadcast_select_fusion.15
  154.3 3.3 %multiply_bitcast_fusion = f32[1,512,2048]{2,1,0:T(8,128)} fusion(f32[512,2048]{1,0:T(8,128)S(1)} %fusion.22, bf16[512,512]{1,0:T(8,128)(2,1)S(1)} %fusion.35, bf16[512,512]{1,0:T(8,128)(2,1)S(1)} %get-tuple-element.10, bf16[512,512]{1,0:T(8,128)(2,1)S(1)} %get-tuple-element.9, bf16[512,512]{1,0:T(8,128)(2,1)S(1)} %get-tuple-element.8, ...), kind=kOutput, calls=%fused_computation.16 | convolution fusion | flops 1084227584 | bytes 11010048 | tf_op jit(solution)/shard_map/rf,rg->fg/dot_general | solution.py:77
  (5 shorter events, 0.1 us)
Async XLA Ops:
  102.6 14.5 %collective-permute-start = (bf16[256,7168]{1,0:T(8,128)(2,1)S(1)}, bf16[256,7168]{1,0:T(8,128)(2,1)S(1)}, u32[]{:S(2)}, u32[]{:S(2)}) collective-permute-start(bf16[256,7168]{1,0:T(8,128)(2,1)S(1)} %get-tuple-element.5), channel_id=1, source_target_pairs={{0,1},{1,0},{2,3},{3,2},{4,5},{5,4},{6,7},{7,6},{8,9},{9,8},{10,11... | collective-permute-start | bytes 11010056 | tf_op jit(solution)/shard_map/ppermute | solution.py:45
  105.2 6.7 %slice-start.2 = ((s8[7340032]{0:T(1024)(128)(4,1)}), s8[4194304]{0:T(1024)(128)(4,1)S(1)}, s32[]{:S(2)}) async-start(s8[7340032]{0:T(1024)(128)(4,1)} %bitcast.118), calls=%async_computation.3 | async-start | bytes 8388608
  105.2 6.7 %slice-start.3 = ((s8[7340032]{0:T(1024)(128)(4,1)}), s8[3145728]{0:T(1024)(128)(4,1)S(1)}, s32[]{:S(2)}) async-start(s8[7340032]{0:T(1024)(128)(4,1)} %bitcast.118), calls=%async_computation.4 | async-start | bytes 6291456
  105.2 19.3 %collective-permute-start.1 = (bf16[256,7168]{1,0:T(8,128)(2,1)S(1)}, bf16[256,7168]{1,0:T(8,128)(2,1)S(1)}, u32[]{:S(2)}, u32[]{:S(2)}) collective-permute-start(bf16[256,7168]{1,0:T(8,128)(2,1)S(1)} %get-tuple-element.6), channel_id=1, source_target_pairs={{0,1},{1,0},{2,3},{3,2},{4,5},{5,4},{6,7},{7,6},{8,9},{9,8},{10,11... | collective-permute-start | bytes 11010056 | tf_op jit(solution)/shard_map/ppermute | solution.py:45
  116.0 15.2 %collective-permute-start.2 = (bf16[512,512]{1,0:T(8,128)(2,1)S(1)}, bf16[512,512]{1,0:T(8,128)(2,1)S(1)}, u32[]{:S(2)}, u32[]{:S(2)}) collective-permute-start(bf16[512,512]{1,0:T(8,128)(2,1)S(1)} %fusion.35), channel_id=1, source_target_pairs={{0,2},{2,0},{1,3},{3,1},{4,6},{6,4},{5,7},{7,5},{8,10},{10,8},{9,1... | collective-permute-start | bytes 1572872 | tf_op jit(solution)/shard_map/ppermute | solution.py:62
  117.0 7.5 %slice-start = ((s8[7340032]{0:T(1024)(128)(4,1)}), s8[4194304]{0:T(1024)(128)(4,1)S(1)}, s32[]{:S(2)}) async-start(s8[7340032]{0:T(1024)(128)(4,1)} %bitcast.116), calls=%async_computation.1 | async-start | bytes 8388608
  122.4 2.1 %slice-start.1 = ((s8[7340032]{0:T(1024)(128)(4,1)}), s8[3145728]{0:T(1024)(128)(4,1)S(1)}, s32[]{:S(2)}) async-start(s8[7340032]{0:T(1024)(128)(4,1)} %bitcast.116), calls=%async_computation.2 | async-start | bytes 6291456
  128.8 16.8 %copy-start.1 = (bf16[256,512]{1,0:T(8,128)(2,1)}, bf16[256,512]{1,0:T(8,128)(2,1)S(1)}, u32[]{:S(2)}) copy-start(bf16[256,512]{1,0:T(8,128)(2,1)S(1)} %multiply_convert_fusion) | copy-start | bytes 786436
  128.9 14.3 %collective-permute-start.3 = (bf16[512,512]{1,0:T(8,128)(2,1)S(1)}, bf16[512,512]{1,0:T(8,128)(2,1)S(1)}, u32[]{:S(2)}, u32[]{:S(2)}) collective-permute-start(bf16[512,512]{1,0:T(8,128)(2,1)S(1)} %get-tuple-element.16), channel_id=1, source_target_pairs={{0,2},{2,0},{1,3},{3,1},{4,6},{6,4},{5,7},{7,5},{8,10},{10,8},{9,1... | collective-permute-start | bytes 1572872 | tf_op jit(solution)/shard_map/ppermute | solution.py:62
  143.2 0.8 copy-start
  145.5 5.6 %collective-permute-start.4 = (bf16[4,512,512]{2,1,0:T(8,128)(2,1)}, bf16[4,512,512]{2,1,0:T(8,128)(2,1)S(1)}, u32[]{:S(2)}, u32[]{:S(2)}) collective-permute-start(bf16[4,512,512]{2,1,0:T(8,128)(2,1)} %pad_maximum_fusion), channel_id=1, source_target_pairs={{0,1},{1,0},{2,3},{3,2},{4,5},{5,4},{6,7},{7,6},{8,9},{9,8},{10,11... | collective-permute-start | bytes 6291464 | tf_op jit(solution)/shard_map/ppermute | solution.py:63
  147.2 5.6 %copy-start.2 = (bf16[256,512]{1,0:T(8,128)(2,1)S(1)}, bf16[256,512]{1,0:T(8,128)(2,1)}, u32[]{:S(2)}) copy-start(bf16[256,512]{1,0:T(8,128)(2,1)} %copy-done.1) | copy-start | bytes 786436

commit v13 on v7

--- a/solution.py
+++ b/solution.py
@@ -53,9 +53,11 @@
         keys = with_layout_constraint(keys, Layout(major_to_minor=(0, 1)))
         own_keys.append(keys)
         far_keys.append(lax.ppermute(keys, "xh", swap_half))
-    relayed = lax.ppermute(jnp.stack(own_keys + far_keys), "core", swap_core)
+    relayed = [
+        lax.ppermute(jnp.stack([own_keys[i], far_keys[i]]), "core", swap_core) for i in range(2)
+    ]
     blocks = [
-        [own_keys[i], relayed[1 - i], far_keys[i], relayed[3 - i]] for i in range(2)
+        [own_keys[i], relayed[1 - i][0], far_keys[i], relayed[1 - i][1]] for i in range(2)
     ]
     on_second_core = lax.axis_index("core") == 1
     on_second_half = lax.axis_index("xh") == 1

time: 152 us -> 168 us (1.11)
  waiting for transfers between devices: 20.5 us -> 29.6 us
  matrix products: 24.9 us -> 30.5 us
    ppermute x2, waiting for transfers between devices: 14.2 us -> 28.4 us  [body(): far_keys.append(lax.ppermute(keys, 'xh', swap_half))]
    dot_general x2, matrix products: 8.05 us -> 11.2 us  [body(): up_pre = jnp.dot(rows, w_up[0], preferred_element_type=jnp.float32)]
    ppermute x1 -> x2, waiting for transfers between devices: 3.99 us -> 1.17 us  [body(): lax.ppermute(jnp.stack([own_keys[i], far_keys[i]]), 'core', swap_core)]
    dot_general x2, matrix products: 7.88 us -> 10.3 us  [body(): gate_pre = jnp.dot(rows, w_gate[0], preferred_element_type=jnp.float32)]
    ppermute x1, waiting for transfers between devices: 2.3 us -> 0.01 us  [body(): lax.ppermute(slot_block, 'core', [(c, (c + 1) % core_count) for c in rang...]
  transfers between devices with their start and end apart: 4 -> 5, of which waited for: 4 -> 3; matrix products, arithmetic and copies ran while one was open for 10% -> 15% of each run, Pallas kernels for 0% -> 0%
where the time goes in v13:
time: 168 us
  blocking collectives  96.5 us (57%)
  matrix products  30.5 us (18%)
  waiting for transfers between devices  29.6 us (18%)
  starting transfers between devices  5.97 us (4%)
  other arithmetic  4.51 us (3%)
    all_to_all x1, blocking collectives, body(): lax.all_to_all(slot_rows, ('expert', 'xh'), split_axis=0, concat_axis=0,...  96.5 us
    ppermute x2, waiting for transfers between devices, body(): far_keys.append(lax.ppermute(keys, 'xh', swap_half))  28.4 us
    dot_general x2, matrix products, body(): up_pre = jnp.dot(rows, w_up[0], preferred_element_type=jnp.float32)  11.2 us
    dot_general x2, matrix products, body(): gate_pre = jnp.dot(rows, w_gate[0], preferred_element_type=jnp.float32)  10.3 us
    dot_general x2, matrix products, body(): jnp.einsum('rf,rg->fg', blocks[i][0], absolute(blocks[i]), preferred_elem...  4.57 us
    dot_general x1, matrix products, body(): jnp.dot(onehot.astype(tokens.dtype), tokens, preferred_element_type=jnp.f...  4.26 us
  transfers between devices with their start and end apart: 5, of which 3 were waited for; matrix products, arithmetic and copies ran while one was open for 15% of the time, Pallas kernels for 0%

profile of v13, /device:TPU:1, one launch (start us, length us, event | category | flops | bytes accessed | tf_op | source)
XLA Modules:
  0.0 167.9 jit_solution(649703403642552589)
XLA Ops:
  0.0 0.7 fusion.30
  1.4 0.2 convolution_convert_fusion.1
  1.6 0.1 fusion.31
  1.7 0.0 slice-start
  1.7 4.3 %fusion = bf16[64,8,7168]{2,1,0:T(8,128)(2,1)S(1)} fusion(pred[512,256]{1,0:T(8,128)(4,1)S(1)} %bitcast.101, bf16[256,7168]{1,0:T(8,128)(2,1)} %param.5), kind=kOutput, calls=%fused_computation.1 | convolution fusion | flops 1882718208 | bytes 11141120 | tf_op jit(solution)/shard_map/dot_general | solution.py:35
  6.0 0.0 slice-start.1
  6.0 96.5 %all_to_all.5 = bf16[64,8,7168]{2,1,0:T(8,128)(2,1)S(1)} all-to-all(bf16[64,8,7168]{2,1,0:T(8,128)(2,1)S(1)} %fusion), channel_id=1, replica_groups=mesh['expert'=32,'xh'=2,'core'=2] {'expert','xh'}, dimensions={0} | all-to-all | bytes 14680064 | tf_op jit(solution)/shard_map/all_to_all | solution.py:39
  102.5 0.0 slice-start.2
  102.5 0.0 slice-start.3
  102.5 2.6 %collective-permute-start = (bf16[512,7168]{1,0:T(8,128)(2,1)S(1)}, bf16[512,7168]{1,0:T(8,128)(2,1)}, u32[]{:S(2)}, u32[]{:S(2)}) collective-permute-start(bf16[512,7168]{1,0:T(8,128)(2,1)S(1)} %bitcast.96), channel_id=1, source_target_pairs={{0,1},{1,0},{2,3},{3,2},{4,5},{5,4},{6,7},{7,6},{8,9},{9,8},{10,11... | collective-permute-start | bytes 22020104 | tf_op jit(solution)/shard_map/ppermute | solution.py:43
  105.1 0.0 slice-done
  105.1 0.0 slice-done.1
  105.1 3.9 %fusion.7 = f32[512,512]{1,0:T(8,128)S(1)} fusion(bf16[1,7168,512]{2,1,0:T(8,128)(2,1)S(1)} %bitcast.103, bf16[64,8,7168]{2,1,0:T(8,128)(2,1)S(1)} %all_to_all.5), kind=kOutput, calls=%fused_computation.8 | convolution fusion | flops 3758096384 | bytes 15728640 | tf_op jit(solution)/shard_map/dot_general | solution.py:50
  109.0 0.0 slice-done.2
  109.0 0.0 slice-done.3
  109.1 4.0 %fusion.27 = bf16[512,512]{1,0:T(8,128)(2,1)S(1)} fusion(bf16[1,7168,512]{2,1,0:T(8,128)(2,1)S(1)} %bitcast.105, f32[512,512]{1,0:T(8,128)S(1)} %fusion.7, bf16[64,8,7168]{2,1,0:T(8,128)(2,1)S(1)} %all_to_all.5), kind=kOutput, calls=%fused_computation.27 | convolution fusion | flops 3759669248 | bytes 16252928 | tf_op jit(solution)/shard_map/dot_general | solution.py:51
  113.1 0.8 collective-permute-start.3
  113.9 14.2 %collective-permute-done.3 = bf16[512,512]{1,0:T(8,128)(2,1)S(1)} collective-permute-done((bf16[512,512]{1,0:T(8,128)(2,1)S(1)}, bf16[512,512]{1,0:T(8,128)(2,1)S(1)}, u32[]{:S(2)}, u32[]{:S(2)}) %collective-permute-start.3) | collective-permute-done | bytes 524320 | tf_op jit(solution)/shard_map/ppermute | solution.py:55
  128.1 1.1 pad_maximum_fusion.1
  129.2 0.9 collective-permute-start.4
  130.1 0.0 collective-permute-done
  130.1 6.4 %fusion.5 = f32[512,512]{1,0:T(8,128)S(1)} fusion(bf16[512,7168]{1,0:T(8,128)(2,1)} %collective-permute-done, bf16[1,7168,512]{2,1,0:T(8,128)(2,1)S(1)} %bitcast.103), kind=kOutput, calls=%fused_computation.6 | convolution fusion | flops 3758096384 | bytes 15728640 | tf_op jit(solution)/shard_map/dot_general | solution.py:50
  136.5 7.2 %multiply_convert_fusion = bf16[512,512]{1,0:T(8,128)(2,1)S(1)} fusion(f32[512,512]{1,0:T(8,128)S(1)} %fusion.5, bf16[512,7168]{1,0:T(8,128)(2,1)} %collective-permute-done, bf16[1,7168,512]{2,1,0:T(8,128)(2,1)S(1)} %bitcast.105), kind=kOutput, calls=%fused_computation.31 | convolution fusion | flops 3759669248 | bytes 16252928 | tf_op jit(solution)/shard_map/dot_general | solution.py:51
  143.6 0.8 collective-permute-start.1
  144.5 14.2 %collective-permute-done.1 = bf16[512,512]{1,0:T(8,128)(2,1)S(1)} collective-permute-done((bf16[512,512]{1,0:T(8,128)(2,1)S(1)}, bf16[512,512]{1,0:T(8,128)(2,1)S(1)}, u32[]{:S(2)}, u32[]{:S(2)}) %collective-permute-start.1) | collective-permute-done | bytes 524320 | tf_op jit(solution)/shard_map/ppermute | solution.py:55
  158.7 1.1 pad_maximum_fusion
  159.8 0.9 collective-permute-start.2
  160.6 0.0 collective-permute-done.4
  160.6 0.2 broadcast_select_fusion.11
  160.8 1.3 fusion.16
  162.1 1.2 collective-permute-done.2
  163.3 1.4 broadcast_select_fusion.15
  164.6 3.3 %multiply_bitcast_fusion = f32[1,512,2048]{2,1,0:T(8,128)} fusion(f32[512,2048]{1,0:T(8,128)S(1)} %fusion.16, bf16[512,512]{1,0:T(8,128)(2,1)S(1)} %fusion.27, bf16[512,512]{1,0:T(8,128)(2,1)S(1)} %get-tuple-element.8, bf16[512,512]{1,0:T(8,128)(2,1)S(1)} %get-tuple-element.7, bf16[512,512]{1,0:T(8,128)(2,1)S(1)} %get-tuple-element.6, ...), kind=kOutput, calls=%fused_computation.10 | convolution fusion | flops 1084227584 | bytes 11010048 | tf_op jit(solution)/shard_map/rf,rg->fg/dot_general | solution.py:72
  (5 shorter events, 0.1 us)
Async XLA Ops:
  1.7 103.4 %slice-start = ((s8[7340032]{0:T(1024)(128)(4,1)}), s8[4194304]{0:T(1024)(128)(4,1)S(1)}, s32[]{:S(2)}) async-start(s8[7340032]{0:T(1024)(128)(4,1)} %bitcast.102), calls=%async_computation.1 | async-start | bytes 8388608
  6.0 99.1 %slice-start.1 = ((s8[7340032]{0:T(1024)(128)(4,1)}), s8[3145728]{0:T(1024)(128)(4,1)S(1)}, s32[]{:S(2)}) async-start(s8[7340032]{0:T(1024)(128)(4,1)} %bitcast.102), calls=%async_computation.2 | async-start | bytes 6291456
  102.5 6.5 %slice-start.2 = ((s8[7340032]{0:T(1024)(128)(4,1)}), s8[4194304]{0:T(1024)(128)(4,1)S(1)}, s32[]{:S(2)}) async-start(s8[7340032]{0:T(1024)(128)(4,1)} %bitcast.104), calls=%async_computation.3 | async-start | bytes 8388608
  102.5 6.5 %slice-start.3 = ((s8[7340032]{0:T(1024)(128)(4,1)}), s8[3145728]{0:T(1024)(128)(4,1)S(1)}, s32[]{:S(2)}) async-start(s8[7340032]{0:T(1024)(128)(4,1)} %bitcast.104), calls=%async_computation.4 | async-start | bytes 6291456
  102.5 27.6 %collective-permute-start = (bf16[512,7168]{1,0:T(8,128)(2,1)S(1)}, bf16[512,7168]{1,0:T(8,128)(2,1)}, u32[]{:S(2)}, u32[]{:S(2)}) collective-permute-start(bf16[512,7168]{1,0:T(8,128)(2,1)S(1)} %bitcast.96), channel_id=1, source_target_pairs={{0,1},{1,0},{2,3},{3,2},{4,5},{5,4},{6,7},{7,6},{8,9},{9,8},{10,11... | collective-permute-start | bytes 22020104 | tf_op jit(solution)/shard_map/ppermute | solution.py:43
  113.1 15.0 %collective-permute-start.3 = (bf16[512,512]{1,0:T(8,128)(2,1)S(1)}, bf16[512,512]{1,0:T(8,128)(2,1)S(1)}, u32[]{:S(2)}, u32[]{:S(2)}) collective-permute-start(bf16[512,512]{1,0:T(8,128)(2,1)S(1)} %fusion.27), channel_id=1, source_target_pairs={{0,2},{2,0},{1,3},{3,1},{4,6},{6,4},{5,7},{7,5},{8,10},{10,8},{9,1... | collective-permute-start | bytes 1572872 | tf_op jit(solution)/shard_map/ppermute | solution.py:55
  129.2 31.4 %collective-permute-start.4 = (bf16[2,512,512]{2,1,0:T(8,128)(2,1)}, bf16[2,512,512]{2,1,0:T(8,128)(2,1)S(1)}, u32[]{:S(2)}, u32[]{:S(2)}) collective-permute-start(bf16[2,512,512]{2,1,0:T(8,128)(2,1)} %pad_maximum_fusion.1), channel_id=1, source_target_pairs={{0,1},{1,0},{2,3},{3,2},{4,5},{5,4},{6,7},{7,6},{8,9},{9,8},{10,11... | collective-permute-start | bytes 3145736 | tf_op jit(solution)/shard_map/ppermute | solution.py:57
  143.6 15.1 %collective-permute-start.1 = (bf16[512,512]{1,0:T(8,128)(2,1)S(1)}, bf16[512,512]{1,0:T(8,128)(2,1)S(1)}, u32[]{:S(2)}, u32[]{:S(2)}) collective-permute-start(bf16[512,512]{1,0:T(8,128)(2,1)S(1)} %multiply_convert_fusion), channel_id=1, source_target_pairs={{0,2},{2,0},{1,3},{3,1},{4,6},{6,4},{5,7},{7,5},{8,10},{10,8},{9,1... | collective-permute-start | bytes 1572872 | tf_op jit(solution)/shard_map/ppermute | solution.py:55
  159.8 3.5 %collective-permute-start.2 = (bf16[2,512,512]{2,1,0:T(8,128)(2,1)}, bf16[2,512,512]{2,1,0:T(8,128)(2,1)}, u32[]{:S(2)}, u32[]{:S(2)}) collective-permute-start(bf16[2,512,512]{2,1,0:T(8,128)(2,1)} %pad_maximum_fusion), channel_id=1, source_target_pairs={{0,1},{1,0},{2,3},{3,2},{4,5},{5,4},{6,7},{7,6},{8,9},{9,8},{10,11... | collective-permute-start | bytes 3145736 | tf_op jit(solution)/shard_map/ppermute | solution.py:57

commit v14 on v7

--- a/solution.py
+++ b/solution.py
@@ -29,13 +29,15 @@
     slot_total, width_model = tokens.shape
     capacity = slot_total * TOP // N_ROUTED
     onehot = slot_onehot(routes, counts[0], expert_count, capacity)
-    onehot = jnp.broadcast_to(
-        onehot[:, None], (expert_count, half_count, capacity, slot_total)
-    ).reshape(expert_count * half_count * capacity, slot_total)
     slot_rows = jnp.dot(
-        onehot.astype(tokens.dtype), tokens, preferred_element_type=jnp.float32
+        onehot.reshape(expert_count * capacity, slot_total).astype(tokens.dtype),
+        tokens,
+        preferred_element_type=jnp.float32,
     ).astype(tokens.dtype)
-    slot_rows = slot_rows.reshape(expert_count * half_count, capacity, width_model)
+    slot_rows = jnp.broadcast_to(
+        slot_rows.reshape(expert_count, 1, capacity, width_model),
+        (expert_count, half_count, capacity, width_model),
+    ).reshape(expert_count * half_count, capacity, width_model)
     slot_block = lax.all_to_all(
         slot_rows, ("expert", "xh"), split_axis=0, concat_axis=0, tiled=True
     )

time: 152 us -> 155 us (1.020)
  matrix products: 24.9 us -> 26.8 us
    dot_general x2, matrix products: 7.88 us -> 10.8 us  [body(): gate_pre = jnp.dot(rows, w_gate[0], preferred_element_type=jnp.float32)]
    ppermute x1, waiting for transfers between devices: 2.3 us -> 0.01 us  [body(): lax.ppermute(slot_block, 'core', [(c, (c + 1) % core_count) for c in rang...]
  transfers between devices with their start and end apart: 4 -> 4, of which waited for: 4 -> 3; matrix products, arithmetic and copies ran while one was open for 10% -> 12% of each run, Pallas kernels for 0% -> 0%
where the time goes in v14:
time: 155 us
  blocking collectives  96.5 us (62%)
  matrix products  26.8 us (17%)
  waiting for transfers between devices  19.5 us (13%)
  starting transfers between devices  6.43 us (4%)
  other arithmetic  3.88 us (3%)
    all_to_all x1, blocking collectives, body(): lax.all_to_all(slot_rows, ('expert', 'xh'), split_axis=0, concat_axis=0,...  96.5 us
    ppermute x2, waiting for transfers between devices, body(): far_keys.append(lax.ppermute(keys, 'xh', swap_half))  15.5 us
    dot_general x2, matrix products, body(): gate_pre = jnp.dot(rows, w_gate[0], preferred_element_type=jnp.float32)  10.8 us
    dot_general x2, matrix products, body(): up_pre = jnp.dot(rows, w_up[0], preferred_element_type=jnp.float32)  8.05 us
    dot_general x2, matrix products, body(): jnp.einsum('rf,rg->fg', blocks[i][0], absolute(blocks[i]), preferred_elem...  4.57 us
    ppermute x1, waiting for transfers between devices, body(): relayed = lax.ppermute(jnp.stack(own_keys + far_keys), 'core', swap_core)  3.99 us
    ppermute x2, starting transfers between devices, body(): far_keys.append(lax.ppermute(keys, 'xh', swap_half))  3.31 us
    dot_general x1, matrix products, body(): jnp.dot(onehot.reshape(expert_count * capacity, slot_total).astype(tokens...  3.19 us
  transfers between devices with their start and end apart: 4, of which 3 were waited for; matrix products, arithmetic and copies ran while one was open for 12% of the time, Pallas kernels for 0%

profile of v14, /device:TPU:1, one launch (start us, length us, event | category | flops | bytes accessed | tf_op | source)
XLA Modules:
  0.0 154.9 jit_solution(4610529588077635641)
XLA Ops:
  0.7 0.7 fusion.30
  1.4 0.2 convolution_convert_fusion.1
  1.6 0.1 eq.45
  1.7 3.2 %fusion = bf16[32,8,7168]{2,1,0:T(8,128)(2,1)S(1)} fusion(bf16[256,7168]{1,0:T(8,128)(2,1)} %param.5, s32[256]{0:T(256)S(1)} %eq.45, s32[32,256]{1,0:T(8,128)S(1)} %convolution_convert_fusion.1, pred[32,256]{1,0:T(8,128)(4,1)S(1)} %and_bitcast_fusion), kind=kOutput, calls=%fused_computation.1 | convolution fusion | flops 941490176 | bytes 7382016 | tf_op jit(solution)/shard_map/dot_general | solution.py:32
  4.9 0.9 broadcast_in_dim.14
  5.8 0.0 slice-start
  5.8 96.5 %all_to_all.5 = bf16[64,8,7168]{2,1,0:T(8,128)(2,1)S(1)} all-to-all(bf16[64,8,7168]{2,1,0:T(8,128)(2,1)S(1)} %bitcast.105), channel_id=1, replica_groups=mesh['expert'=32,'xh'=2,'core'=2] {'expert','xh'}, dimensions={0} | all-to-all | bytes 14680064 | tf_op jit(solution)/shard_map/all_to_all | solution.py:41
  102.3 0.0 slice-start.2
  102.3 0.0 slice-start.3
  102.3 0.0 slice-start.1
  102.3 2.6 %collective-permute-start = (bf16[512,7168]{1,0:T(8,128)(2,1)S(1)}, bf16[512,7168]{1,0:T(8,128)(2,1)S(1)}, u32[]{:S(2)}, u32[]{:S(2)}) collective-permute-start(bf16[512,7168]{1,0:T(8,128)(2,1)S(1)} %bitcast.106), channel_id=1, source_target_pairs={{0,1},{1,0},{2,3},{3,2},{4,5},{5,4},{6,7},{7,6},{8,9},{9,8},{10,11... | collective-permute-start | bytes 22020104 | tf_op jit(solution)/shard_map/ppermute | solution.py:45
  104.9 6.8 %fusion.7 = f32[512,512]{1,0:T(8,128)S(1)} fusion(bf16[1,7168,512]{2,1,0:T(8,128)(2,1)} %param.8, bf16[64,8,7168]{2,1,0:T(8,128)(2,1)S(1)} %all_to_all.5), kind=kOutput, calls=%fused_computation.8 | convolution fusion | flops 3758096384 | bytes 15728640 | tf_op jit(solution)/shard_map/dot_general | solution.py:52
  111.7 0.0 slice-done.2
  111.7 0.0 slice-done.3
  111.8 4.0 %fusion.27 = bf16[512,512]{1,0:T(8,128)(2,1)S(1)} fusion(bf16[1,7168,512]{2,1,0:T(8,128)(2,1)S(1)} %bitcast.114, f32[512,512]{1,0:T(8,128)S(1)} %fusion.7, bf16[64,8,7168]{2,1,0:T(8,128)(2,1)S(1)} %all_to_all.5), kind=kOutput, calls=%fused_computation.28 | convolution fusion | flops 3759669248 | bytes 16252928 | tf_op jit(solution)/shard_map/dot_general | solution.py:53
  115.8 1.1 collective-permute-start.1
  116.9 0.0 collective-permute-done
  116.9 0.0 slice-done
  116.9 0.0 slice-done.1
  116.9 3.9 %fusion.5 = f32[512,512]{1,0:T(8,128)S(1)} fusion(bf16[512,7168]{1,0:T(8,128)(2,1)S(1)} %collective-permute-done, bf16[1,7168,512]{2,1,0:T(8,128)(2,1)S(1)} %bitcast.112), kind=kOutput, calls=%fused_computation.6 | convolution fusion | flops 3758096384 | bytes 15728640 | tf_op jit(solution)/shard_map/dot_general | solution.py:52
  120.9 4.0 %multiply_convert_fusion = bf16[512,512]{1,0:T(8,128)(2,1)S(1)} fusion(f32[512,512]{1,0:T(8,128)S(1)} %fusion.5, bf16[512,7168]{1,0:T(8,128)(2,1)S(1)} %collective-permute-done, bf16[1,7168,512]{2,1,0:T(8,128)(2,1)S(1)} %bitcast.114), kind=kOutput, calls=%fused_computation.30 | convolution fusion | flops 3759669248 | bytes 16252928 | tf_op jit(solution)/shard_map/dot_general | solution.py:53
  124.9 0.0 copy-start
  124.9 2.2 %collective-permute-start.2 = (bf16[512,512]{1,0:T(8,128)(2,1)S(1)}, bf16[512,512]{1,0:T(8,128)(2,1)S(1)}, u32[]{:S(2)}, u32[]{:S(2)}) collective-permute-start(bf16[512,512]{1,0:T(8,128)(2,1)S(1)} %multiply_convert_fusion), channel_id=1, source_target_pairs={{0,2},{2,0},{1,3},{3,1},{4,6},{6,4},{5,7},{7,5},{8,10},{10,8},{9,1... | collective-permute-start | bytes 1572872 | tf_op jit(solution)/shard_map/ppermute | solution.py:57
  127.1 4.2 %collective-permute-done.1 = bf16[512,512]{1,0:T(8,128)(2,1)S(1)} collective-permute-done((bf16[512,512]{1,0:T(8,128)(2,1)S(1)}, bf16[512,512]{1,0:T(8,128)(2,1)S(1)}, u32[]{:S(2)}, u32[]{:S(2)}) %collective-permute-start.1) | collective-permute-done | bytes 524320 | tf_op jit(solution)/shard_map/ppermute | solution.py:57
  131.4 11.2 %collective-permute-done.2 = bf16[512,512]{1,0:T(8,128)(2,1)S(1)} collective-permute-done((bf16[512,512]{1,0:T(8,128)(2,1)S(1)}, bf16[512,512]{1,0:T(8,128)(2,1)S(1)}, u32[]{:S(2)}, u32[]{:S(2)}) %collective-permute-start.2) | collective-permute-done | bytes 524320 | tf_op jit(solution)/shard_map/ppermute | solution.py:57
  142.6 0.0 copy-start.2
  142.6 0.0 copy-done
  142.6 1.6 %pad_maximum_fusion = bf16[4,512,512]{2,1,0:T(8,128)(2,1)} fusion(bf16[1,512,512]{2,1,0:T(8,128)(2,1)S(1)} %bitcast.110, bf16[1,512,512]{2,1,0:T(8,128)(2,1)S(1)} %bitcast.108, bf16[1,512,512]{2,1,0:T(8,128)(2,1)S(1)} %bitcast.109, bf16[1,512,512]{2,1,0:T(8,128)(2,1)S(1)} %bitcast.107), kind=kLoop, calls=%fused_computation.11 | loop fusion | flops 3145728 | bytes 4194304 | tf_op jit(solution)/shard_map/stack | solution.py:58
  144.2 0.0 copy-done.2
  144.2 0.5 collective-permute-start.3
  144.7 0.0 copy-start.1
  144.7 4.0 %collective-permute-done.3 = bf16[4,512,512]{2,1,0:T(8,128)(2,1)S(1)} collective-permute-done((bf16[4,512,512]{2,1,0:T(8,128)(2,1)}, bf16[4,512,512]{2,1,0:T(8,128)(2,1)S(1)}, u32[]{:S(2)}, u32[]{:S(2)}) %collective-permute-start.3) | collective-permute-done | bytes 2097184 | tf_op jit(solution)/shard_map/ppermute | solution.py:58
  148.7 1.4 broadcast_select_fusion.11
  150.1 0.0 copy-done.1
  150.1 1.3 fusion.16
  151.4 0.2 broadcast_select_fusion.15
  151.6 3.3 %multiply_bitcast_fusion = f32[1,512,2048]{2,1,0:T(8,128)} fusion(f32[512,2048]{1,0:T(8,128)S(1)} %fusion.16, bf16[512,512]{1,0:T(8,128)(2,1)S(1)} %fusion.27, bf16[512,512]{1,0:T(8,128)(2,1)S(1)} %get-tuple-element.8, bf16[512,512]{1,0:T(8,128)(2,1)S(1)} %get-tuple-element.7, bf16[512,512]{1,0:T(8,128)(2,1)S(1)} %get-tuple-element.6, ...), kind=kOutput, calls=%fused_computation.10 | convolution fusion | flops 1084227584 | bytes 11010048 | tf_op jit(solution)/shard_map/rf,rg->fg/dot_general | solution.py:72
  (5 shorter events, 0.0 us)
Async XLA Ops:
  5.8 111.1 %slice-start = ((s8[7340032]{0:T(1024)(128)(4,1)}), s8[4194304]{0:T(1024)(128)(4,1)S(1)}, s32[]{:S(2)}) async-start(s8[7340032]{0:T(1024)(128)(4,1)} %bitcast.111), calls=%async_computation.1 | async-start | bytes 8388608
  102.3 9.4 %slice-start.2 = ((s8[7340032]{0:T(1024)(128)(4,1)}), s8[4194304]{0:T(1024)(128)(4,1)S(1)}, s32[]{:S(2)}) async-start(s8[7340032]{0:T(1024)(128)(4,1)} %bitcast.113), calls=%async_computation.3 | async-start | bytes 8388608
  102.3 9.4 %slice-start.3 = ((s8[7340032]{0:T(1024)(128)(4,1)}), s8[3145728]{0:T(1024)(128)(4,1)S(1)}, s32[]{:S(2)}) async-start(s8[7340032]{0:T(1024)(128)(4,1)} %bitcast.113), calls=%async_computation.4 | async-start | bytes 6291456
  102.3 14.6 %slice-start.1 = ((s8[7340032]{0:T(1024)(128)(4,1)}), s8[3145728]{0:T(1024)(128)(4,1)S(1)}, s32[]{:S(2)}) async-start(s8[7340032]{0:T(1024)(128)(4,1)} %bitcast.111), calls=%async_computation.2 | async-start | bytes 6291456
  102.3 14.6 %collective-permute-start = (bf16[512,7168]{1,0:T(8,128)(2,1)S(1)}, bf16[512,7168]{1,0:T(8,128)(2,1)S(1)}, u32[]{:S(2)}, u32[]{:S(2)}) collective-permute-start(bf16[512,7168]{1,0:T(8,128)(2,1)S(1)} %bitcast.106), channel_id=1, source_target_pairs={{0,1},{1,0},{2,3},{3,2},{4,5},{5,4},{6,7},{7,6},{8,9},{9,8},{10,11... | collective-permute-start | bytes 22020104 | tf_op jit(solution)/shard_map/ppermute | solution.py:45
  115.8 15.6 %collective-permute-start.1 = (bf16[512,512]{1,0:T(8,128)(2,1)S(1)}, bf16[512,512]{1,0:T(8,128)(2,1)S(1)}, u32[]{:S(2)}, u32[]{:S(2)}) collective-permute-start(bf16[512,512]{1,0:T(8,128)(2,1)S(1)} %fusion.27), channel_id=1, source_target_pairs={{0,2},{2,0},{1,3},{3,1},{4,6},{6,4},{5,7},{7,5},{8,10},{10,8},{9,1... | collective-permute-start | bytes 1572872 | tf_op jit(solution)/shard_map/ppermute | solution.py:57
  124.9 17.7 %copy-start = (bf16[512,512]{1,0:T(8,128)(2,1)}, bf16[512,512]{1,0:T(8,128)(2,1)S(1)}, u32[]{:S(2)}) copy-start(bf16[512,512]{1,0:T(8,128)(2,1)S(1)} %multiply_convert_fusion) | copy-start | bytes 1572868
  124.9 17.7 %collective-permute-start.2 = (bf16[512,512]{1,0:T(8,128)(2,1)S(1)}, bf16[512,512]{1,0:T(8,128)(2,1)S(1)}, u32[]{:S(2)}, u32[]{:S(2)}) collective-permute-start(bf16[512,512]{1,0:T(8,128)(2,1)S(1)} %multiply_convert_fusion), channel_id=1, source_target_pairs={{0,2},{2,0},{1,3},{3,1},{4,6},{6,4},{5,7},{7,5},{8,10},{10,8},{9,1... | collective-permute-start | bytes 1572872 | tf_op jit(solution)/shard_map/ppermute | solution.py:57
  142.6 1.6 %copy-start.2 = (bf16[512,512]{1,0:T(8,128)(2,1)}, bf16[512,512]{1,0:T(8,128)(2,1)S(1)}, u32[]{:S(2)}) copy-start(bf16[512,512]{1,0:T(8,128)(2,1)S(1)} %collective-permute-done.2) | copy-start | bytes 1572868
  144.2 4.5 %collective-permute-start.3 = (bf16[4,512,512]{2,1,0:T(8,128)(2,1)}, bf16[4,512,512]{2,1,0:T(8,128)(2,1)S(1)}, u32[]{:S(2)}, u32[]{:S(2)}) collective-permute-start(bf16[4,512,512]{2,1,0:T(8,128)(2,1)} %pad_maximum_fusion), channel_id=1, source_target_pairs={{0,1},{1,0},{2,3},{3,2},{4,5},{5,4},{6,7},{7,6},{8,9},{9,8},{10,11... | collective-permute-start | bytes 6291464 | tf_op jit(solution)/shard_map/ppermute | solution.py:58
  144.7 5.4 %copy-start.1 = (bf16[512,512]{1,0:T(8,128)(2,1)S(1)}, bf16[512,512]{1,0:T(8,128)(2,1)}, u32[]{:S(2)}) copy-start(bf16[512,512]{1,0:T(8,128)(2,1)} %copy-done) | copy-start | bytes 1572868
